TPU v7x, 32 devices: a whole 2x2x4 slice. The times are simulated.
32 devices in a mesh: groups: 2 (over x), ctx: 4 (over y, core), head: 4 (over z).
Axes of the slice: x: 2, y: 2, z: 4, core: 2. Of those that a mesh axis runs over, the one named last changes fastest.
Arguments:
- tokens: bfloat16 [8192, 2048], P(('groups', 'ctx')), parts along dimension 0, may hold values from -30 to 30
- norm_one: float32 [2048], replicated, may hold values from 0.1 to 1.9
- w_qkv1: bfloat16 [2048, 3, 2048], P(None, None, 'head'), may hold values from -0.125 to 0.125
- lin_gain: float32 [2048], P('head'), may hold values from 0.1 to 1.9
- w_out1: bfloat16 [2048, 2048], P('head'), may hold values from -0.125 to 0.125
- norm_two: float32 [2048], replicated, may hold values from 0.1 to 1.9
- w_qkv2: bfloat16 [2048, 3, 2048], P(None, None, 'head'), may hold values from -0.125 to 0.125
- q_gain: float32 [128], replicated, may hold values from 0.4 to 2.5
- k_gain: float32 [128], replicated, may hold values from 0.4 to 2.5
- w_out2: bfloat16 [2048, 2048], P('head'), may hold values from -0.125 to 0.125
- neighbours: int32 [16, 8], P('ctx'), may hold values from -1 to 15, as said below
Outputs:
- mixed: bfloat16 [8192, 2048], P(('groups', 'ctx', 'head')), parts along dimension 0
There are 2 independent parts, one for each index of `groups`. A program takes and returns all parts, laid end to end along the dimension named above; an argument that names none is the same for every part. Nothing has to cross between parts.
Inputs may be any that keep to these rules, and one draw needn't show every extreme that they name: `neighbours`: tile (i, j, l) of the 4 x 2 x 2 grid is number (i * 2 + j) * 2 + l, and its tokens are a whole tile of the stream. Entry 0 of row t is t itself; every other entry is -1 or a tile other than t whose grid position differs from t's by at most one in each dimension; the tiles of one row are distinct.
All inputs are finite; a program needn't handle non-finite values.
Results may differ from a plain program's by a relative error of at most 0.013.
Values may be sent and summed in bfloat16 or wider, within the bound.
No kernel may reach another device: no remote copies, remote signals or barrier semaphores. Data moves between devices by JAX's collectives and lax.ppermute only.
A program may use at most 192 MiB of HBM per device.

v0:
```python
import math

import jax
import jax.numpy as jnp
from jax import lax
from jax.sharding import PartitionSpec as P

TILE = 256
GY = 2
GZ = 2


EPS = 1e-06


def with_halo(shard, sides, width):
    for axis, dim in sides:
        size, length = (lax.axis_size(axis), shard.shape[dim])
        up = [(i, (i + 1) % size) for i in range(size - 1)]
        down = [(j, i) for i, j in up]
        last = lax.slice_in_dim(shard, length - width, length, axis=dim)
        first = lax.slice_in_dim(shard, 0, width, axis=dim)
        before = lax.ppermute(last, axis, up)
        after = lax.ppermute(first, axis, down)
        shard = jnp.concatenate([before, shard, after], axis=dim)
    return shard


def rms_rows(value, gain):
    mean_sq = jnp.mean(value * value, axis=-1, keepdims=True)
    return value * lax.rsqrt(mean_sq + EPS) * gain


def feature_map(value):
    return jnp.where(value > 0, value + 1.0, jnp.exp(jnp.minimum(value, 0.0)))


def split_two(value):
    high_part = value.astype(jnp.bfloat16)
    low_part = (value - high_part.astype(jnp.float32)).astype(jnp.bfloat16)
    return (high_part, low_part)


def on_device(
    tokens, norm_one, w_qkv1, lin_gain, w_out1, norm_two, w_qkv2, q_gain, k_gain, w_out2, neighbours
):
    highest = lax.Precision.HIGHEST
    tok_rows, feature_width = tokens.shape
    inner_dev = w_qkv1.shape[2]
    head_dim = q_gain.shape[0]
    heads_dev = inner_dev // head_dim
    span_count = tok_rows // TILE
    block_rows = 2 * TILE
    block_count = tok_rows // block_rows
    rows_mine = tok_rows // lax.axis_size("head")
    head_index = lax.axis_index("head")
    normed = rms_rows(tokens.astype(jnp.float32), norm_one).astype(jnp.bfloat16)
    projected = jnp.dot(
        normed, w_qkv1.reshape(feature_width, 3 * inner_dev), preferred_element_type=jnp.float32
    )
    projected = projected.reshape(tok_rows, 3, heads_dev, head_dim)
    query_map = feature_map(projected[:, 0]).astype(jnp.bfloat16)
    key_map = feature_map(projected[:, 1]).astype(jnp.bfloat16)
    value_one = projected[:, 2].astype(jnp.bfloat16)
    span_states = jnp.einsum(
        "cthe,cthf->chef",
        key_map.reshape(span_count, TILE, heads_dev, head_dim),
        value_one.reshape(span_count, TILE, heads_dev, head_dim),
        preferred_element_type=jnp.float32,
    )
    all_states = lax.all_gather(span_states.astype(jnp.bfloat16), "ctx", axis=0, tiled=True).astype(
        span_states.dtype
    )
    own_spans = lax.axis_index("ctx") * span_count + jnp.arange(span_count, dtype=jnp.int32)
    all_spans = jnp.arange(all_states.shape[0], dtype=jnp.int32)
    earlier = (all_spans[None, :] < own_spans[:, None]).astype(jnp.float32)
    carried = jnp.einsum("ij,jhef->ihef", earlier, all_states, precision=highest)
    q_blocks = query_map.reshape(block_count, block_rows, heads_dev, head_dim)
    k_blocks = key_map.reshape(block_count, block_rows, heads_dev, head_dim)
    v_blocks = value_one.reshape(block_count, block_rows, heads_dev, head_dim)
    scores = jnp.einsum("nthe,nshe->nhts", q_blocks, k_blocks, preferred_element_type=jnp.float32)
    causal = lax.broadcasted_iota(jnp.int32, (block_rows, block_rows), 0) >= lax.broadcasted_iota(
        jnp.int32, (block_rows, block_rows), 1
    )
    scores = jnp.where(causal, scores, 0.0)
    score_high, score_low = split_two(scores)
    within = jnp.einsum("nhts,nshe->nthe", score_high, v_blocks, preferred_element_type=jnp.float32)
    within = within + jnp.einsum(
        "nhts,nshe->nthe", score_low, v_blocks, preferred_element_type=jnp.float32
    )
    state_high, state_low = split_two(carried[0::2])
    carried_term = jnp.einsum(
        "nthe,nhef->nthf", q_blocks, state_high, preferred_element_type=jnp.float32
    )
    carried_term = carried_term + jnp.einsum(
        "nthe,nhef->nthf", q_blocks, state_low, preferred_element_type=jnp.float32
    )
    combined = (within + carried_term).reshape(tok_rows, heads_dev, head_dim)
    attn_one = (
        rms_rows(combined, lin_gain.reshape(heads_dev, head_dim))
        .astype(jnp.bfloat16)
        .reshape(tok_rows, inner_dev)
    )
    w_qkv2_flat = w_qkv2.reshape(feature_width, 3 * inner_dev)
    attn_rows = attn_one
    summed = lax.psum_scatter(
        jnp.dot(attn_rows, w_out1, preferred_element_type=jnp.float32).astype(jnp.bfloat16),
        "head",
        scatter_dimension=0,
        tiled=True,
    ).astype(jnp.float32)
    tokens_mine = lax.dynamic_slice_in_dim(tokens, head_index * rows_mine, rows_mine, 0)
    residual_mine = (tokens_mine.astype(jnp.float32) + summed).astype(jnp.bfloat16)
    normed_mine = rms_rows(residual_mine.astype(jnp.float32), norm_two).astype(jnp.bfloat16)
    projected_two = jnp.dot(
        lax.all_gather(normed_mine, "head", axis=0, tiled=True),
        w_qkv2_flat,
        preferred_element_type=jnp.float32,
    )
    projected_two = projected_two.reshape(tok_rows, 3, heads_dev, head_dim)
    query_hat = rms_rows(projected_two[:, 0], q_gain).astype(jnp.bfloat16)
    key_hat = rms_rows(projected_two[:, 1], k_gain).astype(jnp.bfloat16)
    value_two = projected_two[:, 2].astype(jnp.bfloat16)
    key_value = jnp.stack([key_hat, value_two], axis=1).reshape(tok_rows, 2 * inner_dev)
    plane_tiles = GY * GZ
    widened = with_halo(key_value, (("ctx", 0),), plane_tiles * TILE)
    buffer_tiles = widened.shape[0] // TILE
    tile_count = tok_rows // TILE
    base_tile = lax.axis_index("ctx") * tile_count - plane_tiles
    local_index = jnp.clip(neighbours - base_tile, 0, buffer_tiles - 1)
    valid_slots = neighbours >= 0
    picked = jnp.take(widened.reshape(buffer_tiles, TILE, 2 * inner_dev), local_index, axis=0)
    picked = picked.reshape(tile_count, neighbours.shape[1] * TILE, 2, heads_dev, head_dim)
    query_tiles = query_hat.reshape(tile_count, TILE, heads_dev, head_dim)
    score_scale = 1.0 / math.sqrt(head_dim)
    tile_scores = (
        jnp.einsum(
            "pthe,pshe->phts", query_tiles, picked[:, :, 0], preferred_element_type=jnp.float32
        )
        * score_scale
    )
    valid_keys = jnp.repeat(valid_slots, TILE, axis=1)
    unnormed = jnp.where(valid_keys[:, None, None, :], jnp.exp(tile_scores), 0.0)
    weights = (unnormed / jnp.sum(unnormed, axis=-1, keepdims=True)).astype(jnp.bfloat16)
    attn_two = jnp.einsum(
        "phts,pshe->pthe", weights, picked[:, :, 1], preferred_element_type=jnp.float32
    )
    attn_two = attn_two.astype(jnp.bfloat16).reshape(tok_rows, inner_dev)
    attn_rows = attn_two
    summed_two = lax.psum_scatter(
        jnp.dot(attn_rows, w_out2, preferred_element_type=jnp.float32).astype(jnp.bfloat16),
        "head",
        scatter_dimension=0,
        tiled=True,
    ).astype(jnp.float32)
    return (residual_mine.astype(jnp.float32) + summed_two).astype(jnp.bfloat16)


def solution(mesh):
    in_specs = (
        P(("groups", "ctx"), None),
        P(),
        P(None, None, "head"),
        P("head"),
        P("head", None),
        P(),
        P(None, None, "head"),
        P(),
        P(),
        P("head", None),
        P("ctx", None),
    )
    out_specs = P(("groups", "ctx", "head"), None)
    return jax.shard_map(
        on_device, mesh=mesh, in_specs=in_specs, out_specs=out_specs, check_vma=False
    )
```

profile of v0, /device:TPU:1, one launch (start us, length us, event | category | flops | bytes accessed | tf_op | source)
XLA Modules:
  0.0 478.9 jit_solution(6588057674238877262)
XLA Ops:
  6.5 0.0 all-gather.3.cloned.1.call-start
  6.5 3.2 fusion.2
  9.8 0.0 copy-start.11
  9.8 8.9 %copy.64 = bf16[2048,3,512]{0,2,1:T(8,128)(2,1)} copy(bf16[2048,3,512]{2,0,1:T(8,128)(2,1)} %param.13) | data formatting | bytes 12582912 | tf_op args[2]
  18.7 0.0 copy-done.11
  18.7 10.3 %fusion.9 = f32[1024,3,4,128]{3,0,2,1:T(8,128)S(1)} fusion(bf16[3,4,128,2048]{3,2,1,0:T(8,128)(2,1)} %bitcast.91, bf16[1024,2048]{1,0:T(8,128)(2,1)} %param.11, f32[2048]{0:T(1024)S(1)} %copy-done.11, f32[1024]{0:T(1024)S(1)} %add_rsqrt_fusion.3), kind=kOutput, calls=%fused_computation.20 | convolution fusion | flops 6450839552 | bytes 16789504 | tf_op jit(solution)/shard_map/dot_general | solution.py:58
  29.0 0.1 slice.63
  29.1 1.0 select_convert_fusion.2
  30.1 0.0 copy-start.6
  30.1 1.0 copy-done.6
  31.1 1.3 convolution_convert_fusion.2
  32.3 0.0 all-gather.3.cloned.1.call-update
  32.4 0.2 reduce-scatter.3.cloned.1.call-start
  32.6 0.1 iota_compare_fusion
  32.7 2.6 fusion.34
  35.3 0.0 copy-done.3
  35.3 2.9 fusion.6
  38.2 3.2 fusion.7
  41.4 16.2 %all-gather.3.cloned.1.call-done = bf16[16,4,128,128]{3,2,1,0:T(8,128)(2,1)} async-done(((bf16[4,4,128,128]{3,2,1,0:T(8,128)(2,1)}), bf16[16,4,128,128]{3,2,1,0:T(8,128)(2,1)}) %all-gather.3.cloned.1.call-update) | async-done | bytes 2097168 | tf_op jit(solution)/shard_map/all_gather | solution.py:71
  57.6 3.9 fusion.25
  61.4 10.4 %slice.31 = f32[2,4,128,128]{3,0,2,1:T(2,128)} slice(f32[4,4,128,128]{3,0,2,1:T(4,128)} %fusion.25), slice={[0:4:2], [0:4:1], [0:128:1], [0:128:1]} | slice | bytes 1048576 | tf_op jit(solution)/shard_map/slice | solution.py:91
  71.9 1.7 subtract_convert_fusion.2
  73.6 0.5 fusion.42
  74.1 0.3 copy-done.5
  74.4 2.1 multiply_reduce_fusion.2
  76.5 0.2 copy.77
  76.7 2.9 copy.76
  79.7 1.2 mul.127
  80.9 5.9 %convolution_convert_fusion.1 = bf16[1024,2048]{1,0:T(8,128)(2,1)} fusion(bf16[512,2048]{1,0:T(8,128)(2,1)S(1)} %copy-done, f32[128,8,4,128]{3,2,1,0:T(4,128)S(1)} %bitcast.94, f32[128,8,4,128]{3,2,1,0:T(4,128)} %bitcast.95, f32[512]{0:T(512)S(1)} %copy-done.12), kind=kOutput, calls=%fused_computation.30 | convolution fusion | flops 2151153664 | bytes 10487808 | tf_op jit(solution)/shard_map/dot_general | solution.py:107
  86.8 0.0 reduce-scatter.3.cloned.1.call-update
  86.8 0.0 all-gather.5.cloned.1.call-start
  86.9 76.5 %reduce-scatter.3.cloned.1.call-done = bf16[256,2048]{1,0:T(8,128)(2,1)} async-done(((bf16[1024,2048]{1,0:T(8,128)(2,1)}), bf16[256,2048]{1,0:T(8,128)(2,1)}) %reduce-scatter.3.cloned.1.call-update) | async-done | bytes 1048592 | tf_op jit(solution)/shard_map/reduce_scatter | solution.py:106
  163.4 2.0 fusion.19
  165.4 1.3 fusion.21
  166.7 0.0 all-gather.5.cloned.1.call-update
  166.7 0.3 reduce-scatter.5.cloned.1.call-start
  167.0 9.0 %copy.78 = bf16[2048,3,512]{0,2,1:T(8,128)(2,1)} copy(bf16[2048,3,512]{2,0,1:T(8,128)(2,1)} %param.17) | data formatting | bytes 12582912 | tf_op args[6]
  176.0 72.2 %all-gather.5.cloned.1.call-done = bf16[1024,2048]{1,0:T(8,128)(2,1)} async-done(((bf16[256,2048]{1,0:T(8,128)(2,1)}), bf16[1024,2048]{1,0:T(8,128)(2,1)}) %all-gather.5.cloned.1.call-update) | async-done | bytes 4194320 | tf_op jit(solution)/shard_map/all_gather | solution.py:116
  248.1 10.1 %fusion.11 = f32[1024,3,4,128]{0,3,2,1:T(8,128)S(1)} fusion(bf16[3,4,128,2048]{3,2,1,0:T(8,128)(2,1)} %bitcast.90, bf16[1024,2048]{1,0:T(8,128)(2,1)} %all-gather.5.cloned.1.call-done), kind=kOutput, calls=%fused_computation.21 | convolution fusion | flops 6442450944 | bytes 16777216 | tf_op jit(solution)/shard_map/dot_general | solution.py:115
  258.2 0.0 copy-start.10
  258.2 0.6 multiply_reduce_fusion
  258.8 0.2 slice.62
  259.0 1.7 fusion.54
  260.7 0.2 pad_maximum_fusion.1
  260.9 2.6 copy.79
  263.5 2.6 collective-permute-start.1
  266.1 3.0 collective-permute-start
  269.1 0.1 reshape.154
  269.2 0.1 broadcast_bitcast_fusion
  269.4 2.2 squeeze.7
  271.6 1.8 copy.84
  273.4 17.8 %collective-permute-done.1 = bf16[1024,1024]{1,0:T(8,128)(2,1)} collective-permute-done((bf16[1024,1024]{1,0:T(8,128)(2,1)}, bf16[1024,1024]{1,0:T(8,128)(2,1)}, u32[]{:S(2)}, u32[]{:S(2)}) %collective-permute-start.1) | collective-permute-done | bytes 2097184 | tf_op jit(solution)/shard_map/ppermute | solution.py:24
  291.2 1.2 collective-permute-done
  292.4 5.9 %pad_maximum_fusion = bf16[3072,1024]{1,0:T(8,128)(2,1)} fusion(bf16[1024,1024]{1,0:T(8,128)(2,1)} %collective-permute-done.1, bf16[1024,1024]{1,0:T(8,128)(2,1)} %copy.79, bf16[1024,1024]{1,0:T(8,128)(2,1)} %collective-permute-done), kind=kLoop, calls=%fused_computation.16 | loop fusion | flops 18874368 | bytes 12582912 | tf_op jit(solution)/shard_map/concatenate | solution.py:25
  298.3 10.0 %gather_fusion = bf16[32,256,1024]{2,1,0:T(8,128)(2,1)} fusion(bf16[12,256,1024]{2,1,0:T(8,128)(2,1)} %bitcast.82, s32[1024]{0:T(1024)S(1)} %pad_clamp_fusion), kind=kCustom, calls=%fused_computation | custom fusion | bytes 33554560 | tf_op jit(solution)/shard_map/jit(_take)/gather | solution.py:132
  308.3 27.4 %gather.7 = bf16[4,2048,2,4,128]{4,3,2,1,0:T(4,128)(2,1)} reshape(bf16[32,256,1024]{2,1,0:T(8,128)(2,1)} %gather_fusion) | data formatting | bytes 33554432 | tf_op jit(solution)/shard_map/jit(_take)/gather | solution.py:132
  335.7 15.5 %copy_select_fusion = bf16[4,2048,2,4,128]{4,1,3,0,2:T(8,128)(2,1)} fusion(bf16[4,2048,2,4,128]{4,3,2,1,0:T(4,128)(2,1)} %gather.7, pred[4,2048]{1,0:T(4,128)(4,1)S(1)} %bitcast.98), kind=kLoop, calls=%fused_computation.4 | loop fusion | flops 8388608 | bytes 33562624 | tf_op jit(solution)/shard_map/jit(_take)/select_n | solution.py:132
  351.2 17.5 %fusion = (f32[4,4,256]{2,1,0:T(4,128)S(1)}, f32[4,4,256,2048]{3,2,1,0:T(8,128)}) fusion(pred[4,2048]{1,0:T(4,128)(4,1)S(1)} %bitcast.100, bf16[4,2048,2,4,128]{4,1,3,0,2:T(8,128)(2,1)} %copy_select_fusion, f32[4,256,4,128]{3,1,2,0:T(8,128)S(1)} %copy-done.7, f32[128]{0:T(128)S(1)} %copy-done.13, f32[4,256,4]{1,2,0:T(4,128)S(1)} %bitcast.99), kind=kOutput, calls=%fused_computation.3 | convolution fusion | flops 2174218240 | bytes 44081664 | tf_op jit(solution)/shard_map/pthe,pshe->phts/dot_general | solution.py:137
  368.7 16.9 %fusion.28 = bf16[4,256,4,128]{1,3,2,0:T(8,128)(2,1)S(1)} fusion(f32[4,4,256,2048]{3,2,1,0:T(8,128)} %get-tuple-element.21, f32[4,4,256]{2,1,0:T(4,128)S(1)} %get-tuple-element.20, pred[4,2048]{1,0:T(4,128)(4,1)S(1)} %bitcast.101, bf16[4,2048,2,4,128]{4,1,3,0,2:T(8,128)(2,1)} %copy_select_fusion), kind=kOutput, calls=%fused_computation.56 | convolution fusion | flops 2181562368 | bytes 43016192 | tf_op jit(solution)/shard_map/phts,pshe->pthe/dot_general | solution.py:145
  385.7 1.4 copy.86
  387.1 6.3 %convolution_convert_fusion = bf16[1024,2048]{1,0:T(8,128)(2,1)} fusion(bf16[512,2048]{1,0:T(8,128)(2,1)} %param.20, bf16[128,8,4,128]{3,2,1,0:T(4,128)(2,1)} %bitcast.96), kind=kOutput, calls=%fused_computation.29 | convolution fusion | flops 2149580800 | bytes 7340032 | tf_op jit(solution)/shard_map/dot_general | solution.py:151
  393.4 0.0 reduce-scatter.5.cloned.1.call-update
  393.5 76.3 %reduce-scatter.5.cloned.1.call-done = bf16[256,2048]{1,0:T(8,128)(2,1)} async-done(((bf16[1024,2048]{1,0:T(8,128)(2,1)}), bf16[256,2048]{1,0:T(8,128)(2,1)}) %reduce-scatter.5.cloned.1.call-update) | async-done | bytes 1048592 | tf_op jit(solution)/shard_map/reduce_scatter | solution.py:150
  469.8 2.6 fusion.22
  (30 shorter events, 0.1 us)
Async XLA Ops:
  6.5 74.4 %copy-start = (bf16[512,2048]{1,0:T(8,128)(2,1)S(1)}, bf16[512,2048]{1,0:T(8,128)(2,1)}, u32[]{:S(2)}) copy-start(bf16[512,2048]{1,0:T(8,128)(2,1)} %param.15) | copy-start | bytes 6291460
  6.5 51.1 %all-gather.3.cloned.1.call-start = ((), (), s32[]{:S(2)}) async-start(), calls=%async_computation.2 | async-start | bytes 2621440 | tf_op jit(solution)/shard_map/all_gather | solution.py:71
  9.8 8.9 %copy-start.11 = (f32[2048]{0:T(1024)S(1)}, f32[2048]{0:T(1024)}, u32[]{:S(2)}) copy-start(f32[2048]{0:T(1024)} %param.12) | copy-start | bytes 24580
  29.1 1.0 copy-start.2
  30.1 1.0 copy-start.6
  32.4 131.0 %reduce-scatter.3.cloned.1.call-start = ((), (), s32[]{:S(2)}) async-start(), calls=%async_computation.3 | async-start | bytes 5242880 | tf_op jit(solution)/shard_map/reduce_scatter | solution.py:106
  32.7 2.6 copy-start.3
  71.9 2.2 copy-start.4
  71.9 2.5 copy-start.5
  76.5 4.4 copy-start.12
  86.8 78.6 %copy-start.8 = (f32[2048]{0:T(1024)S(1)}, f32[2048]{0:T(1024)}, u32[]{:S(2)}) copy-start(f32[2048]{0:T(1024)} %param.16) | copy-start | bytes 24580
  86.8 161.3 %all-gather.5.cloned.1.call-start = ((), (), s32[]{:S(2)}) async-start(), calls=%async_computation.4 | async-start | bytes 5242880 | tf_op jit(solution)/shard_map/all_gather | solution.py:116
  166.7 303.0 %reduce-scatter.5.cloned.1.call-start = ((), (), s32[]{:S(2)}) async-start(), calls=%async_computation.5 | async-start | bytes 5242880 | tf_op jit(solution)/shard_map/reduce_scatter | solution.py:150
  258.2 0.8 copy-start.10
  260.7 8.4 %copy-start.9 = (s32[4,8]{1,0:T(4,128)S(1)}, s32[4,8]{1,0:T(4,128)}, u32[]{:S(2)}) copy-start(s32[4,8]{1,0:T(4,128)} %param.21) | copy-start | bytes 388
  263.5 27.7 %collective-permute-start.1 = (bf16[1024,1024]{1,0:T(8,128)(2,1)}, bf16[1024,1024]{1,0:T(8,128)(2,1)}, u32[]{:S(2)}, u32[]{:S(2)}) collective-permute-start(bf16[1024,1024]{1,0:T(8,128)(2,1)} %copy.79), channel_id=1, source_target_pairs={{4,0},{8,4},{12,8},{5,1},{9,5},{13,9},{6,2},{10,6},{14,10},{7,3},{... | collective-permute-start | bytes 6291464 | tf_op jit(solution)/shard_map/ppermute | solution.py:24
  266.1 26.3 %collective-permute-start = (bf16[1024,1024]{1,0:T(8,128)(2,1)}, bf16[1024,1024]{1,0:T(8,128)(2,1)}, u32[]{:S(2)}, u32[]{:S(2)}) collective-permute-start(bf16[1024,1024]{1,0:T(8,128)(2,1)} %copy.79), channel_id=1, source_target_pairs={{0,4},{4,8},{8,12},{1,5},{5,9},{9,13},{2,6},{6,10},{10,14},{3,7},{... | collective-permute-start | bytes 6291464 | tf_op jit(solution)/shard_map/ppermute | solution.py:23
  335.7 15.5 %copy-start.7 = (f32[4,256,4,128]{3,1,2,0:T(8,128)S(1)}, f32[4,256,4,128]{3,1,2,0:T(8,128)}, u32[]{:S(2)}) copy-start(f32[4,256,4,128]{3,1,2,0:T(8,128)} %copy.84) | copy-start | bytes 6291460
  335.7 15.5 %copy-start.13 = (f32[128]{0:T(128)S(1)}, f32[128]{0:T(128)}, u32[]{:S(2)}) copy-start(f32[128]{0:T(128)} %param.18) | copy-start | bytes 1540
  387.1 85.3 %copy-start.1 = (bf16[512,2048]{1,0:T(8,128)(2,1)S(1)}, bf16[512,2048]{1,0:T(8,128)(2,1)}, u32[]{:S(2)}) copy-start(bf16[512,2048]{1,0:T(8,128)(2,1)} %param.15) | copy-start | bytes 6291460
Sparse Core Ops, SparseCore 0:
  32.5 25.0 all-gather.2
  86.9 76.3 reduce-scatter.2
  166.9 81.2 all-gather.4
  393.6 76.1 reduce-scatter.4
where the time goes:
time: 482 us; the launch traced here: 479 us
  waiting for transfers between devices  260 us (54%)
  matrix products  83.4 us (17%)
  local copies, waits for them, and re-layouts  79.8 us (17%)
  other arithmetic  35.9 us (7%)
  between operations  13.4 us (3%)
  starting transfers between devices  6.12 us (1%)
    reduce_scatter x1, waiting for transfers between devices, on_device(): lax.psum_scatter(jnp.dot(attn_rows, w_out1, preferred_element_type=jnp.fl...  76.5 us
    reduce_scatter x1, waiting for transfers between devices, on_device(): lax.psum_scatter(jnp.dot(attn_rows, w_out2, preferred_element_type=jnp.fl...  76.3 us
    all_gather x1, waiting for transfers between devices, on_device(): lax.all_gather(normed_mine, 'head', axis=0, tiled=True)  72.2 us
    gather x2, local copies, waits for them, and re-layouts, on_device(): jnp.take(widened.reshape(buffer_tiles, TILE, 2 * inner_dev), local_index,...  37.3 us
    unnamed x33, local copies, waits for them, and re-layouts  19.3 us
    ppermute x1, waiting for transfers between devices, with_halo(): after = lax.ppermute(first, axis, down)  17.8 us
    dot_general x1, matrix products, on_device(): jnp.einsum('pthe,pshe->phts', query_tiles, picked[:, :, 0], preferred_ele...  17.5 us
    dot_general x1, matrix products, on_device(): jnp.einsum('phts,pshe->pthe', weights, picked[:, :, 1], preferred_element...  16.9 us
  transfers between devices with their start and end apart: 6, of which 6 were waited for; matrix products, arithmetic and copies ran while one was open for 5% of the time, Pallas kernels for 0%

commit v1 on v0

v1 whole, which is shorter than its diff:
```python
import math

import jax
import jax.numpy as jnp
from jax import lax
from jax.sharding import PartitionSpec as P

TILE = 256
GY = 2
GZ = 2


EPS = 1e-06


def with_halo(shard, sides, width):
    for axis, dim in sides:
        size, length = (lax.axis_size(axis), shard.shape[dim])
        up = [(i, (i + 1) % size) for i in range(size - 1)]
        down = [(j, i) for i, j in up]
        last = lax.slice_in_dim(shard, length - width, length, axis=dim)
        first = lax.slice_in_dim(shard, 0, width, axis=dim)
        before = lax.ppermute(last, axis, up)
        after = lax.ppermute(first, axis, down)
        shard = jnp.concatenate([before, shard, after], axis=dim)
    return shard


def rms_rows(value, gain):
    mean_sq = jnp.mean(value * value, axis=-1, keepdims=True)
    return value * lax.rsqrt(mean_sq + EPS) * gain


def feature_map(value):
    return jnp.where(value > 0, value + 1.0, jnp.exp(jnp.minimum(value, 0.0)))


def split_two(value):
    high_part = value.astype(jnp.bfloat16)
    low_part = (value - high_part.astype(jnp.float32)).astype(jnp.bfloat16)
    return (high_part, low_part)


def on_device(
    tokens, norm_one, w_qkv1, lin_gain, w_out1, norm_two, w_qkv2, q_gain, k_gain, w_out2, neighbours
):
    f32, bf16 = jnp.float32, jnp.bfloat16
    tok_rows, feature_width = tokens.shape
    inner_dev = w_qkv1.shape[2]
    head_dim = q_gain.shape[0]
    heads_dev = inner_dev // head_dim
    block_rows = 2 * TILE
    block_count = tok_rows // block_rows
    rows_mine = tok_rows // lax.axis_size("head")
    head_index = lax.axis_index("head")
    ctx_index = lax.axis_index("ctx")
    ctx_size = lax.axis_size("ctx")

    normed = rms_rows(tokens.astype(f32), norm_one).astype(bf16)
    projected = jnp.dot(
        normed, w_qkv1.reshape(feature_width, 3 * inner_dev), preferred_element_type=f32
    )
    projected = projected.reshape(tok_rows, 3, heads_dev, head_dim)
    query_map = feature_map(projected[:, 0]).astype(bf16)
    key_map = feature_map(projected[:, 1]).astype(bf16)
    value_one = projected[:, 2].astype(bf16)
    q_blocks = query_map.reshape(block_count, block_rows, heads_dev, head_dim)
    k_blocks = key_map.reshape(block_count, block_rows, heads_dev, head_dim)
    v_blocks = value_one.reshape(block_count, block_rows, heads_dev, head_dim)
    block_states = jnp.einsum(
        "nthe,nthf->nhef", k_blocks, v_blocks, preferred_element_type=f32
    )
    own_total = jnp.sum(block_states, axis=0)
    all_totals = lax.all_gather(own_total.astype(bf16), "ctx", axis=0).astype(f32)
    earlier_dev = jnp.arange(ctx_size, dtype=jnp.int32) < ctx_index
    carried = jnp.sum(jnp.where(earlier_dev[:, None, None, None], all_totals, 0.0), axis=0)

    causal = lax.broadcasted_iota(jnp.int32, (block_rows, block_rows), 0) >= lax.broadcasted_iota(
        jnp.int32, (block_rows, block_rows), 1
    )
    w_qkv2_flat = w_qkv2.reshape(feature_width, 3 * inner_dev)
    residual_parts = []
    q_parts, k_parts, v_parts = [], [], []
    previous = None
    for n in range(block_count):
        q_n, k_n, v_n = q_blocks[n], k_blocks[n], v_blocks[n]
        scores = jnp.einsum("the,she->hts", q_n, k_n, preferred_element_type=f32)
        scores = jnp.where(causal, scores, 0.0)
        score_high, score_low = split_two(scores)
        within = jnp.einsum("hts,she->the", score_high, v_n, preferred_element_type=f32)
        within = within + jnp.einsum("hts,she->the", score_low, v_n, preferred_element_type=f32)
        state_high, state_low = split_two(carried)
        carried_term = jnp.einsum("the,hef->thf", q_n, state_high, preferred_element_type=f32)
        carried_term = carried_term + jnp.einsum(
            "the,hef->thf", q_n, state_low, preferred_element_type=f32
        )
        carried = carried + block_states[n]
        combined = within + carried_term
        attn_n = (
            rms_rows(combined, lin_gain.reshape(heads_dev, head_dim))
            .astype(bf16)
            .reshape(block_rows, inner_dev)
        )
        partial = jnp.dot(attn_n, w_out1, preferred_element_type=f32).astype(bf16)
        if previous is not None:
            partial, previous = lax.optimization_barrier((partial, previous))
            residual_parts[-1] = previous
        summed = lax.psum(partial, "head").astype(f32)
        tokens_n = tokens[n * block_rows : (n + 1) * block_rows].astype(f32)
        residual_n = (tokens_n + summed).astype(bf16)
        residual_parts.append(residual_n)
        previous = residual_n
        normed_n = rms_rows(residual_n.astype(f32), norm_two).astype(bf16)
        proj_n = jnp.dot(normed_n, w_qkv2_flat, preferred_element_type=f32)
        proj_n = proj_n.reshape(block_rows, 3, heads_dev, head_dim)
        q_parts.append(rms_rows(proj_n[:, 0], q_gain).astype(bf16))
        k_parts.append(rms_rows(proj_n[:, 1], k_gain).astype(bf16))
        v_parts.append(proj_n[:, 2].astype(bf16))
    residual = jnp.concatenate(residual_parts, axis=0)
    query_hat = jnp.concatenate(q_parts, axis=0)
    key_hat = jnp.concatenate(k_parts, axis=0)
    value_two = jnp.concatenate(v_parts, axis=0)

    key_value = jnp.stack([key_hat, value_two], axis=1).reshape(tok_rows, 2 * inner_dev)
    plane_tiles = GY * GZ
    widened = with_halo(key_value, (("ctx", 0),), plane_tiles * TILE)
    buffer_rows = widened.shape[0]
    buffer_tiles = buffer_rows // TILE
    tile_count = tok_rows // TILE
    base_tile = ctx_index * tile_count - plane_tiles
    widened = widened.reshape(buffer_rows, 2, heads_dev, head_dim)
    buffer_ids = base_tile + jnp.arange(buffer_tiles, dtype=jnp.int32)
    valid = jnp.any(
        (neighbours[:, :, None] == buffer_ids[None, None, :]) & (neighbours[:, :, None] >= 0),
        axis=1,
    )
    valid_keys = jnp.repeat(valid, TILE, axis=1)
    query_tiles = query_hat.reshape(tile_count, TILE, heads_dev, head_dim)
    score_scale = 1.0 / math.sqrt(head_dim)
    tile_scores = (
        jnp.einsum(
            "pthe,she->phts", query_tiles, widened[:, 0], preferred_element_type=f32
        )
        * score_scale
    )
    unnormed = jnp.where(valid_keys[:, None, None, :], jnp.exp(tile_scores), 0.0)
    weights = (unnormed / jnp.sum(unnormed, axis=-1, keepdims=True)).astype(bf16)
    attn_two = jnp.einsum("phts,she->pthe", weights, widened[:, 1], preferred_element_type=f32)
    attn_two = attn_two.astype(bf16).reshape(tok_rows, inner_dev)
    summed_two = lax.psum_scatter(
        jnp.dot(attn_two, w_out2, preferred_element_type=f32).astype(bf16),
        "head",
        scatter_dimension=0,
        tiled=True,
    ).astype(f32)
    residual_mine = lax.dynamic_slice_in_dim(residual, head_index * rows_mine, rows_mine, 0)
    return (residual_mine.astype(f32) + summed_two).astype(bf16)


def solution(mesh):
    in_specs = (
        P(("groups", "ctx"), None),
        P(),
        P(None, None, "head"),
        P("head"),
        P("head", None),
        P(),
        P(None, None, "head"),
        P(),
        P(),
        P("head", None),
        P("ctx", None),
    )
    out_specs = P(("groups", "ctx", "head"), None)
    return jax.shard_map(
        on_device, mesh=mesh, in_specs=in_specs, out_specs=out_specs, check_vma=False
    )
```

time: 482 us -> 426 us (0.88)
  local copies, waits for them, and re-layouts: 79.8 us -> 36.2 us
  other arithmetic: 35.9 us -> 23 us
  waiting for transfers between devices: 260 us -> 248 us
  blocking collectives: 0 us -> 8.73 us
  matrix products: 83.4 us -> 88.3 us
    psum x0 -> x2, waiting for transfers between devices: none -> 153 us  [on_device(): summed = lax.psum(partial, 'head').astype(f32)]
    all_gather x2 -> x0, waiting for transfers between devices: 88.4 us -> none  [the longest x1 72.2 us: on_device(): lax.all_gather(normed_mine, 'head', axis=0, tiled=True)]
    reduce_scatter x2 -> x1, waiting for transfers between devices: 153 us -> 74.7 us  [on_device(): lax.psum_scatter(jnp.dot(attn_two, w_out2, preferred_element_type=f32).as...]
    gather x2 -> x0, local copies, waits for them, and re-layouts: 37.3 us -> none  [on_device(): jnp.take(widened.reshape(buffer_tiles, TILE, 2 * inner_dev), local_index,...]
    select_n x1 -> x0, other arithmetic: 15.5 us -> none  [on_device(): jnp.take(widened.reshape(buffer_tiles, TILE, 2 * inner_dev), local_index,...]
    slice x3 -> x1, local copies, waits for them, and re-layouts: 10.7 us -> 1.11 us  [on_device(): value_one = projected[:, 2].astype(bf16)]
    all_gather x0 -> x1, blocking collectives: none -> 8.73 us  [on_device(): lax.all_gather(own_total.astype(bf16), 'ctx', axis=0).astype(f32)]
    concatenate x0 -> x2, local copies, waits for them, and re-layouts: none -> 7.9 us  [with_halo(): shard = jnp.concatenate([before, shard, after], axis=dim)]
  transfers between devices with their start and end apart: 6 -> 5, of which waited for: 6 -> 4; matrix products, arithmetic and copies ran while one was open for 5% -> 6% of each run, Pallas kernels for 0% -> 0%
where the time goes in v1:
time: 426 us; the launch traced here: 424 us
  waiting for transfers between devices  248 us (58%)
  matrix products  88.3 us (21%)
  local copies, waits for them, and re-layouts  36.2 us (8%)
  other arithmetic  23 us (5%)
  between operations  13.6 us (3%)
  blocking collectives  8.73 us (2%)
  starting transfers between devices  6.13 us (1%)
    psum x2, waiting for transfers between devices, on_device(): summed = lax.psum(partial, 'head').astype(f32)  153 us
    reduce_scatter x1, waiting for transfers between devices, on_device(): lax.psum_scatter(jnp.dot(attn_two, w_out2, preferred_element_type=f32).as...  74.7 us
    unnamed x38, local copies, waits for them, and re-layouts  22.4 us
    dot_general x1, matrix products, on_device(): jnp.einsum('phts,she->pthe', weights, widened[:, 1], preferred_element_ty...  22.4 us
    ppermute x1, waiting for transfers between devices, with_halo(): after = lax.ppermute(first, axis, down)  20.6 us
    dot_general x1, matrix products, on_device(): jnp.einsum('pthe,she->phts', query_tiles, widened[:, 0], preferred_elemen...  19.7 us
    dot_general x2, matrix products, on_device(): proj_n = jnp.dot(normed_n, w_qkv2_flat, preferred_element_type=f32)  12.2 us
    reduce_sum x5, other arithmetic, rms_rows(): mean_sq = jnp.mean(value * value, axis=-1, keepdims=True)  10.8 us
  transfers between devices with their start and end apart: 5, of which 4 were waited for; matrix products, arithmetic and copies ran while one was open for 6% of the time, Pallas kernels for 0%

profile of v1, /device:TPU:1, one launch (start us, length us, event | category | flops | bytes accessed | tf_op | source)
XLA Modules:
  0.0 424.0 jit_solution(1946575152552089847)
XLA Ops:
  6.5 0.1 iota_compare_fusion
  6.6 3.2 fusion.2
  9.9 8.8 %copy.60 = bf16[2048,3,512]{0,2,1:T(8,128)(2,1)} copy(bf16[2048,3,512]{2,0,1:T(8,128)(2,1)} %param.13) | data formatting | bytes 12582912 | tf_op args[2]
  18.7 10.3 %fusion.12 = f32[1024,3,4,128]{3,0,2,1:T(8,128)S(1)} fusion(bf16[3,4,128,2048]{3,2,1,0:T(8,128)(2,1)} %bitcast.165, bf16[1024,2048]{1,0:T(8,128)(2,1)} %param.11, f32[2048]{0:T(1024)S(1)} %copy-done.15, f32[1024]{0:T(1024)S(1)} %add_rsqrt_fusion.6), kind=kOutput, calls=%fused_computation.21 | convolution fusion | flops 6450839552 | bytes 16789504 | tf_op jit(solution)/shard_map/dot_general | solution.py:60
  29.0 1.1 slice.199
  30.1 1.0 select_convert_fusion.4
  31.1 2.6 fusion.56
  33.7 2.7 fusion.57
  36.4 2.0 fusion.73
  38.5 8.7 %all-gather = bf16[16,128,128]{2,1,0:T(8,128)(2,1)S(1)} all-gather(bf16[4,128,128]{2,1,0:T(8,128)(2,1)S(1)} %get-tuple-element.27), channel_id=2, replica_groups=mesh['groups'=2,'ctx'=4,'head'=4] {'ctx'}, dimensions={0}, use_global_device_ids=true | all-gather | bytes 655360 | tf_op jit(solution)/shard_map/all_gather | solution.py:74
  47.2 0.2 fusion.50
  47.4 0.3 fusion.59
  47.7 0.3 convolution_add_fusion
  48.1 0.4 fusion.58
  48.5 0.4 convolution_add_fusion.1
  48.8 1.1 copy-done.3
  49.9 0.3 copy-done.4
  50.2 0.9 fusion.18
  51.1 0.6 copy-done.2
  51.7 0.9 fusion.17
  52.6 1.1 multiply_reduce_fusion.4
  53.6 0.0 copy-start.12
  53.7 1.1 multiply_reduce_fusion.5
  54.8 0.3 multiply_convert_fusion.4
  55.1 2.6 convolution_convert_fusion.1
  57.6 0.0 all-reduce.3.cloned.1.call-update
  57.7 0.0 all-reduce.5.cloned.1.call-start
  57.7 2.6 convolution_convert_fusion.2
  60.3 84.4 %all-reduce.3.cloned.1.call-done = bf16[512,2048]{1,0:T(8,128)(2,1)} async-done(((bf16[512,2048]{1,0:T(8,128)(2,1)}), bf16[512,2048]{1,0:T(8,128)(2,1)}) %all-reduce.3.cloned.1.call-update) | async-done | bytes 2097168 | tf_op jit(solution)/shard_map/psum | solution.py:108
  144.7 3.2 fusion.5
  147.9 0.0 all-reduce.5.cloned.1.call-update
  147.9 0.3 reduce-scatter.2.cloned.1.call-start
  148.2 9.3 %copy.71 = bf16[2048,3,512]{0,2,1:T(8,128)(2,1)} copy(bf16[2048,3,512]{2,0,1:T(8,128)(2,1)} %param.17) | data formatting | bytes 12582912 | tf_op args[6]
  157.5 5.7 %fusion.25 = f32[512,3,4,128]{3,0,2,1:T(8,128)S(1)} fusion(bf16[3,4,128,2048]{3,2,1,0:T(8,128)(2,1)} %bitcast.163, bf16[512,2048]{1,0:T(8,128)(2,1)S(1)} %get-tuple-element.7, f32[2048]{0:T(1024)S(1)} %copy-done.16, f32[512]{0:T(512)S(1)} %add_rsqrt_fusion.8), kind=kOutput, calls=%fused_computation.45 | convolution fusion | flops 3225419776 | bytes 11544576 | tf_op jit(solution)/shard_map/dot_general | solution.py:114
  163.3 0.6 multiply_reduce_fusion.3
  163.9 1.0 copy-done.7
  165.0 0.1 fusion.54
  165.0 68.5 %all-reduce.5.cloned.1.call-done = bf16[512,2048]{1,0:T(8,128)(2,1)} async-done(((bf16[512,2048]{1,0:T(8,128)(2,1)}), bf16[512,2048]{1,0:T(8,128)(2,1)}) %all-reduce.5.cloned.1.call-update) | async-done | bytes 2097168 | tf_op jit(solution)/shard_map/psum | solution.py:108
  233.5 3.2 fusion.8
  236.7 6.5 %fusion.22 = f32[512,3,4,128]{3,0,2,1:T(8,128)S(1)} fusion(bf16[3,4,128,2048]{3,2,1,0:T(8,128)(2,1)} %bitcast.164, bf16[512,2048]{1,0:T(8,128)(2,1)S(1)} %get-tuple-element.16, f32[512]{0:T(512)S(1)} %add_rsqrt_fusion.7, f32[2048]{0:T(1024)S(1)} %copy-done.16), kind=kOutput, calls=%fused_computation.43 | convolution fusion | flops 3225419776 | bytes 11544576 | tf_op jit(solution)/shard_map/dot_general | solution.py:114
  243.3 0.6 multiply_reduce_fusion.2
  243.9 0.1 fusion.55
  244.0 0.1 maximum_bitcast_fusion.1
  244.1 1.0 copy-done.8
  245.1 1.4 multiply_convert_fusion.2
  246.5 0.1 maximum_bitcast_fusion
  246.6 1.5 pad_maximum_fusion.1
  248.1 4.0 copy.72
  252.1 2.6 collective-permute-start.1
  254.7 3.2 collective-permute-start
  258.0 0.1 and_reduce_fusion
  258.1 0.1 broadcast_bitcast_fusion
  258.2 1.0 pad_maximum_fusion.2
  259.2 20.6 %collective-permute-done.1 = bf16[1024,1024]{0,1:T(8,128)(2,1)} collective-permute-done((bf16[1024,1024]{0,1:T(8,128)(2,1)}, bf16[1024,1024]{0,1:T(8,128)(2,1)}, u32[]{:S(2)}, u32[]{:S(2)}) %collective-permute-start.1) | collective-permute-done | bytes 2097184 | tf_op jit(solution)/shard_map/ppermute | solution.py:24
  279.8 3.9 copy.74
  283.7 4.0 copy.73
  287.7 3.1 pad_maximum_fusion
  290.8 19.7 %fusion = (f32[4,4,256]{2,0,1:T(4,128)S(1)}, f32[4,3072,4,256]{3,1,2,0:T(8,128)}) fusion(pred[4,3072]{1,0:T(4,128)(4,1)S(1)} %bitcast.174, bf16[4,256,4,128]{3,1,0,2:T(8,128)(2,1)S(1)} %bitcast.170, bf16[3072,2,4,128]{3,0,2,1:T(8,128)(2,1)S(1)} %pad_maximum_fusion), kind=kOutput, calls=%fused_computation.2 | convolution fusion | flops 3258970112 | bytes 54554624 | tf_op jit(solution)/shard_map/pthe,she->phts/dot_general | solution.py:141
  310.5 22.4 %fusion.40 = bf16[4,256,4,128]{1,3,0,2:T(8,128)(2,1)S(1)} fusion(f32[4,3072,4,256]{3,1,2,0:T(8,128)} %get-tuple-element.34, f32[4,4,256]{2,0,1:T(4,128)S(1)} %get-tuple-element.33, pred[4,3072]{1,0:T(4,128)(4,1)S(1)} %bitcast.175, bf16[3072,2,4,128]{3,0,2,1:T(8,128)(2,1)S(1)} %pad_maximum_fusion), kind=kOutput, calls=%fused_computation.64 | convolution fusion | flops 3272081408 | bytes 54554624 | tf_op jit(solution)/shard_map/phts,she->pthe/dot_general | solution.py:148
  332.9 0.7 copy.77
  333.5 5.9 %convolution_convert_fusion = bf16[1024,2048]{1,0:T(8,128)(2,1)} fusion(bf16[512,2048]{1,0:T(8,128)(2,1)} %param.20, bf16[128,8,4,128]{3,2,1,0:T(4,128)(2,1)S(1)} %bitcast.171), kind=kOutput, calls=%fused_computation.32 | convolution fusion | flops 2149580800 | bytes 7340032 | tf_op jit(solution)/shard_map/dot_general | solution.py:151
  339.4 0.0 reduce-scatter.2.cloned.1.call-update
  339.4 74.7 %reduce-scatter.2.cloned.1.call-done = bf16[256,2048]{1,0:T(8,128)(2,1)} async-done(((bf16[1024,2048]{1,0:T(8,128)(2,1)}), bf16[256,2048]{1,0:T(8,128)(2,1)}) %reduce-scatter.2.cloned.1.call-update) | async-done | bytes 1048592 | tf_op jit(solution)/shard_map/reduce_scatter | solution.py:150
  414.1 3.3 add_convert_fusion.2
  (42 shorter events, 0.2 us)
Async XLA Ops:
  6.5 48.5 %copy-start = (bf16[512,2048]{1,0:T(8,128)(2,1)S(1)}, bf16[512,2048]{1,0:T(8,128)(2,1)}, u32[]{:S(2)}) copy-start(bf16[512,2048]{1,0:T(8,128)(2,1)} %param.15) | copy-start | bytes 6291460
  6.5 138.1 %all-reduce.3.cloned.1.call-start = ((), (), s32[]{:S(2)}) async-start(), calls=%async_computation.1 | async-start | bytes 4194304 | tf_op jit(solution)/shard_map/psum | solution.py:108
  9.8 8.9 %copy-start.15 = (f32[2048]{0:T(1024)S(1)}, f32[2048]{0:T(1024)}, u32[]{:S(2)}) copy-start(f32[2048]{0:T(1024)} %param.12) | copy-start | bytes 24580
  31.1 2.6 copy-start.9
  47.7 2.2 copy-start.3
  47.7 2.5 copy-start.4
  48.4 3.2 copy-start.2
  53.6 1.1 copy-start.12
  57.7 175.9 %all-reduce.5.cloned.1.call-start = ((), (), s32[]{:S(2)}) async-start(), calls=%async_computation.2 | async-start | bytes 4194304 | tf_op jit(solution)/shard_map/psum | solution.py:108
  147.9 9.7 %copy-start.5 = (bf16[512,2048]{1,0:T(8,128)(2,1)}, bf16[512,2048]{1,0:T(8,128)(2,1)S(1)}, u32[]{:S(2)}) copy-start(bf16[512,2048]{1,0:T(8,128)(2,1)S(1)} %get-tuple-element.7) | copy-start | bytes 6291460
  147.9 9.6 %copy-start.16 = (f32[2048]{0:T(1024)S(1)}, f32[2048]{0:T(1024)}, u32[]{:S(2)}) copy-start(f32[2048]{0:T(1024)} %param.16) | copy-start | bytes 24580
  147.9 266.2 %reduce-scatter.2.cloned.1.call-start = ((), (), s32[]{:S(2)}) async-start(), calls=%async_computation.3 | async-start | bytes 5242880 | tf_op jit(solution)/shard_map/reduce_scatter | solution.py:150
  163.3 1.7 copy-start.7
  236.7 6.5 %copy-start.6 = (bf16[512,2048]{1,0:T(8,128)(2,1)}, bf16[512,2048]{1,0:T(8,128)(2,1)S(1)}, u32[]{:S(2)}) copy-start(bf16[512,2048]{1,0:T(8,128)(2,1)S(1)} %get-tuple-element.16) | copy-start | bytes 6291460
  243.2 1.9 copy-start.8
  243.3 1.9 copy-start.13
  243.3 1.9 copy-start.14
  246.6 11.3 %copy-start.11 = (s32[4,8]{1,0:T(4,128)S(1)}, s32[4,8]{1,0:T(4,128)}, u32[]{:S(2)}) copy-start(s32[4,8]{1,0:T(4,128)} %param.21) | copy-start | bytes 388
  252.1 27.7 %collective-permute-start.1 = (bf16[1024,1024]{0,1:T(8,128)(2,1)}, bf16[1024,1024]{0,1:T(8,128)(2,1)}, u32[]{:S(2)}, u32[]{:S(2)}) collective-permute-start(bf16[1024,1024]{0,1:T(8,128)(2,1)} %bitcast.168), channel_id=1, source_target_pairs={{4,0},{8,4},{12,8},{5,1},{9,5},{13,9},{6,2},{10,6},{14,10},{7,3},{... | collective-permute-start | bytes 6291464 | tf_op jit(solution)/shard_map/ppermute | solution.py:24
  254.7 29.0 %collective-permute-start = (bf16[1024,1024]{0,1:T(8,128)(2,1)}, bf16[1024,1024]{0,1:T(8,128)(2,1)}, u32[]{:S(2)}, u32[]{:S(2)}) collective-permute-start(bf16[1024,1024]{0,1:T(8,128)(2,1)} %bitcast.169), channel_id=1, source_target_pairs={{0,4},{4,8},{8,12},{1,5},{5,9},{9,13},{2,6},{6,10},{10,14},{3,7},{... | collective-permute-start | bytes 6291464 | tf_op jit(solution)/shard_map/ppermute | solution.py:23
  287.7 3.1 copy-start.10
  339.4 78.0 %copy-start.1 = (bf16[512,2048]{1,0:T(8,128)(2,1)S(1)}, bf16[512,2048]{1,0:T(8,128)(2,1)}, u32[]{:S(2)}) copy-start(bf16[512,2048]{1,0:T(8,128)(2,1)} %param.15) | copy-start | bytes 6291460
Sparse Core Ops, SparseCore 0:
  57.8 86.8 all-reduce.2
  148.0 85.4 all-reduce.4
  339.6 74.5 reduce-scatter.1

commit v2 on v1

--- a/solution.py
+++ b/solution.py
@@ -2,6 +2,7 @@
 
 import jax
 import jax.numpy as jnp
+import numpy as np
 from jax import lax
 from jax.sharding import PartitionSpec as P
 
@@ -121,38 +122,64 @@
     key_hat = jnp.concatenate(k_parts, axis=0)
     value_two = jnp.concatenate(v_parts, axis=0)
 
-    key_value = jnp.stack([key_hat, value_two], axis=1).reshape(tok_rows, 2 * inner_dev)
     plane_tiles = GY * GZ
-    widened = with_halo(key_value, (("ctx", 0),), plane_tiles * TILE)
-    buffer_rows = widened.shape[0]
-    buffer_tiles = buffer_rows // TILE
+    halo_rows = plane_tiles * TILE
     tile_count = tok_rows // TILE
-    base_tile = ctx_index * tile_count - plane_tiles
-    widened = widened.reshape(buffer_rows, 2, heads_dev, head_dim)
-    buffer_ids = base_tile + jnp.arange(buffer_tiles, dtype=jnp.int32)
-    valid = jnp.any(
-        (neighbours[:, :, None] == buffer_ids[None, None, :]) & (neighbours[:, :, None] >= 0),
-        axis=1,
-    )
-    valid_keys = jnp.repeat(valid, TILE, axis=1)
-    query_tiles = query_hat.reshape(tile_count, TILE, heads_dev, head_dim)
+    head_size = lax.axis_size("head")
+    up = [(i, i + 1) for i in range(ctx_size - 1)]
+    down = [(i + 1, i) for i in range(ctx_size - 1)]
+    key_prev = lax.ppermute(key_hat[tok_rows - halo_rows :], "ctx", up)
+    value_prev = lax.ppermute(value_two[tok_rows - halo_rows :], "ctx", up)
+    key_next = lax.ppermute(key_hat[:halo_rows], "ctx", down)
+    value_next = lax.ppermute(value_two[:halo_rows], "ctx", down)
+    own_first = ctx_index * tile_count
+    arange_halo = jnp.arange(plane_tiles, dtype=jnp.int32)
+    pieces = (
+        (key_prev, value_prev, own_first - plane_tiles + arange_halo),
+        (key_hat, value_two, own_first + jnp.arange(tile_count, dtype=jnp.int32)),
+        (key_next, value_next, own_first + tile_count + arange_halo),
+    )
+    present = neighbours >= 0
+    tile_masks = [
+        jnp.any((neighbours[:, :, None] == ids[None, None, :]) & present[:, :, None], axis=1)
+        for _, _, ids in pieces
+    ]
     score_scale = 1.0 / math.sqrt(head_dim)
-    tile_scores = (
-        jnp.einsum(
-            "pthe,she->phts", query_tiles, widened[:, 0], preferred_element_type=f32
+    chunks = 2 if rows_mine % 2 == 0 else 1
+    part_rows = rows_mine // chunks
+    mixed_parts = []
+    for c in range(chunks):
+        rows = (
+            np.arange(head_size)[:, None] * rows_mine + c * part_rows + np.arange(part_rows)[None, :]
+        ).reshape(-1)
+        row_tiles = rows // TILE
+        q_c = query_hat.reshape(head_size, chunks, part_rows, heads_dev, head_dim)[:, c]
+        q_c = q_c.reshape(head_size * part_rows, heads_dev, head_dim)
+        exps, total = [], 0.0
+        for (keys, _, _), mask in zip(pieces, tile_masks):
+            key_ok = jnp.repeat(mask[row_tiles], TILE, axis=1)
+            scores = (
+                jnp.einsum("the,she->hts", q_c, keys, preferred_element_type=f32) * score_scale
+            )
+            unnormed = jnp.where(key_ok[None], jnp.exp(scores), 0.0)
+            exps.append(unnormed)
+            total = total + jnp.sum(unnormed, axis=-1, keepdims=True)
+        attn_c = 0.0
+        for (_, values, _), unnormed in zip(pieces, exps):
+            weights = (unnormed / total).astype(bf16)
+            attn_c = attn_c + jnp.einsum(
+                "hts,she->the", weights, values, preferred_element_type=f32
+            )
+        attn_c = attn_c.astype(bf16).reshape(head_size * part_rows, inner_dev)
+        mixed_parts.append(
+            lax.psum_scatter(
+                jnp.dot(attn_c, w_out2, preferred_element_type=f32).astype(bf16),
+                "head",
+                scatter_dimension=0,
+                tiled=True,
+            )
         )
-        * score_scale
-    )
-    unnormed = jnp.where(valid_keys[:, None, None, :], jnp.exp(tile_scores), 0.0)
-    weights = (unnormed / jnp.sum(unnormed, axis=-1, keepdims=True)).astype(bf16)
-    attn_two = jnp.einsum("phts,she->pthe", weights, widened[:, 1], preferred_element_type=f32)
-    attn_two = attn_two.astype(bf16).reshape(tok_rows, inner_dev)
-    summed_two = lax.psum_scatter(
-        jnp.dot(attn_two, w_out2, preferred_element_type=f32).astype(bf16),
-        "head",
-        scatter_dimension=0,
-        tiled=True,
-    ).astype(f32)
+    summed_two = jnp.concatenate(mixed_parts, axis=0).astype(f32)
     residual_mine = lax.dynamic_slice_in_dim(residual, head_index * rows_mine, rows_mine, 0)
     return (residual_mine.astype(f32) + summed_two).astype(bf16)
 

time: 426 us -> 410 us (0.962); the launches traced: 424 us -> 403 us
  waiting for transfers between devices: 248 us -> 218 us
  matrix products: 88.3 us -> 98.3 us
  starting transfers between devices: 6.13 us -> 12 us
  other arithmetic: 23 us -> 18.7 us
    ppermute x2 -> x4, waiting for transfers between devices: 20.6 us -> 7.01 us  [the longest x1 7 us: on_device(): key_prev = lax.ppermute(key_hat[tok_rows - halo_rows:], 'ctx', up)]
    psum x2, waiting for transfers between devices: 153 us -> 142 us  [on_device(): summed = lax.psum(partial, 'head').astype(f32)]
    dot_general x3 -> x14, matrix products: 47.9 us -> 57.9 us  [the longest x6 28 us: on_device(): jnp.einsum('hts,she->the', weights, values, preferred_element_type=f32)]
    concatenate x2 -> x0, local copies, waits for them, and re-layouts: 7.9 us -> none  [with_halo(): shard = jnp.concatenate([before, shard, after], axis=dim)]
    ppermute x2 -> x4, starting transfers between devices: 5.82 us -> 11.6 us  [the longest x1 3.74 us: on_device(): key_prev = lax.ppermute(key_hat[tok_rows - halo_rows:], 'ctx', up)]
    reduce_scatter x1 -> x2, waiting for transfers between devices: 74.7 us -> 69.1 us  [on_device(): lax.psum_scatter(jnp.dot(attn_c, w_out2, preferred_element_type=f32).asty...]
    broadcast_in_dim x0 -> x3, local copies, waits for them, and re-layouts: none -> 4.8 us  [on_device(): key_ok = jnp.repeat(mask[row_tiles], TILE, axis=1)]
    unnamed x38 -> x55, local copies, waits for them, and re-layouts: 22.4 us -> 23.2 us
  transfers between devices with their start and end apart: 5 -> 8, of which waited for: 4 -> 5; matrix products, arithmetic and copies ran while one was open for 6% -> 20% of each run, Pallas kernels for 0% -> 0%
where the time goes in v2:
time: 410 us; the launch traced here: 403 us
  waiting for transfers between devices  218 us (53%)
  matrix products  98.3 us (24%)
  local copies, waits for them, and re-layouts  32.8 us (8%)
  other arithmetic  18.7 us (5%)
  between operations  14.1 us (3%)
  starting transfers between devices  12 us (3%)
  blocking collectives  8.76 us (2%)
    psum x2, waiting for transfers between devices, on_device(): summed = lax.psum(partial, 'head').astype(f32)  142 us
    reduce_scatter x2, waiting for transfers between devices, on_device(): lax.psum_scatter(jnp.dot(attn_c, w_out2, preferred_element_type=f32).asty...  69.1 us
    dot_general x6, matrix products, on_device(): jnp.einsum('hts,she->the', weights, values, preferred_element_type=f32)  28 us
    dot_general x6, matrix products, on_device(): jnp.einsum('the,she->hts', q_c, keys, preferred_element_type=f32)  24.6 us
    unnamed x55, local copies, waits for them, and re-layouts  23.2 us
    dot_general x2, matrix products, on_device(): proj_n = jnp.dot(normed_n, w_qkv2_flat, preferred_element_type=f32)  12.2 us
    reduce_sum x5, other arithmetic, rms_rows(): mean_sq = jnp.mean(value * value, axis=-1, keepdims=True)  10.8 us
    dot_general x1, matrix products, on_device(): jnp.dot(normed, w_qkv1.reshape(feature_width, 3 * inner_dev), preferred_e...  10.3 us
  transfers between devices with their start and end apart: 8, of which 5 were waited for; matrix products, arithmetic and copies ran while one was open for 20% of the time, Pallas kernels for 0%

profile of v2, /device:TPU:1, one launch (start us, length us, event | category | flops | bytes accessed | tf_op | source)
XLA Modules:
  0.0 402.9 jit_solution(9763360756637188600)
XLA Ops:
  6.6 3.2 fusion
  9.9 8.8 %copy.72 = bf16[2048,3,512]{0,2,1:T(8,128)(2,1)} copy(bf16[2048,3,512]{2,0,1:T(8,128)(2,1)} %param.21) | data formatting | bytes 12582912 | tf_op args[2]
  18.7 10.3 %fusion.16 = f32[1024,3,4,128]{3,0,2,1:T(8,128)S(1)} fusion(bf16[3,4,128,2048]{3,2,1,0:T(8,128)(2,1)} %bitcast.151, bf16[1024,2048]{1,0:T(8,128)(2,1)} %param.19, f32[2048]{0:T(1024)S(1)} %copy-done.23, f32[1024]{0:T(1024)S(1)} %add_rsqrt_fusion.6), kind=kOutput, calls=%fused_computation.37 | convolution fusion | flops 6450839552 | bytes 16789504 | tf_op jit(solution)/shard_map/dot_general | solution.py:61
  29.0 1.1 slice.197
  30.1 1.0 select_convert_fusion.4
  31.1 2.6 fusion.67
  33.7 2.7 fusion.68
  36.4 2.0 fusion.97
  38.4 8.8 %all-gather = bf16[16,128,128]{2,1,0:T(8,128)(2,1)S(1)} all-gather(bf16[4,128,128]{2,1,0:T(8,128)(2,1)S(1)} %get-tuple-element.38), channel_id=2, replica_groups=mesh['groups'=2,'ctx'=4,'head'=4] {'ctx'}, dimensions={0}, use_global_device_ids=true | all-gather | bytes 655360 | tf_op jit(solution)/shard_map/all_gather | solution.py:75
  47.4 0.3 fusion.70
  47.8 0.3 convolution_add_fusion
  48.1 0.4 fusion.69
  48.5 0.4 convolution_add_fusion.1
  48.8 1.1 copy-done.3
  50.2 0.9 fusion.27
  51.1 0.6 copy-done.2
  51.7 0.9 fusion.26
  52.6 1.1 multiply_reduce_fusion.4
  53.7 1.1 multiply_reduce_fusion.5
  55.1 2.6 convolution_convert_fusion.2
  57.8 0.4 and_reduce_fusion.1
  58.2 2.6 convolution_convert_fusion.3
  60.8 84.0 %all-reduce.3.cloned.1.call-done = bf16[512,2048]{1,0:T(8,128)(2,1)} async-done(((bf16[512,2048]{1,0:T(8,128)(2,1)}), bf16[512,2048]{1,0:T(8,128)(2,1)}) %all-reduce.3.cloned.1.call-update) | async-done | bytes 2097168 | tf_op jit(solution)/shard_map/psum | solution.py:109
  144.7 3.2 fusion.9
  148.3 1.2 gather_fusion.2
  149.5 1.2 gather_fusion.1
  150.7 1.2 gather_fusion
  151.8 1.6 broadcast_in_dim.151
  153.7 1.6 broadcast_in_dim.156
  155.3 1.1 copy.110
  156.4 1.6 broadcast_in_dim.160
  158.0 1.0 copy.111
  159.0 8.9 %copy.83 = bf16[2048,3,512]{0,2,1:T(8,128)(2,1)} copy(bf16[2048,3,512]{2,0,1:T(8,128)(2,1)} %param.25) | data formatting | bytes 12582912 | tf_op args[6]
  167.9 5.7 %fusion.34 = f32[512,3,4,128]{3,0,2,1:T(8,128)S(1)} fusion(bf16[3,4,128,2048]{3,2,1,0:T(8,128)(2,1)} %bitcast.149, bf16[512,2048]{1,0:T(8,128)(2,1)S(1)} %get-tuple-element.7, f32[2048]{0:T(1024)S(1)} %copy-done.24, f32[512]{0:T(512)S(1)} %add_rsqrt_fusion.8), kind=kOutput, calls=%fused_computation.65 | convolution fusion | flops 3225419776 | bytes 11544576 | tf_op jit(solution)/shard_map/dot_general | solution.py:115
  173.7 0.6 multiply_reduce_fusion.1
  174.3 1.0 copy-done.7
  175.4 58.2 %all-reduce.5.cloned.1.call-done = bf16[512,2048]{1,0:T(8,128)(2,1)} async-done(((bf16[512,2048]{1,0:T(8,128)(2,1)}), bf16[512,2048]{1,0:T(8,128)(2,1)}) %all-reduce.5.cloned.1.call-update) | async-done | bytes 2097168 | tf_op jit(solution)/shard_map/psum | solution.py:109
  233.6 3.2 fusion.12
  236.8 6.5 %fusion.31 = f32[512,3,4,128]{3,0,2,1:T(8,128)S(1)} fusion(bf16[3,4,128,2048]{3,2,1,0:T(8,128)(2,1)} %bitcast.150, bf16[512,2048]{1,0:T(8,128)(2,1)S(1)} %get-tuple-element.25, f32[512]{0:T(512)S(1)} %add_rsqrt_fusion.7, f32[2048]{0:T(1024)S(1)} %copy-done.24), kind=kOutput, calls=%fused_computation.63 | convolution fusion | flops 3225419776 | bytes 11544576 | tf_op jit(solution)/shard_map/dot_general | solution.py:115
  243.3 0.6 multiply_reduce_fusion
  244.0 1.0 pad_maximum_fusion
  245.1 2.6 collective-permute-start.3
  247.7 3.0 collective-permute-start
  250.7 1.4 multiply_convert_fusion
  252.2 2.3 collective-permute-start.2
  254.5 3.7 collective-permute-start.1
  258.5 1.3 fusion.94
  259.7 7.1 %fusion.4 = (f32[4,512]{1,0:T(4,128)S(1)}, f32[4,512]{1,0:T(4,128)S(1)}, f32[4,512,1024]{2,1,0:T(8,128)}) fusion(pred[512,1024]{1,0:T(8,128)(4,1)S(1)} %bitcast.164, f32[4,512,1024]{2,1,0:T(8,128)S(1)} %fusion.94, bf16[512,4,128]{2,0,1:T(8,128)(2,1)S(1)} %bitcast.168, bf16[512,4,128]{2,0,1:T(8,128)(2,1)S(1)} %get-tuple-element.30, ...), kind=kOutput, calls=%fused_computation.21 | convolution fusion | flops 551546880 | bytes 18890752 | tf_op jit(solution)/shard_map/the,she->hts/dot_general | solution.py:162
  266.8 7.0 %collective-permute-done.1 = bf16[1024,4,128]{2,0,1:T(8,128)(2,1)S(1)} collective-permute-done((bf16[1024,4,128]{2,0,1:T(8,128)(2,1)S(1)}, bf16[1024,4,128]{2,0,1:T(8,128)(2,1)S(1)}, u32[]{:S(2)}, u32[]{:S(2)}) %collective-permute-start.1) | collective-permute-done | bytes 1048608 | tf_op jit(solution)/shard_map/ppermute | solution.py:131
  273.8 1.3 fusion.98
  275.1 1.3 fusion.99
  276.4 6.8 %fusion.3 = (f32[4,512]{1,0:T(4,128)S(1)}, f32[4,512]{1,0:T(4,128)S(1)}, f32[4,512,1024]{2,1,0:T(8,128)}) fusion(pred[512,1024]{1,0:T(8,128)(4,1)S(1)} %bitcast.158, f32[4,512,1024]{2,1,0:T(8,128)S(1)} %fusion.98, bf16[512,4,128]{2,0,1:T(8,128)(2,1)} %bitcast.169, bf16[1024,4,128]{2,0,1:T(8,128)(2,1)S(1)} %copy-done.11), kind=kOutput, calls=%fused_computation.20 | convolution fusion | flops 549449728 | bytes 18890752 | tf_op jit(solution)/shard_map/the,she->hts/dot_general | solution.py:162
  283.2 6.9 %fusion.5 = (f32[4,512]{1,0:T(4,128)S(1)}, f32[4,512]{1,0:T(4,128)S(1)}, f32[4,512,1024]{2,1,0:T(8,128)}) fusion(pred[512,1024]{1,0:T(8,128)(4,1)S(1)} %bitcast.161, f32[4,512,1024]{2,1,0:T(8,128)S(1)} %fusion.99, bf16[512,4,128]{2,0,1:T(8,128)(2,1)} %bitcast.170, bf16[1024,4,128]{2,0,1:T(8,128)(2,1)S(1)} %collective-permute-done.2), kind=kOutput, calls=%fused_computation.22 | convolution fusion | flops 549449728 | bytes 18890752 | tf_op jit(solution)/shard_map/the,she->hts/dot_general | solution.py:162
  290.2 3.9 fusion.25
  294.1 2.7 fusion.24
  296.8 4.2 %fusion.59 = bf16[4,128,512]{2,1,0:T(8,128)(2,1)S(1)} fusion(f32[4,128,512]{2,1,0:T(8,128)S(1)} %fusion.25, f32[4,128,512]{2,1,0:T(8,128)S(1)} %fusion.24, bf16[1024,4,128]{2,0,1:T(8,128)(2,1)} %collective-permute-done, f32[4,512,1024]{2,1,0:T(8,128)S(1)} %fusion.98, f32[4,512]{1,0:T(4,128)S(1)} %add_add_fusion, pred[512,1024]{1,0:T(8,128)(4,1)S(1)} %bitcast.159), kind=kOutput, calls=%fused_computation.95 | convolution fusion | flops 546045952 | bytes 12591104 | tf_op jit(solution)/shard_map/hts,she->the/dot_general | solution.py:170
  300.9 2.6 convolution_convert_fusion
  303.7 5.3 %fusion.21 = f32[4,128,512]{2,1,0:T(8,128)S(1)} fusion(f32[4,512,1024]{2,1,0:T(8,128)} %get-tuple-element.46, f32[4,512]{1,0:T(4,128)S(1)} %add_add_fusion.1, pred[512,1024]{1,0:T(8,128)(4,1)S(1)} %bitcast.166, bf16[512,4,128]{2,0,1:T(8,128)(2,1)S(1)} %fusion.66, bf16[512,4,128]{2,0,1:T(8,128)(2,1)S(1)} %fusion.65), kind=kOutput, calls=%fused_computation.47 | convolution fusion | flops 547356672 | bytes 11018240 | tf_op jit(solution)/shard_map/hts,she->the/dot_general | solution.py:170
  309.0 5.5 %fusion.22 = f32[4,128,512]{2,1,0:T(8,128)S(1)} fusion(bf16[1024,4,128]{2,0,1:T(8,128)(2,1)} %collective-permute-done.3, f32[4,512,1024]{2,1,0:T(8,128)} %get-tuple-element.44, f32[4,512]{1,0:T(4,128)S(1)} %add_add_fusion.1, pred[512,1024]{1,0:T(8,128)(4,1)S(1)} %bitcast.163), kind=kOutput, calls=%fused_computation.48 | convolution fusion | flops 545259520 | bytes 11018240 | tf_op jit(solution)/shard_map/hts,she->the/dot_general | solution.py:170
  314.5 6.5 %fusion.58 = bf16[4,128,512]{2,1,0:T(8,128)(2,1)S(1)} fusion(f32[4,128,512]{2,1,0:T(8,128)S(1)} %fusion.22, f32[4,128,512]{2,1,0:T(8,128)S(1)} %fusion.21, bf16[1024,4,128]{2,0,1:T(8,128)(2,1)} %collective-permute-done, f32[4,512,1024]{2,1,0:T(8,128)} %get-tuple-element.45, f32[4,512]{1,0:T(4,128)S(1)} %add_add_fusion.1, pred[512,1024]{1,0:T(8,128)(4,1)S(1)} %bitcast.160), kind=kOutput, calls=%fused_computation.94 | convolution fusion | flops 546045952 | bytes 12591104 | tf_op jit(solution)/shard_map/hts,she->the/dot_general | solution.py:170
  321.0 2.6 convolution_convert_fusion.1
  323.7 23.6 %reduce-scatter.5.cloned.1.call-done = bf16[128,2048]{1,0:T(8,128)(2,1)} async-done(((bf16[512,2048]{1,0:T(8,128)(2,1)}), bf16[128,2048]{1,0:T(8,128)(2,1)}) %reduce-scatter.5.cloned.1.call-update) | async-done | bytes 524304 | tf_op jit(solution)/shard_map/reduce_scatter | solution.py:175
  347.3 45.5 %reduce-scatter.3.cloned.1.call-done = bf16[128,2048]{1,0:T(8,128)(2,1)} async-done(((bf16[512,2048]{1,0:T(8,128)(2,1)}), bf16[128,2048]{1,0:T(8,128)(2,1)}) %reduce-scatter.3.cloned.1.call-update) | async-done | bytes 524304 | tf_op jit(solution)/shard_map/reduce_scatter | solution.py:175
  392.8 3.3 add_convert_fusion.2
  (82 shorter events, 2.1 us)
Async XLA Ops:
  6.5 48.5 %copy-start = (bf16[512,2048]{1,0:T(8,128)(2,1)S(1)}, bf16[512,2048]{1,0:T(8,128)(2,1)}, u32[]{:S(2)}) copy-start(bf16[512,2048]{1,0:T(8,128)(2,1)} %param.23) | copy-start | bytes 6291460
  6.5 138.2 %all-reduce.3.cloned.1.call-start = ((), (), s32[]{:S(2)}) async-start(), calls=%async_computation.2 | async-start | bytes 4194304 | tf_op jit(solution)/shard_map/psum | solution.py:109
  9.8 8.9 %copy-start.23 = (f32[2048]{0:T(1024)S(1)}, f32[2048]{0:T(1024)}, u32[]{:S(2)}) copy-start(f32[2048]{0:T(1024)} %param.20) | copy-start | bytes 24580
  31.1 2.6 copy-start.9
  47.7 2.2 copy-start.3
  47.7 2.5 copy-start.4
  48.5 3.2 copy-start.2
  53.7 1.1 copy-start.18
  55.1 2.7 copy-start.16
  57.7 175.9 %all-reduce.5.cloned.1.call-start = ((), (), s32[]{:S(2)}) async-start(), calls=%async_computation.3 | async-start | bytes 4194304 | tf_op jit(solution)/shard_map/psum | solution.py:109
  60.8 87.5 %copy-start.17 = (s32[512]{0:T(512)S(1)}, s32[512]{0:T(512)}, u32[]{:S(2)}) copy-start(s32[512]{0:T(512)} %constant.53) | copy-start | bytes 6148
  147.9 20.0 %copy-start.5 = (bf16[512,2048]{1,0:T(8,128)(2,1)}, bf16[512,2048]{1,0:T(8,128)(2,1)S(1)}, u32[]{:S(2)}) copy-start(bf16[512,2048]{1,0:T(8,128)(2,1)S(1)} %get-tuple-element.7) | copy-start | bytes 6291460
  148.0 199.4 %reduce-scatter.5.cloned.1.call-start = ((), (), s32[]{:S(2)}) async-start(), calls=%async_computation.5 | async-start | bytes 2621440 | tf_op jit(solution)/shard_map/reduce_scatter | solution.py:175
  159.0 8.9 %copy-start.24 = (f32[2048]{0:T(1024)S(1)}, f32[2048]{0:T(1024)}, u32[]{:S(2)}) copy-start(f32[2048]{0:T(1024)} %param.24) | copy-start | bytes 24580
  173.6 1.7 copy-start.7
  236.8 6.5 %copy-start.6 = (bf16[512,2048]{1,0:T(8,128)(2,1)}, bf16[512,2048]{1,0:T(8,128)(2,1)S(1)}, u32[]{:S(2)}) copy-start(bf16[512,2048]{1,0:T(8,128)(2,1)S(1)} %get-tuple-element.25) | copy-start | bytes 6291460
  243.3 7.4 %copy-start.8 = (f32[512,3,4,128]{3,0,2,1:T(8,128)S(1)}, f32[512,3,4,128]{3,0,2,1:T(8,128)}, u32[]{:S(2)}) copy-start(f32[512,3,4,128]{3,0,2,1:T(8,128)} %copy-done.7) | copy-start | bytes 9437188
  243.3 7.4 %copy-start.19 = (f32[128]{0:T(128)S(1)}, f32[128]{0:T(128)}, u32[]{:S(2)}) copy-start(f32[128]{0:T(128)} %param.27) | copy-start | bytes 1540
  243.3 7.4 %copy-start.20 = (f32[128]{0:T(128)S(1)}, f32[128]{0:T(128)}, u32[]{:S(2)}) copy-start(f32[128]{0:T(128)} %param.26) | copy-start | bytes 1540
  245.1 45.1 %collective-permute-start.3 = (bf16[1024,4,128]{2,0,1:T(8,128)(2,1)}, bf16[1024,4,128]{2,0,1:T(8,128)(2,1)}, u32[]{:S(2)}, u32[]{:S(2)}) collective-permute-start(bf16[1024,4,128]{2,0,1:T(8,128)(2,1)} %pad_maximum_fusion), channel_id=1, source_target_pairs={{4,0},{8,4},{12,8},{5,1},{9,5},{13,9},{6,2},{10,6},{14,10},{7,3},{... | collective-permute-start | bytes 3145736 | tf_op jit(solution)/shard_map/ppermute | solution.py:134
  247.7 49.1 %collective-permute-start = (bf16[1024,4,128]{2,0,1:T(8,128)(2,1)}, bf16[1024,4,128]{2,0,1:T(8,128)(2,1)}, u32[]{:S(2)}, u32[]{:S(2)}) collective-permute-start(bf16[1024,4,128]{2,0,1:T(8,128)(2,1)} %pad_maximum_fusion), channel_id=1, source_target_pairs={{0,4},{4,8},{8,12},{1,5},{5,9},{9,13},{2,6},{6,10},{10,14},{3,7},{... | collective-permute-start | bytes 3145736 | tf_op jit(solution)/shard_map/ppermute | solution.py:132
  252.2 22.9 %collective-permute-start.2 = (bf16[1024,4,128]{2,0,1:T(8,128)(2,1)S(1)}, bf16[1024,4,128]{2,0,1:T(8,128)(2,1)S(1)}, u32[]{:S(2)}, u32[]{:S(2)}) collective-permute-start(bf16[1024,4,128]{2,0,1:T(8,128)(2,1)S(1)} %pad_maximum_fusion.2), channel_id=1, source_target_pairs={{4,0},{8,4},{12,8},{5,1},{9,5},{13,9},{6,2},{10,6},{14,10},{7,3},{... | collective-permute-start | bytes 3145736 | tf_op jit(solution)/shard_map/ppermute | solution.py:133
  254.5 19.3 %collective-permute-start.1 = (bf16[1024,4,128]{2,0,1:T(8,128)(2,1)S(1)}, bf16[1024,4,128]{2,0,1:T(8,128)(2,1)S(1)}, u32[]{:S(2)}, u32[]{:S(2)}) collective-permute-start(bf16[1024,4,128]{2,0,1:T(8,128)(2,1)S(1)} %pad_maximum_fusion.2), channel_id=1, source_target_pairs={{0,4},{4,8},{8,12},{1,5},{5,9},{9,13},{2,6},{6,10},{10,14},{3,7},{... | collective-permute-start | bytes 3145736 | tf_op jit(solution)/shard_map/ppermute | solution.py:131
  258.4 1.3 copy-start.15
  258.5 1.3 copy-start.13
  273.8 1.3 copy-start.10
  275.1 1.3 copy-start.11
  276.4 6.8 %copy-start.12 = (pred[64,8,4,256]{3,1,2,0:T(8,128)(4,1)S(1)}, pred[64,8,4,256]{3,1,2,0:T(8,128)(4,1)}, u32[]{:S(2)}) copy-start(pred[64,8,4,256]{3,1,2,0:T(8,128)(4,1)} %copy.111) | copy-start | bytes 1572868
  296.7 4.2 %copy-start.21 = (bf16[512,2048]{1,0:T(8,128)(2,1)S(1)}, bf16[512,2048]{1,0:T(8,128)(2,1)}, u32[]{:S(2)}) copy-start(bf16[512,2048]{1,0:T(8,128)(2,1)} %param.28) | copy-start | bytes 6291460
  300.9 2.8 copy-start.14
  303.6 89.2 %reduce-scatter.3.cloned.1.call-start = ((), (), s32[]{:S(2)}) async-start(), calls=%async_computation.4 | async-start | bytes 2621440 | tf_op jit(solution)/shard_map/reduce_scatter | solution.py:175
  314.5 6.6 %copy-start.22 = (bf16[512,2048]{1,0:T(8,128)(2,1)S(1)}, bf16[512,2048]{1,0:T(8,128)(2,1)}, u32[]{:S(2)}) copy-start(bf16[512,2048]{1,0:T(8,128)(2,1)} %param.28) | copy-start | bytes 6291460
  323.7 72.4 %copy-start.1 = (bf16[512,2048]{1,0:T(8,128)(2,1)S(1)}, bf16[512,2048]{1,0:T(8,128)(2,1)}, u32[]{:S(2)}) copy-start(bf16[512,2048]{1,0:T(8,128)(2,1)} %param.23) | copy-start | bytes 6291460
Sparse Core Ops, SparseCore 0:
  57.8 86.8 all-reduce.2
  148.1 85.4 all-reduce.4
  303.7 43.5 reduce-scatter.4
  349.6 43.1 reduce-scatter.2

commit v3 on v2

--- a/solution.py
+++ b/solution.py
@@ -1,9 +1,11 @@
+import functools
 import math
 
 import jax
 import jax.numpy as jnp
 import numpy as np
 from jax import lax
+from jax.experimental import pallas as pl
 from jax.sharding import PartitionSpec as P
 
 TILE = 256
@@ -40,6 +42,52 @@
     high_part = value.astype(jnp.bfloat16)
     low_part = (value - high_part.astype(jnp.float32)).astype(jnp.bfloat16)
     return (high_part, low_part)
+
+
+def _attn_kernel(q_ref, kp_ref, ko_ref, kn_ref, vp_ref, vo_ref, vn_ref, m_ref, o_ref, *, scale):
+    query = q_ref[...]
+    mask = m_ref[0]
+    exps = []
+    total = None
+    offset = 0
+    for k_ref in (kp_ref, ko_ref, kn_ref):
+        rows = k_ref.shape[0]
+        scores = (
+            lax.dot_general(
+                query, k_ref[...], (((1,), (1,)), ((), ())), preferred_element_type=jnp.float32
+            )
+            * scale
+        )
+        unnormed = jnp.where(mask[:, offset : offset + rows] > 0.5, jnp.exp(scores), 0.0)
+        exps.append(unnormed)
+        part = jnp.sum(unnormed, axis=-1, keepdims=True)
+        total = part if total is None else total + part
+        offset += rows
+    acc = None
+    for unnormed, v_ref in zip(exps, (vp_ref, vo_ref, vn_ref)):
+        weights = (unnormed / total).astype(jnp.bfloat16)
+        term = jnp.dot(weights, v_ref[...], preferred_element_type=jnp.float32)
+        acc = term if acc is None else acc + term
+    o_ref[...] = acc.astype(o_ref.dtype)
+
+
+def tile_attention(query, keys, values, mask, block_rows, head_dim, interpret=False):
+    rows, inner = query.shape
+    heads = inner // head_dim
+    blocks = rows // block_rows
+    key_width = mask.shape[-1]
+    kv_specs = [pl.BlockSpec((k.shape[0], head_dim), lambda h, b: (0, h)) for k in keys]
+    return pl.pallas_call(
+        functools.partial(_attn_kernel, scale=1.0 / math.sqrt(head_dim)),
+        out_shape=jax.ShapeDtypeStruct((rows, inner), jnp.bfloat16),
+        grid=(heads, blocks),
+        in_specs=[pl.BlockSpec((block_rows, head_dim), lambda h, b: (b, h))]
+        + kv_specs
+        + kv_specs
+        + [pl.BlockSpec((1, 1, key_width), lambda h, b: (b, 0, 0))],
+        out_specs=pl.BlockSpec((block_rows, head_dim), lambda h, b: (b, h)),
+        interpret=interpret,
+    )(query, *keys, *values, mask)
 
 
 def on_device(
@@ -144,33 +192,18 @@
         jnp.any((neighbours[:, :, None] == ids[None, None, :]) & present[:, :, None], axis=1)
         for _, _, ids in pieces
     ]
-    score_scale = 1.0 / math.sqrt(head_dim)
     chunks = 2 if rows_mine % 2 == 0 else 1
     part_rows = rows_mine // chunks
+    keys = [p[0].reshape(-1, inner_dev) for p in pieces]
+    values = [p[1].reshape(-1, inner_dev) for p in pieces]
+    key_ok = jnp.repeat(jnp.concatenate(tile_masks, axis=1), TILE, axis=1).astype(f32)
     mixed_parts = []
     for c in range(chunks):
-        rows = (
-            np.arange(head_size)[:, None] * rows_mine + c * part_rows + np.arange(part_rows)[None, :]
-        ).reshape(-1)
-        row_tiles = rows // TILE
-        q_c = query_hat.reshape(head_size, chunks, part_rows, heads_dev, head_dim)[:, c]
-        q_c = q_c.reshape(head_size * part_rows, heads_dev, head_dim)
-        exps, total = [], 0.0
-        for (keys, _, _), mask in zip(pieces, tile_masks):
-            key_ok = jnp.repeat(mask[row_tiles], TILE, axis=1)
-            scores = (
-                jnp.einsum("the,she->hts", q_c, keys, preferred_element_type=f32) * score_scale
-            )
-            unnormed = jnp.where(key_ok[None], jnp.exp(scores), 0.0)
-            exps.append(unnormed)
-            total = total + jnp.sum(unnormed, axis=-1, keepdims=True)
-        attn_c = 0.0
-        for (_, values, _), unnormed in zip(pieces, exps):
-            weights = (unnormed / total).astype(bf16)
-            attn_c = attn_c + jnp.einsum(
-                "hts,she->the", weights, values, preferred_element_type=f32
-            )
-        attn_c = attn_c.astype(bf16).reshape(head_size * part_rows, inner_dev)
+        block_tiles = (np.arange(head_size) * rows_mine + c * part_rows) // TILE
+        q_c = query_hat.reshape(head_size, chunks, part_rows, inner_dev)[:, c]
+        q_c = q_c.reshape(head_size * part_rows, inner_dev)
+        mask_c = key_ok[block_tiles][:, None, :]
+        attn_c = tile_attention(q_c, keys, values, mask_c, part_rows, head_dim)
         mixed_parts.append(
             lax.psum_scatter(
                 jnp.dot(attn_c, w_out2, preferred_element_type=f32).astype(bf16),

time: 410 us -> 413 us (level); the launches traced: 403 us -> 411 us
  matrix products: 98.3 us -> 48.6 us
  Pallas kernels: 0 us -> 35.7 us
  local copies, waits for them, and re-layouts: 32.8 us -> 58.5 us
  waiting for transfers between devices: 218 us -> 209 us
  other arithmetic: 18.7 us -> 25.4 us
    dot_general x12 -> x0, matrix products: 52.6 us -> none  [the longest x6 28 us: on_device(): jnp.einsum('hts,she->the', weights, values, preferred_element_type=f32)]
    pallas_call x0 -> x2, Pallas kernels: none -> 35.7 us  [tile_attention(): pl.pallas_call(functools.partial(_attn_kernel, scale=1.0 / math.sqrt(head...]
    reshape x0 -> x5, local copies, waits for them, and re-layouts: none -> 9.9 us  [the longest x2 4.59 us: on_device(): keys = [p[0].reshape(-1, inner_dev) for p in pieces]]
    unnamed x55 -> x50, local copies, waits for them, and re-layouts: 23.2 us -> 30.8 us
    ppermute x1, waiting for transfers between devices: 7 us -> 0.01 us  [on_device(): key_prev = lax.ppermute(key_hat[tok_rows - halo_rows:], 'ctx', up)]
    reduce_scatter x2, waiting for transfers between devices: 69.1 us -> 63.8 us  [on_device(): lax.psum_scatter(jnp.dot(attn_c, w_out2, preferred_element_type=f32).asty...]
    convert_element_type x2 -> x4, local copies, waits for them, and re-layouts: 0.14 us -> 5.32 us  [on_device(): v_parts.append(proj_n[:, 2].astype(bf16))]
    broadcast_in_dim x3 -> x1, local copies, waits for them, and re-layouts: 4.8 us -> 0.65 us  [on_device(): mask_c = key_ok[block_tiles][:, None, :]]
  transfers between devices with their start and end apart: 8 -> 8, of which waited for: 5 -> 4; matrix products, arithmetic and copies ran while one was open for 20% -> 15% of each run, Pallas kernels for 0% -> 4%
where the time goes in v3:
time: 413 us; the launch traced here: 411 us
  waiting for transfers between devices  209 us (51%)
  local copies, waits for them, and re-layouts  58.5 us (14%)
  matrix products  48.6 us (12%)
  Pallas kernels  35.7 us (9%)
  other arithmetic  25.4 us (6%)
  between operations  13.7 us (3%)
  starting transfers between devices  11.7 us (3%)
  blocking collectives  8.74 us (2%)
    psum x2, waiting for transfers between devices, on_device(): summed = lax.psum(partial, 'head').astype(f32)  145 us
    reduce_scatter x2, waiting for transfers between devices, on_device(): lax.psum_scatter(jnp.dot(attn_c, w_out2, preferred_element_type=f32).asty...  63.8 us
    pallas_call x2, Pallas kernels, tile_attention(): pl.pallas_call(functools.partial(_attn_kernel, scale=1.0 / math.sqrt(head...  35.7 us
    unnamed x50, local copies, waits for them, and re-layouts  30.8 us
    dot_general x2, matrix products, on_device(): proj_n = jnp.dot(normed_n, w_qkv2_flat, preferred_element_type=f32)  12.2 us
    reduce_sum x5, other arithmetic, rms_rows(): mean_sq = jnp.mean(value * value, axis=-1, keepdims=True)  11.7 us
    dot_general x1, matrix products, on_device(): jnp.dot(normed, w_qkv1.reshape(feature_width, 3 * inner_dev), preferred_e...  10.3 us
    all_gather x1, blocking collectives, on_device(): lax.all_gather(own_total.astype(bf16), 'ctx', axis=0).astype(f32)  8.74 us
  transfers between devices with their start and end apart: 8, of which 4 were waited for; matrix products, arithmetic and copies ran while one was open for 15% of the time, Pallas kernels for 4%

profile of v3, /device:TPU:1, one launch (start us, length us, event | category | flops | bytes accessed | tf_op | source)
XLA Modules:
  0.0 411.0 jit_solution(17671426101481506187)
XLA Ops:
  6.6 3.2 fusion
  9.9 8.8 %copy.86 = bf16[2048,3,512]{0,2,1:T(8,128)(2,1)} copy(bf16[2048,3,512]{2,0,1:T(8,128)(2,1)} %param.17) | data formatting | bytes 12582912 | tf_op args[2]
  18.7 10.3 %fusion.10 = f32[1024,3,4,128]{3,0,2,1:T(8,128)S(1)} fusion(bf16[3,4,128,2048]{3,2,1,0:T(8,128)(2,1)} %bitcast.146, bf16[1024,2048]{1,0:T(8,128)(2,1)} %param.15, f32[2048]{0:T(1024)S(1)} %copy-done.20, f32[1024]{0:T(1024)S(1)} %add_rsqrt_fusion.6), kind=kOutput, calls=%fused_computation.17 | convolution fusion | flops 6450839552 | bytes 16789504 | tf_op jit(solution)/shard_map/dot_general | solution.py:109
  29.0 1.1 slice.181
  30.1 1.0 select_convert_fusion.4
  31.1 2.7 fusion.53
  33.7 2.7 fusion.54
  36.4 2.0 fusion.69
  38.4 8.7 %all-gather = bf16[16,128,128]{2,1,0:T(8,128)(2,1)S(1)} all-gather(bf16[4,128,128]{2,1,0:T(8,128)(2,1)S(1)} %get-tuple-element.34), channel_id=2, replica_groups=mesh['groups'=2,'ctx'=4,'head'=4] {'ctx'}, dimensions={0}, use_global_device_ids=true | all-gather | bytes 655360 | tf_op jit(solution)/shard_map/all_gather | solution.py:123
  48.1 0.4 fusion.55
  48.5 0.4 convolution_add_fusion.1
  48.8 1.4 copy-done.3
  50.6 0.9 fusion.15
  51.4 1.3 copy-done.2
  52.7 0.9 fusion.14
  53.6 1.1 multiply_reduce_fusion.2
  54.7 1.1 multiply_reduce_fusion.3
  56.2 2.6 convolution_convert_fusion.2
  59.5 2.7 convolution_convert_fusion.3
  62.2 83.6 %all-reduce.3.cloned.1.call-done = bf16[512,2048]{1,0:T(8,128)(2,1)} async-done(((bf16[512,2048]{1,0:T(8,128)(2,1)}), bf16[512,2048]{1,0:T(8,128)(2,1)}) %all-reduce.3.cloned.1.call-update) | async-done | bytes 2097168 | tf_op jit(solution)/shard_map/psum | solution.py:157
  145.8 3.2 fusion.3
  149.3 0.6 gather_fusion
  149.9 0.6 broadcast_in_dim.40.m_ref
  150.5 8.7 %copy.97 = bf16[2048,3,512]{0,2,1:T(8,128)(2,1)} copy(bf16[2048,3,512]{2,0,1:T(8,128)(2,1)} %param.21) | data formatting | bytes 12582912 | tf_op args[6]
  159.2 5.8 %fusion.22 = f32[512,3,4,128]{0,3,2,1:T(8,128)S(1)} fusion(bf16[3,4,128,2048]{3,2,1,0:T(8,128)(2,1)} %bitcast.144, bf16[512,2048]{1,0:T(8,128)(2,1)S(1)} %get-tuple-element.7, f32[2048]{0:T(1024)S(1)} %copy-done.21, f32[512]{0:T(512)S(1)} %add_rsqrt_fusion.8), kind=kOutput, calls=%fused_computation.39 | convolution fusion | flops 3225419776 | bytes 11544576 | tf_op jit(solution)/shard_map/dot_general | solution.py:163
  165.1 1.6 copy-done.5
  166.7 1.0 copy.130
  167.7 1.8 fusion.47
  170.0 1.3 copy.124
  171.4 2.1 slice_bitcast_fusion.21
  173.5 61.2 %all-reduce.5.cloned.1.call-done = bf16[512,2048]{1,0:T(8,128)(2,1)} async-done(((bf16[512,2048]{1,0:T(8,128)(2,1)}), bf16[512,2048]{1,0:T(8,128)(2,1)}) %all-reduce.5.cloned.1.call-update) | async-done | bytes 2097168 | tf_op jit(solution)/shard_map/psum | solution.py:157
  234.6 3.2 fusion.6
  237.8 6.5 %fusion.19 = f32[512,3,4,128]{0,3,2,1:T(8,128)S(1)} fusion(bf16[3,4,128,2048]{3,2,1,0:T(8,128)(2,1)} %bitcast.145, bf16[512,2048]{1,0:T(8,128)(2,1)S(1)} %get-tuple-element.19, f32[512]{0:T(512)S(1)} %add_rsqrt_fusion.7, f32[2048]{0:T(1024)S(1)} %copy-done.21), kind=kOutput, calls=%fused_computation.37 | convolution fusion | flops 3225419776 | bytes 11544576 | tf_op jit(solution)/shard_map/dot_general | solution.py:163
  244.8 2.6 copy-done.6
  247.4 0.9 fusion.46
  248.3 1.1 pad_maximum_fusion.1
  249.4 2.6 collective-permute-start.1
  252.0 3.0 collective-permute-start
  255.0 1.1 pad_maximum_fusion.3
  256.2 2.3 collective-permute-start.3
  258.5 3.5 collective-permute-start.2
  262.1 0.9 slice.182
  263.0 2.1 copy.131
  265.1 1.1 mul.233
  266.2 2.6 copy.127
  268.8 1.3 copy.126
  270.1 0.7 reshape.213
  270.9 2.5 fusion.68
  273.4 3.6 copy.133
  276.9 2.3 pad_maximum_fusion.4.vo_ref
  279.2 1.8 multiply_convert_fusion.1
  281.0 1.1 pad_maximum_fusion.2.ko_ref
  282.0 2.3 copy.128.kn_ref
  284.3 2.3 copy.123.kp_ref
  286.6 2.3 copy.132.vn_ref
  288.9 2.3 copy.129.vp_ref
  291.2 17.8 %shard_map.145 = bf16[512,512]{1,0:T(8,128)(2,1)} custom-call(bf16[512,512]{1,0:T(8,128)(2,1)} %bitcast.151, bf16[1024,512]{1,0:T(8,128)(2,1)} %copy.123.kp_ref, bf16[1024,512]{1,0:T(8,128)(2,1)} %pad_maximum_fusion.2.ko_ref, bf16[1024,512]{1,0:T(8,128)(2,1)} %copy.128.kn_ref, bf16[1024,512]{1,0:T(8,128)(2,1)} %copy.129.vp_ref, ...), custom_call_target="tpu_custom_call" | custom-call | tf_op jit(solution)/shard_map/pallas_call | solution.py:80
  309.0 4.4 %convolution_convert_fusion.1 = bf16[512,2048]{1,0:T(8,128)(2,1)} fusion(bf16[512,512]{1,0:T(8,128)(2,1)} %shard_map.145, bf16[512,2048]{1,0:T(8,128)(2,1)} %param.24), kind=kOutput, calls=%fused_computation.29 | convolution fusion | flops 1074790400 | bytes 4718592 | tf_op jit(solution)/shard_map/dot_general | solution.py:209
  313.5 2.3 copy.134
  315.8 18.0 %shard_map.146 = bf16[512,512]{1,0:T(8,128)(2,1)} custom-call(bf16[512,512]{1,0:T(8,128)(2,1)} %bitcast.152, bf16[1024,512]{1,0:T(8,128)(2,1)} %copy.123.kp_ref, bf16[1024,512]{1,0:T(8,128)(2,1)} %pad_maximum_fusion.2.ko_ref, bf16[1024,512]{1,0:T(8,128)(2,1)} %copy.128.kn_ref, bf16[1024,512]{1,0:T(8,128)(2,1)} %copy.129.vp_ref, ...), custom_call_target="tpu_custom_call" | custom-call | tf_op jit(solution)/shard_map/pallas_call | solution.py:80
  333.7 3.6 convolution_convert_fusion
  337.4 18.4 %reduce-scatter.3.cloned.1.call-done = bf16[128,2048]{1,0:T(8,128)(2,1)} async-done(((bf16[512,2048]{1,0:T(8,128)(2,1)}), bf16[128,2048]{1,0:T(8,128)(2,1)}) %reduce-scatter.3.cloned.1.call-update) | async-done | bytes 524304 | tf_op jit(solution)/shard_map/reduce_scatter | solution.py:208
  355.8 45.4 %reduce-scatter.5.cloned.1.call-done = bf16[128,2048]{1,0:T(8,128)(2,1)} async-done(((bf16[512,2048]{1,0:T(8,128)(2,1)}), bf16[128,2048]{1,0:T(8,128)(2,1)}) %reduce-scatter.5.cloned.1.call-update) | async-done | bytes 524304 | tf_op jit(solution)/shard_map/reduce_scatter | solution.py:208
  401.2 3.3 add_convert_fusion.2
  (86 shorter events, 3.7 us)
Async XLA Ops:
  6.5 49.6 %copy-start = (bf16[512,2048]{1,0:T(8,128)(2,1)S(1)}, bf16[512,2048]{1,0:T(8,128)(2,1)}, u32[]{:S(2)}) copy-start(bf16[512,2048]{1,0:T(8,128)(2,1)} %param.19) | copy-start | bytes 6291460
  6.5 139.2 %all-reduce.3.cloned.1.call-start = ((), (), s32[]{:S(2)}) async-start(), calls=%async_computation.2 | async-start | bytes 4194304 | tf_op jit(solution)/shard_map/psum | solution.py:157
  9.8 8.8 %copy-start.20 = (f32[2048]{0:T(1024)S(1)}, f32[2048]{0:T(1024)}, u32[]{:S(2)}) copy-start(f32[2048]{0:T(1024)} %param.16) | copy-start | bytes 24580
  31.1 2.7 copy-start.12
  48.1 2.2 copy-start.3
  48.1 2.5 copy-start.7
  50.6 2.2 copy-start.2
  54.7 1.1 copy-start.16
  56.1 2.7 copy-start.15
  56.1 3.3 copy-start.17
  58.8 175.9 %all-reduce.5.cloned.1.call-start = ((), (), s32[]{:S(2)}) async-start(), calls=%async_computation.3 | async-start | bytes 4194304 | tf_op jit(solution)/shard_map/psum | solution.py:157
  149.0 10.2 %copy-start.8 = (bf16[512,2048]{1,0:T(8,128)(2,1)}, bf16[512,2048]{1,0:T(8,128)(2,1)S(1)}, u32[]{:S(2)}) copy-start(bf16[512,2048]{1,0:T(8,128)(2,1)S(1)} %get-tuple-element.7) | copy-start | bytes 6291460
  149.0 206.8 %reduce-scatter.3.cloned.1.call-start = ((), (), s32[]{:S(2)}) async-start(), calls=%async_computation.4 | async-start | bytes 2621440 | tf_op jit(solution)/shard_map/reduce_scatter | solution.py:208
  150.5 8.7 %copy-start.21 = (f32[2048]{0:T(1024)S(1)}, f32[2048]{0:T(1024)}, u32[]{:S(2)}) copy-start(f32[2048]{0:T(1024)} %param.20) | copy-start | bytes 24580
  165.0 1.7 copy-start.5
  166.7 3.3 slice-start.1
  237.8 6.5 %copy-start.9 = (bf16[512,2048]{1,0:T(8,128)(2,1)}, bf16[512,2048]{1,0:T(8,128)(2,1)S(1)}, u32[]{:S(2)}) copy-start(bf16[512,2048]{1,0:T(8,128)(2,1)S(1)} %get-tuple-element.19) | copy-start | bytes 6291460
  244.3 18.7 %copy-start.4 = (f32[512,3,4,128]{0,3,2,1:T(8,128)}, f32[512,3,4,128]{0,3,2,1:T(8,128)S(1)}, u32[]{:S(2)}) copy-start(f32[512,3,4,128]{0,3,2,1:T(8,128)S(1)} %fusion.19) | copy-start | bytes 9437188
  244.4 3.0 copy-start.6
  244.4 3.0 copy-start.18
  247.4 7.6 %copy-start.14 = (bf16[512,4,128]{0,2,1:T(8,128)(2,1)S(1)}, bf16[512,4,128]{0,2,1:T(8,128)(2,1)}, u32[]{:S(2)}) copy-start(bf16[512,4,128]{0,2,1:T(8,128)(2,1)} %slice_bitcast_fusion.21) | copy-start | bytes 1572868
  249.4 32.6 %collective-permute-start.1 = (bf16[1024,4,128]{0,2,1:T(8,128)(2,1)}, bf16[1024,4,128]{0,2,1:T(8,128)(2,1)}, u32[]{:S(2)}, u32[]{:S(2)}) collective-permute-start(bf16[1024,4,128]{0,2,1:T(8,128)(2,1)} %pad_maximum_fusion.1), channel_id=1, source_target_pairs={{4,0},{8,4},{12,8},{5,1},{9,5},{13,9},{6,2},{10,6},{14,10},{7,3},{... | collective-permute-start | bytes 3145736 | tf_op jit(solution)/shard_map/ppermute | solution.py:181
  252.0 32.3 %collective-permute-start = (bf16[1024,4,128]{0,2,1:T(8,128)(2,1)}, bf16[1024,4,128]{0,2,1:T(8,128)(2,1)}, u32[]{:S(2)}, u32[]{:S(2)}) collective-permute-start(bf16[1024,4,128]{0,2,1:T(8,128)(2,1)} %pad_maximum_fusion.1), channel_id=1, source_target_pairs={{0,4},{4,8},{8,12},{1,5},{5,9},{9,13},{2,6},{6,10},{10,14},{3,7},{... | collective-permute-start | bytes 3145736 | tf_op jit(solution)/shard_map/ppermute | solution.py:179
  256.2 30.5 %collective-permute-start.3 = (bf16[1024,4,128]{0,2,1:T(8,128)(2,1)}, bf16[1024,4,128]{0,2,1:T(8,128)(2,1)}, u32[]{:S(2)}, u32[]{:S(2)}) collective-permute-start(bf16[1024,4,128]{0,2,1:T(8,128)(2,1)} %pad_maximum_fusion.3), channel_id=1, source_target_pairs={{4,0},{8,4},{12,8},{5,1},{9,5},{13,9},{6,2},{10,6},{14,10},{7,3},{... | collective-permute-start | bytes 3145736 | tf_op jit(solution)/shard_map/ppermute | solution.py:182
  258.5 30.5 %collective-permute-start.2 = (bf16[1024,4,128]{0,2,1:T(8,128)(2,1)}, bf16[1024,4,128]{0,2,1:T(8,128)(2,1)}, u32[]{:S(2)}, u32[]{:S(2)}) collective-permute-start(bf16[1024,4,128]{0,2,1:T(8,128)(2,1)} %pad_maximum_fusion.3), channel_id=1, source_target_pairs={{0,4},{4,8},{8,12},{1,5},{5,9},{9,13},{2,6},{6,10},{10,14},{3,7},{... | collective-permute-start | bytes 3145736 | tf_op jit(solution)/shard_map/ppermute | solution.py:180
  263.0 5.8 %slice-start = ((f32[512,3,4,128]{0,3,2,1:T(8,128)}), f32[512,1,4,128]{0,3,2,1:T(8,128)S(1)}, s32[]{:S(2)}) async-start(f32[512,3,4,128]{0,3,2,1:T(8,128)} %copy-done.4), calls=%async_computation.6 | async-start | bytes 2097152 | tf_op jit(solution)/shard_map/slice | solution.py:166
  270.9 8.3 %copy-start.10 = (f32[512,512]{1,0:T(8,128)S(1)}, f32[512,512]{1,0:T(8,128)}, u32[]{:S(2)}) copy-start(f32[512,512]{1,0:T(8,128)} %copy.124) | copy-start | bytes 3145732
  273.4 5.8 %copy-start.11 = (f32[512,512]{1,0:T(8,128)S(1)}, f32[512,512]{1,0:T(8,128)}, u32[]{:S(2)}) copy-start(f32[512,512]{1,0:T(8,128)} %copy.127) | copy-start | bytes 3145732
  309.0 4.5 %copy-start.13 = (bf16[4,1,128,512]{2,1,0,3:T(2,128)(2,1)S(1)}, bf16[4,1,128,512]{2,1,0,3:T(2,128)(2,1)}, u32[]{:S(2)}) copy-start(bf16[4,1,128,512]{2,1,0,3:T(2,128)(2,1)} %get-tuple-element.27) | copy-start | bytes 1572868
  313.4 87.7 %reduce-scatter.5.cloned.1.call-start = ((), (), s32[]{:S(2)}) async-start(), calls=%async_computation.5 | async-start | bytes 2621440 | tf_op jit(solution)/shard_map/reduce_scatter | solution.py:208
  315.8 18.0 %copy-start.19 = (bf16[512,2048]{1,0:T(8,128)(2,1)S(1)}, bf16[512,2048]{1,0:T(8,128)(2,1)}, u32[]{:S(2)}) copy-start(bf16[512,2048]{1,0:T(8,128)(2,1)} %param.24) | copy-start | bytes 6291460
  337.4 67.1 %copy-start.1 = (bf16[512,2048]{1,0:T(8,128)(2,1)S(1)}, bf16[512,2048]{1,0:T(8,128)(2,1)}, u32[]{:S(2)}) copy-start(bf16[512,2048]{1,0:T(8,128)(2,1)} %param.19) | copy-start | bytes 6291460
Sparse Core Ops, SparseCore 0:
  58.9 86.8 all-reduce.2
  149.1 85.4 all-reduce.4
  313.6 42.1 reduce-scatter.2
  358.0 43.1 reduce-scatter.4

commit v4 on v3

--- a/solution.py
+++ b/solution.py
@@ -71,24 +71,22 @@
     o_ref[...] = acc.astype(o_ref.dtype)
 
 
-def tile_attention(query, keys, values, mask, block_rows, head_dim, interpret=False):
-    rows, inner = query.shape
-    heads = inner // head_dim
+def tile_attention(query, keys, values, mask, block_rows, interpret=False):
+    heads, rows, head_dim = query.shape
     blocks = rows // block_rows
     key_width = mask.shape[-1]
-    kv_specs = [pl.BlockSpec((k.shape[0], head_dim), lambda h, b: (0, h)) for k in keys]
+    kv_specs = [pl.BlockSpec((None, k.shape[1], head_dim), lambda h, b: (h, 0, 0)) for k in keys]
     return pl.pallas_call(
         functools.partial(_attn_kernel, scale=1.0 / math.sqrt(head_dim)),
-        out_shape=jax.ShapeDtypeStruct((rows, inner), jnp.bfloat16),
+        out_shape=jax.ShapeDtypeStruct((heads, rows, head_dim), jnp.bfloat16),
         grid=(heads, blocks),
-        in_specs=[pl.BlockSpec((block_rows, head_dim), lambda h, b: (b, h))]
+        in_specs=[pl.BlockSpec((None, block_rows, head_dim), lambda h, b: (h, b, 0))]
         + kv_specs
         + kv_specs
         + [pl.BlockSpec((1, 1, key_width), lambda h, b: (b, 0, 0))],
-        out_specs=pl.BlockSpec((block_rows, head_dim), lambda h, b: (b, h)),
+        out_specs=pl.BlockSpec((None, block_rows, head_dim), lambda h, b: (h, b, 0)),
         interpret=interpret,
     )(query, *keys, *values, mask)
-
 
 def on_device(
     tokens, norm_one, w_qkv1, lin_gain, w_out1, norm_two, w_qkv2, q_gain, k_gain, w_out2, neighbours
@@ -176,10 +174,13 @@
     head_size = lax.axis_size("head")
     up = [(i, i + 1) for i in range(ctx_size - 1)]
     down = [(i + 1, i) for i in range(ctx_size - 1)]
-    key_prev = lax.ppermute(key_hat[tok_rows - halo_rows :], "ctx", up)
-    value_prev = lax.ppermute(value_two[tok_rows - halo_rows :], "ctx", up)
-    key_next = lax.ppermute(key_hat[:halo_rows], "ctx", down)
-    value_next = lax.ppermute(value_two[:halo_rows], "ctx", down)
+    key_hat = jnp.transpose(key_hat, (1, 0, 2))
+    value_two = jnp.transpose(value_two, (1, 0, 2))
+    query_hat = jnp.transpose(query_hat, (1, 0, 2))
+    key_prev = lax.ppermute(key_hat[:, tok_rows - halo_rows :], "ctx", up)
+    value_prev = lax.ppermute(value_two[:, tok_rows - halo_rows :], "ctx", up)
+    key_next = lax.ppermute(key_hat[:, :halo_rows], "ctx", down)
+    value_next = lax.ppermute(value_two[:, :halo_rows], "ctx", down)
     own_first = ctx_index * tile_count
     arange_halo = jnp.arange(plane_tiles, dtype=jnp.int32)
     pieces = (
@@ -194,19 +195,21 @@
     ]
     chunks = 2 if rows_mine % 2 == 0 else 1
     part_rows = rows_mine // chunks
-    keys = [p[0].reshape(-1, inner_dev) for p in pieces]
-    values = [p[1].reshape(-1, inner_dev) for p in pieces]
+    keys = [p[0] for p in pieces]
+    values = [p[1] for p in pieces]
+    w_out2_heads = w_out2.reshape(heads_dev, head_dim, w_out2.shape[1])
     key_ok = jnp.repeat(jnp.concatenate(tile_masks, axis=1), TILE, axis=1).astype(f32)
     mixed_parts = []
     for c in range(chunks):
         block_tiles = (np.arange(head_size) * rows_mine + c * part_rows) // TILE
-        q_c = query_hat.reshape(head_size, chunks, part_rows, inner_dev)[:, c]
-        q_c = q_c.reshape(head_size * part_rows, inner_dev)
+        q_c = query_hat.reshape(heads_dev, head_size, chunks, part_rows, head_dim)[:, :, c]
+        q_c = q_c.reshape(heads_dev, head_size * part_rows, head_dim)
         mask_c = key_ok[block_tiles][:, None, :]
-        attn_c = tile_attention(q_c, keys, values, mask_c, part_rows, head_dim)
+        attn_c = tile_attention(q_c, keys, values, mask_c, part_rows)
+        out_c = jnp.einsum("hte,hef->tf", attn_c, w_out2_heads, preferred_element_type=f32)
         mixed_parts.append(
             lax.psum_scatter(
-                jnp.dot(attn_c, w_out2, preferred_element_type=f32).astype(bf16),
+                out_c.astype(bf16),
                 "head",
                 scatter_dimension=0,
                 tiled=True,

time: 413 us -> 400 us (0.969)
  local copies, waits for them, and re-layouts: 58.5 us -> 27 us
  waiting for transfers between devices: 209 us -> 230 us
    ppermute x4, waiting for transfers between devices: 0.01 us -> 14.6 us  [the longest x1 6.84 us: on_device(): value_prev = lax.ppermute(value_two[:, tok_rows - halo_rows:], 'ctx', up)]
    reshape x5 -> x0, local copies, waits for them, and re-layouts: 9.9 us -> none  [the longest x2 4.59 us: on_device(): keys = [p[0].reshape(-1, inner_dev) for p in pieces]]
    unnamed x50 -> x42, local copies, waits for them, and re-layouts: 30.8 us -> 23.6 us
    concatenate x4 -> x0, other arithmetic: 5.57 us -> none  [the longest x2 3.39 us: on_device(): value_two = jnp.concatenate(v_parts, axis=0)]
    psum x2, waiting for transfers between devices: 145 us -> 150 us  [on_device(): summed = lax.psum(partial, 'head').astype(f32)]
    convert_element_type x4 -> x2, local copies, waits for them, and re-layouts: 5.32 us -> 0.93 us  [on_device(): v_parts.append(proj_n[:, 2].astype(bf16))]
  transfers between devices with their start and end apart: 8 -> 8, of which waited for: 4 -> 7; matrix products, arithmetic and copies ran while one was open for 15% -> 8% of each run, Pallas kernels for 4% -> 4%
where the time goes in v4:
time: 400 us; the launch traced here: 398 us
  waiting for transfers between devices  230 us (58%)
  matrix products  48.2 us (12%)
  Pallas kernels  35.3 us (9%)
  local copies, waits for them, and re-layouts  27 us (7%)
  other arithmetic  23.1 us (6%)
  between operations  13.6 us (3%)
  starting transfers between devices  11.6 us (3%)
  blocking collectives  9.17 us (2%)
    psum x2, waiting for transfers between devices, on_device(): summed = lax.psum(partial, 'head').astype(f32)  150 us
    reduce_scatter x2, waiting for transfers between devices, on_device(): lax.psum_scatter(out_c.astype(bf16), 'head', scatter_dimension=0, tiled=T...  65.5 us
    pallas_call x2, Pallas kernels, tile_attention(): pl.pallas_call(functools.partial(_attn_kernel, scale=1.0 / math.sqrt(head...  35.3 us
    unnamed x42, local copies, waits for them, and re-layouts  23.6 us
    dot_general x2, matrix products, on_device(): proj_n = jnp.dot(normed_n, w_qkv2_flat, preferred_element_type=f32)  12.9 us
    reduce_sum x5, other arithmetic, rms_rows(): mean_sq = jnp.mean(value * value, axis=-1, keepdims=True)  12.2 us
    all_gather x1, blocking collectives, on_device(): lax.all_gather(own_total.astype(bf16), 'ctx', axis=0).astype(f32)  9.17 us
    dot_general x1, matrix products, on_device(): jnp.dot(normed, w_qkv1.reshape(feature_width, 3 * inner_dev), preferred_e...  9.07 us
  transfers between devices with their start and end apart: 8, of which 7 were waited for; matrix products, arithmetic and copies ran while one was open for 8% of the time, Pallas kernels for 4%

profile of v4, /device:TPU:1, one launch (start us, length us, event | category | flops | bytes accessed | tf_op | source)
XLA Modules:
  0.0 398.3 jit_solution(12040527016808955264)
XLA Ops:
  6.5 9.0 %copy.56 = bf16[2048,3,512]{0,2,1:T(8,128)(2,1)} copy(bf16[2048,3,512]{2,0,1:T(8,128)(2,1)} %param.17) | data formatting | bytes 12582912 | tf_op args[2]
  15.5 3.2 fusion
  18.8 0.2 copy-done.3
  19.0 9.1 %fusion.10 = f32[1024,3,4,128]{3,0,2,1:T(8,128)S(1)} fusion(bf16[3,4,128,2048]{3,2,1,0:T(8,128)(2,1)} %bitcast.142, bf16[1024,2048]{1,0:T(8,128)(2,1)S(1)} %copy-done.3, f32[2048]{0:T(1024)S(1)} %copy-done.17, f32[1024]{0:T(1024)S(1)} %add_rsqrt_fusion.6), kind=kOutput, calls=%fused_computation.17 | convolution fusion | flops 6450839552 | bytes 16789504 | tf_op jit(solution)/shard_map/dot_general | solution.py:107
  28.0 1.0 select_convert_fusion.4
  29.0 0.1 slice.193
  29.2 0.1 iota_compare_fusion
  29.3 2.6 fusion.49
  31.9 2.7 fusion.50
  34.6 1.3 fusion.65
  35.9 9.2 %all-gather = bf16[16,128,128]{2,1,0:T(8,128)(2,1)} all-gather(bf16[4,128,128]{2,1,0:T(8,128)(2,1)S(1)} %get-tuple-element.32), channel_id=2, replica_groups=mesh['groups'=2,'ctx'=4,'head'=4] {'ctx'}, dimensions={0}, use_global_device_ids=true | all-gather | bytes 655360 | tf_op jit(solution)/shard_map/all_gather | solution.py:121
  45.1 1.3 fusion.43
  46.4 0.3 fusion.52
  46.8 0.3 convolution_add_fusion
  47.1 0.4 fusion.51
  47.5 0.4 convolution_add_fusion.1
  47.9 1.4 copy-done.2
  49.3 0.3 copy-done.6
  49.6 0.9 fusion.15
  50.5 1.3 copy-done.1
  51.8 0.9 fusion.14
  52.7 1.1 multiply_reduce_fusion.4
  53.8 1.1 multiply_reduce_fusion.5
  54.9 0.3 multiply_convert_fusion.4
  55.2 1.3 copy-done.16
  56.5 2.7 convolution_convert_fusion
  59.2 8.9 %copy.67 = bf16[2048,3,512]{0,2,1:T(8,128)(2,1)} copy(bf16[2048,3,512]{2,0,1:T(8,128)(2,1)} %param.21) | data formatting | bytes 12582912 | tf_op args[6]
  68.1 4.3 %convolution_convert_fusion.1 = bf16[512,2048]{1,0:T(8,128)(2,1)} fusion(bf16[512,512]{0,1:T(8,128)(2,1)S(1)} %bitcast.149, bf16[512,2048]{1,0:T(8,128)(2,1)} %param.19), kind=kOutput, calls=%fused_computation.31 | convolution fusion | flops 1074790400 | bytes 4718592 | tf_op jit(solution)/shard_map/dot_general | solution.py:151
  72.4 73.8 %all-reduce.3.cloned.1.call-done = bf16[512,2048]{1,0:T(8,128)(2,1)} async-done(((bf16[512,2048]{1,0:T(8,128)(2,1)}), bf16[512,2048]{1,0:T(8,128)(2,1)}) %all-reduce.3.cloned.1.call-update) | async-done | bytes 2097168 | tf_op jit(solution)/shard_map/psum | solution.py:155
  146.2 4.5 %fusion.3 = (f32[512]{0:T(512)S(1)}, bf16[512,2048]{1,0:T(8,128)(2,1)}) fusion(bf16[512,2048]{1,0:T(8,128)(2,1)} %all-reduce.3.cloned.1.call-done, bf16[1024,2048]{1,0:T(8,128)(2,1)} %param.15), kind=kLoop, calls=%fused_computation.10 | loop fusion | flops 7339520 | bytes 6293504 | tf_op jit(solution)/shard_map/reduce_sum | solution.py:33
  150.7 0.3 reduce-scatter.5.cloned.1.call-start
  151.0 6.4 %fusion.22 = f32[512,3,4,128]{3,0,2,1:T(8,128)S(1)} fusion(bf16[3,4,128,2048]{3,2,1,0:T(8,128)(2,1)} %bitcast.140, bf16[512,2048]{1,0:T(8,128)(2,1)} %get-tuple-element.7, f32[2048]{0:T(1024)S(1)} %copy-done.18, f32[512]{0:T(512)S(1)} %add_rsqrt_fusion.8), kind=kOutput, calls=%fused_computation.39 | convolution fusion | flops 3225419776 | bytes 11544576 | tf_op jit(solution)/shard_map/dot_general | solution.py:161
  157.5 0.6 multiply_reduce_fusion.1
  158.1 1.0 copy-done.8
  159.1 0.9 fusion.47
  160.0 76.3 %all-reduce.5.cloned.1.call-done = bf16[512,2048]{1,0:T(8,128)(2,1)} async-done(((bf16[512,2048]{1,0:T(8,128)(2,1)}), bf16[512,2048]{1,0:T(8,128)(2,1)}) %all-reduce.5.cloned.1.call-update) | async-done | bytes 2097168 | tf_op jit(solution)/shard_map/psum | solution.py:155
  236.3 3.2 fusion.6
  239.6 6.5 %fusion.19 = f32[512,3,4,128]{3,0,2,1:T(8,128)S(1)} fusion(bf16[3,4,128,2048]{3,2,1,0:T(8,128)(2,1)} %bitcast.141, bf16[512,2048]{1,0:T(8,128)(2,1)S(1)} %get-tuple-element.19, f32[512]{0:T(512)S(1)} %add_rsqrt_fusion.7, f32[2048]{0:T(1024)S(1)} %copy-done.18), kind=kOutput, calls=%fused_computation.37 | convolution fusion | flops 3225419776 | bytes 11544576 | tf_op jit(solution)/shard_map/dot_general | solution.py:161
  246.2 0.6 multiply_reduce_fusion
  246.8 2.1 multiply_convert_fusion
  248.9 0.1 maximum_bitcast_fusion.ko_ref
  249.0 3.8 collective-permute-start
  252.8 1.9 collective-permute-start.1
  254.8 0.1 fusion.48
  254.8 1.0 maximum_bitcast_fusion.1.vo_ref
  255.9 3.6 collective-permute-start.2
  259.5 1.9 collective-permute-start.3
  261.5 0.4 and_reduce_fusion.2
  261.8 0.1 add_convert_fusion.3
  261.9 0.1 broadcast_bitcast_fusion
  262.1 0.6 gather_fusion
  262.6 0.7 broadcast_in_dim.40.m_ref
  263.3 1.3 pad_maximum_fusion
  264.6 1.1 fusion.64
  265.7 3.4 collective-permute-done.1.kn_ref
  269.1 6.8 %collective-permute-done.2.vp_ref = bf16[4,1024,128]{2,1,0:T(8,128)(2,1)} collective-permute-done((bf16[4,1024,128]{2,1,0:T(8,128)(2,1)}, bf16[4,1024,128]{2,1,0:T(8,128)(2,1)}, u32[]{:S(2)}, u32[]{:S(2)}) %collective-permute-start.2) | collective-permute-done | bytes 1048608 | tf_op jit(solution)/shard_map/ppermute | solution.py:181
  275.9 4.4 %collective-permute-done.3.vn_ref = bf16[4,1024,128]{2,1,0:T(8,128)(2,1)} collective-permute-done((bf16[4,1024,128]{2,1,0:T(8,128)(2,1)}, bf16[4,1024,128]{2,1,0:T(8,128)(2,1)}, u32[]{:S(2)}, u32[]{:S(2)}) %collective-permute-start.3) | collective-permute-done | bytes 1048608 | tf_op jit(solution)/shard_map/ppermute | solution.py:183
  280.3 17.6 %shard_map.146 = bf16[4,512,128]{2,1,0:T(8,128)(2,1)} custom-call(bf16[4,512,128]{2,1,0:T(8,128)(2,1)} %bitcast.147, bf16[4,1024,128]{2,1,0:T(8,128)(2,1)} %collective-permute-done.kp_ref, bf16[4,1024,128]{2,1,0:T(8,128)(2,1)} %copy-done.4, bf16[4,1024,128]{2,1,0:T(8,128)(2,1)} %collective-permute-done.1.kn_ref, ...), custom_call_target="tpu_custom_call" | custom-call | tf_op jit(solution)/shard_map/pallas_call | solution.py:79
  297.9 3.7 bitcast_convert_fusion
  301.6 17.7 %shard_map.145 = bf16[4,512,128]{2,1,0:T(8,128)(2,1)} custom-call(bf16[4,512,128]{2,1,0:T(8,128)(2,1)} %bitcast.146, bf16[4,1024,128]{2,1,0:T(8,128)(2,1)} %collective-permute-done.kp_ref, bf16[4,1024,128]{2,1,0:T(8,128)(2,1)} %copy-done.4, bf16[4,1024,128]{2,1,0:T(8,128)(2,1)} %collective-permute-done.1.kn_ref, ...), custom_call_target="tpu_custom_call" | custom-call | tf_op jit(solution)/shard_map/pallas_call | solution.py:79
  319.3 3.6 bitcast_convert_fusion.1
  322.9 20.0 %reduce-scatter.5.cloned.1.call-done = bf16[128,2048]{1,0:T(8,128)(2,1)} async-done(((bf16[512,2048]{1,0:T(8,128)(2,1)}), bf16[128,2048]{1,0:T(8,128)(2,1)}) %reduce-scatter.5.cloned.1.call-update) | async-done | bytes 524304 | tf_op jit(solution)/shard_map/reduce_scatter | solution.py:211
  342.9 45.5 %reduce-scatter.3.cloned.1.call-done = bf16[128,2048]{1,0:T(8,128)(2,1)} async-done(((bf16[512,2048]{1,0:T(8,128)(2,1)}), bf16[128,2048]{1,0:T(8,128)(2,1)}) %reduce-scatter.3.cloned.1.call-update) | async-done | bytes 524304 | tf_op jit(solution)/shard_map/reduce_scatter | solution.py:211
  388.4 3.3 add_convert_fusion.2
  (55 shorter events, 0.4 us)
Async XLA Ops:
  6.5 291.4 %copy-start = (bf16[512,2048]{1,0:T(8,128)(2,1)S(1)}, bf16[512,2048]{1,0:T(8,128)(2,1)}, u32[]{:S(2)}) copy-start(bf16[512,2048]{1,0:T(8,128)(2,1)} %param.24) | copy-start | bytes 6291460
  6.5 139.7 %all-reduce.3.cloned.1.call-start = ((), (), s32[]{:S(2)}) async-start(), calls=%async_computation.2 | async-start | bytes 4194304 | tf_op jit(solution)/shard_map/psum | solution.py:155
  15.5 3.4 copy-start.3
  15.5 3.4 copy-start.17
  29.2 5.4 %copy-start.5 = (bf16[1024,1,4,128]{3,0,2,1:T(8,128)(2,1)}, bf16[1024,1,4,128]{3,0,2,1:T(8,128)(2,1)S(1)}, u32[]{:S(2)}) copy-start(bf16[1024,1,4,128]{3,0,2,1:T(8,128)(2,1)S(1)} %slice.193) | copy-start | bytes 3145732
  45.1 2.0 copy-start.11
  47.1 2.2 copy-start.2
  47.1 2.5 copy-start.6
  49.6 2.2 copy-start.1
  53.8 1.1 copy-start.13
  54.9 1.6 copy-start.16
  59.2 8.9 %copy-start.12 = (s32[4,8]{1,0:T(4,128)S(1)}, s32[4,8]{1,0:T(4,128)}, u32[]{:S(2)}) copy-start(s32[4,8]{1,0:T(4,128)} %param.25) | copy-start | bytes 388
  59.2 177.2 %all-reduce.5.cloned.1.call-start = ((), (), s32[]{:S(2)}) async-start(), calls=%async_computation.3 | async-start | bytes 4194304 | tf_op jit(solution)/shard_map/psum | solution.py:155
  72.4 78.6 %copy-start.18 = (f32[2048]{0:T(1024)S(1)}, f32[2048]{0:T(1024)}, u32[]{:S(2)}) copy-start(f32[2048]{0:T(1024)} %param.20) | copy-start | bytes 24580
  150.7 192.2 %reduce-scatter.5.cloned.1.call-start = ((), (), s32[]{:S(2)}) async-start(), calls=%async_computation.5 | async-start | bytes 2621440 | tf_op jit(solution)/shard_map/reduce_scatter | solution.py:211
  157.4 1.7 copy-start.8
  239.6 6.6 %copy-start.7 = (bf16[512,2048]{1,0:T(8,128)(2,1)}, bf16[512,2048]{1,0:T(8,128)(2,1)S(1)}, u32[]{:S(2)}) copy-start(bf16[512,2048]{1,0:T(8,128)(2,1)S(1)} %get-tuple-element.19) | copy-start | bytes 6291460
  239.6 7.2 %copy-start.9 = (f32[512,3,4,128]{3,0,2,1:T(8,128)S(1)}, f32[512,3,4,128]{3,0,2,1:T(8,128)}, u32[]{:S(2)}) copy-start(f32[512,3,4,128]{3,0,2,1:T(8,128)} %copy-done.8) | copy-start | bytes 9437188
  239.6 7.2 %copy-start.14 = (f32[128]{0:T(128)S(1)}, f32[128]{0:T(128)}, u32[]{:S(2)}) copy-start(f32[128]{0:T(128)} %param.23) | copy-start | bytes 1540
  239.6 7.2 %copy-start.15 = (f32[128]{0:T(128)S(1)}, f32[128]{0:T(128)}, u32[]{:S(2)}) copy-start(f32[128]{0:T(128)} %param.22) | copy-start | bytes 1540
  248.9 5.9 %copy-start.10 = (bf16[512,4,128]{2,0,1:T(8,128)(2,1)S(1)}, bf16[512,4,128]{2,0,1:T(8,128)(2,1)}, u32[]{:S(2)}) copy-start(bf16[512,4,128]{2,0,1:T(8,128)(2,1)} %fusion.47) | copy-start | bytes 1572868
  249.0 16.6 %copy-start.4 = (bf16[4,1024,128]{2,1,0:T(8,128)(2,1)}, bf16[4,1024,128]{2,1,0:T(8,128)(2,1)S(1)}, u32[]{:S(2)}) copy-start(bf16[4,1024,128]{2,1,0:T(8,128)(2,1)S(1)} %maximum_bitcast_fusion.ko_ref) | copy-start | bytes 3145732
  249.0 16.6 %collective-permute-start = (bf16[4,1024,128]{2,1,0:T(8,128)(2,1)S(1)}, bf16[4,1024,128]{2,1,0:T(8,128)(2,1)}, u32[]{:S(2)}, u32[]{:S(2)}) collective-permute-start(bf16[4,1024,128]{2,1,0:T(8,128)(2,1)S(1)} %maximum_bitcast_fusion.ko_ref), channel_id=1, source_target_pairs={{0,4},{4,8},{8,12},{1,5},{5,9},{9,13},{2,6},{6,10},{10,14},{3,7},{... | collective-permute-start | bytes 3145736 | tf_op jit(solution)/shard_map/ppermute | solution.py:180
  252.8 16.2 %collective-permute-start.1 = (bf16[4,1024,128]{2,1,0:T(8,128)(2,1)S(1)}, bf16[4,1024,128]{2,1,0:T(8,128)(2,1)}, u32[]{:S(2)}, u32[]{:S(2)}) collective-permute-start(bf16[4,1024,128]{2,1,0:T(8,128)(2,1)S(1)} %maximum_bitcast_fusion.ko_ref), channel_id=1, source_target_pairs={{4,0},{8,4},{12,8},{5,1},{9,5},{13,9},{6,2},{10,6},{14,10},{7,3},{... | collective-permute-start | bytes 3145736 | tf_op jit(solution)/shard_map/ppermute | solution.py:182
  255.9 20.0 %collective-permute-start.2 = (bf16[4,1024,128]{2,1,0:T(8,128)(2,1)}, bf16[4,1024,128]{2,1,0:T(8,128)(2,1)}, u32[]{:S(2)}, u32[]{:S(2)}) collective-permute-start(bf16[4,1024,128]{2,1,0:T(8,128)(2,1)} %maximum_bitcast_fusion.1.vo_ref), channel_id=1, source_target_pairs={{0,4},{4,8},{8,12},{1,5},{5,9},{9,13},{2,6},{6,10},{10,14},{3,7},{... | collective-permute-start | bytes 3145736 | tf_op jit(solution)/shard_map/ppermute | solution.py:181
  259.5 20.8 %collective-permute-start.3 = (bf16[4,1024,128]{2,1,0:T(8,128)(2,1)}, bf16[4,1024,128]{2,1,0:T(8,128)(2,1)}, u32[]{:S(2)}, u32[]{:S(2)}) collective-permute-start(bf16[4,1024,128]{2,1,0:T(8,128)(2,1)} %maximum_bitcast_fusion.1.vo_ref), channel_id=1, source_target_pairs={{4,0},{8,4},{12,8},{5,1},{9,5},{13,9},{6,2},{10,6},{14,10},{7,3},{... | collective-permute-start | bytes 3145736 | tf_op jit(solution)/shard_map/ppermute | solution.py:183
  301.6 86.9 %reduce-scatter.3.cloned.1.call-start = ((), (), s32[]{:S(2)}) async-start(), calls=%async_computation.4 | async-start | bytes 2621440 | tf_op jit(solution)/shard_map/reduce_scatter | solution.py:211
Sparse Core Ops, SparseCore 0:
  59.3 86.8 all-reduce.2
  150.8 85.4 all-reduce.4
  301.7 41.2 reduce-scatter.4
  345.2 43.1 reduce-scatter.2

commit v5 on v4

--- a/solution.py
+++ b/solution.py
@@ -125,10 +125,30 @@
     causal = lax.broadcasted_iota(jnp.int32, (block_rows, block_rows), 0) >= lax.broadcasted_iota(
         jnp.int32, (block_rows, block_rows), 1
     )
-    w_qkv2_flat = w_qkv2.reshape(feature_width, 3 * inner_dev)
-    residual_parts = []
-    q_parts, k_parts, v_parts = [], [], []
-    previous = None
+    head_size = lax.axis_size("head")
+    core = ctx_index % 2
+    partner = [(i, i ^ 1) for i in range(ctx_size)]
+    half_rows = inner_dev // 2
+
+    def gather_rows(w):
+        local = lax.dynamic_slice_in_dim(w, core * half_rows, half_rows, 0)
+        mine = lax.all_gather(local, "head", axis=0)
+        other = lax.ppermute(mine, "ctx", partner)
+        return mine, other
+
+    def project_out(parts, mine, other):
+        total = 0.0
+        for g in range(head_size):
+            a_mine = lax.dynamic_slice_in_dim(parts[g], core * half_rows, half_rows, 1)
+            a_other = lax.dynamic_slice_in_dim(parts[g], (1 - core) * half_rows, half_rows, 1)
+            term = jnp.dot(a_mine, mine[g], preferred_element_type=f32) + jnp.dot(
+                a_other, other[g], preferred_element_type=f32
+            )
+            total = total + term.astype(bf16).astype(f32)
+        return total
+
+    w1_mine, w1_other = gather_rows(w_out1)
+    attn_parts = []
     for n in range(block_count):
         q_n, k_n, v_n = q_blocks[n], k_blocks[n], v_blocks[n]
         scores = jnp.einsum("the,she->hts", q_n, k_n, preferred_element_type=f32)
@@ -143,35 +163,29 @@
         )
         carried = carried + block_states[n]
         combined = within + carried_term
-        attn_n = (
+        attn_parts.append(
             rms_rows(combined, lin_gain.reshape(heads_dev, head_dim))
             .astype(bf16)
             .reshape(block_rows, inner_dev)
         )
-        partial = jnp.dot(attn_n, w_out1, preferred_element_type=f32).astype(bf16)
-        if previous is not None:
-            partial, previous = lax.optimization_barrier((partial, previous))
-            residual_parts[-1] = previous
-        summed = lax.psum(partial, "head").astype(f32)
-        tokens_n = tokens[n * block_rows : (n + 1) * block_rows].astype(f32)
-        residual_n = (tokens_n + summed).astype(bf16)
-        residual_parts.append(residual_n)
-        previous = residual_n
-        normed_n = rms_rows(residual_n.astype(f32), norm_two).astype(bf16)
-        proj_n = jnp.dot(normed_n, w_qkv2_flat, preferred_element_type=f32)
-        proj_n = proj_n.reshape(block_rows, 3, heads_dev, head_dim)
-        q_parts.append(rms_rows(proj_n[:, 0], q_gain).astype(bf16))
-        k_parts.append(rms_rows(proj_n[:, 1], k_gain).astype(bf16))
-        v_parts.append(proj_n[:, 2].astype(bf16))
-    residual = jnp.concatenate(residual_parts, axis=0)
-    query_hat = jnp.concatenate(q_parts, axis=0)
-    key_hat = jnp.concatenate(k_parts, axis=0)
-    value_two = jnp.concatenate(v_parts, axis=0)
+    attn_one = jnp.concatenate(attn_parts, axis=0)
+    gathered_one = lax.all_gather(attn_one, "head", axis=0)
+    w2_local, gathered_one = lax.optimization_barrier((w_out2, gathered_one))
+    w2_mine, w2_other = gather_rows(w2_local)
+    residual = (tokens.astype(f32) + project_out(gathered_one, w1_mine, w1_other)).astype(bf16)
+
+    normed_two = rms_rows(residual.astype(f32), norm_two).astype(bf16)
+    projected_two = jnp.dot(
+        normed_two, w_qkv2.reshape(feature_width, 3 * inner_dev), preferred_element_type=f32
+    )
+    projected_two = projected_two.reshape(tok_rows, 3, heads_dev, head_dim)
+    query_hat = rms_rows(projected_two[:, 0], q_gain).astype(bf16)
+    key_hat = rms_rows(projected_two[:, 1], k_gain).astype(bf16)
+    value_two = projected_two[:, 2].astype(bf16)
 
     plane_tiles = GY * GZ
     halo_rows = plane_tiles * TILE
     tile_count = tok_rows // TILE
-    head_size = lax.axis_size("head")
     up = [(i, i + 1) for i in range(ctx_size - 1)]
     down = [(i + 1, i) for i in range(ctx_size - 1)]
     key_hat = jnp.transpose(key_hat, (1, 0, 2))
@@ -193,31 +207,16 @@
         jnp.any((neighbours[:, :, None] == ids[None, None, :]) & present[:, :, None], axis=1)
         for _, _, ids in pieces
     ]
-    chunks = 2 if rows_mine % 2 == 0 else 1
-    part_rows = rows_mine // chunks
-    keys = [p[0] for p in pieces]
-    values = [p[1] for p in pieces]
-    w_out2_heads = w_out2.reshape(heads_dev, head_dim, w_out2.shape[1])
     key_ok = jnp.repeat(jnp.concatenate(tile_masks, axis=1), TILE, axis=1).astype(f32)
-    mixed_parts = []
-    for c in range(chunks):
-        block_tiles = (np.arange(head_size) * rows_mine + c * part_rows) // TILE
-        q_c = query_hat.reshape(heads_dev, head_size, chunks, part_rows, head_dim)[:, :, c]
-        q_c = q_c.reshape(heads_dev, head_size * part_rows, head_dim)
-        mask_c = key_ok[block_tiles][:, None, :]
-        attn_c = tile_attention(q_c, keys, values, mask_c, part_rows)
-        out_c = jnp.einsum("hte,hef->tf", attn_c, w_out2_heads, preferred_element_type=f32)
-        mixed_parts.append(
-            lax.psum_scatter(
-                out_c.astype(bf16),
-                "head",
-                scatter_dimension=0,
-                tiled=True,
-            )
-        )
-    summed_two = jnp.concatenate(mixed_parts, axis=0).astype(f32)
+    attn_two = tile_attention(
+        query_hat, [p[0] for p in pieces], [p[1] for p in pieces], key_ok[:, None, :], TILE
+    )
+    attn_two = attn_two.reshape(heads_dev, head_size, rows_mine, head_dim)
+    attn_two = lax.all_to_all(attn_two, "head", 1, 1, tiled=True)
+    attn_two = jnp.transpose(attn_two, (1, 2, 0, 3)).reshape(head_size, rows_mine, inner_dev)
     residual_mine = lax.dynamic_slice_in_dim(residual, head_index * rows_mine, rows_mine, 0)
-    return (residual_mine.astype(f32) + summed_two).astype(bf16)
+    mixed = residual_mine.astype(f32) + project_out(attn_two, w2_mine, w2_other)
+    return mixed.astype(bf16)
 
 
 def solution(mesh):

time: 400 us -> 348 us (0.87)
  waiting for transfers between devices: 230 us -> 163 us
  matrix products: 48.2 us -> 72.9 us
  other arithmetic: 23.1 us -> 10.7 us
  Pallas kernels: 35.3 us -> 24.6 us
  local copies, waits for them, and re-layouts: 27 us -> 37.5 us
  starting transfers between devices: 11.6 us -> 16.2 us
    psum x2 -> x0, waiting for transfers between devices: 150 us -> none  [on_device(): summed = lax.psum(partial, 'head').astype(f32)]
    all_gather x0 -> x3, waiting for transfers between devices: none -> 135 us  [the longest x1 71.3 us: on_device(): gathered_one = lax.all_gather(attn_one, 'head', axis=0)]
    reduce_scatter x2 -> x0, waiting for transfers between devices: 65.5 us -> none  [on_device(): lax.psum_scatter(out_c.astype(bf16), 'head', scatter_dimension=0, tiled=T...]
    dot_general x6 -> x17, matrix products: 27.1 us -> 56.5 us  [the longest x8 34.1 us: project_out(): jnp.dot(a_other, other[g], preferred_element_type=f32)]
    all_to_all x0 -> x1, waiting for transfers between devices: none -> 15.2 us  [on_device(): attn_two = lax.all_to_all(attn_two, 'head', 1, 1, tiled=True)]
    pallas_call x2 -> x1, Pallas kernels: 35.3 us -> 24.6 us  [tile_attention(): pl.pallas_call(functools.partial(_attn_kernel, scale=1.0 / math.sqrt(head...]
    reduce_sum x5 -> x2, other arithmetic: 12.2 us -> 4.82 us  [rms_rows(): mean_sq = jnp.mean(value * value, axis=-1, keepdims=True)]
    all_gather x0 -> x1, local copies, waits for them, and re-layouts: none -> 6.48 us  [on_device(): gathered_one = lax.all_gather(attn_one, 'head', axis=0)]
  transfers between devices with their start and end apart: 8 -> 10, of which waited for: 7 -> 6; matrix products, arithmetic and copies ran while one was open for 8% -> 31% of each run, Pallas kernels for 4% -> 7%
where the time goes in v5:
time: 348 us; the launch traced here: 347 us
  waiting for transfers between devices  163 us (47%)
  matrix products  72.9 us (21%)
  local copies, waits for them, and re-layouts  37.5 us (11%)
  Pallas kernels  24.6 us (7%)
  starting transfers between devices  16.2 us (5%)
  between operations  13.5 us (4%)
  other arithmetic  10.7 us (3%)
  blocking collectives  8.67 us (2%)
    all_gather x1, waiting for transfers between devices, on_device(): gathered_one = lax.all_gather(attn_one, 'head', axis=0)  71.3 us
    all_gather x2, waiting for transfers between devices, gather_rows(): mine = lax.all_gather(local, 'head', axis=0)  63.2 us
    dot_general x8, matrix products, project_out(): jnp.dot(a_other, other[g], preferred_element_type=f32)  34.1 us
    pallas_call x1, Pallas kernels, tile_attention(): pl.pallas_call(functools.partial(_attn_kernel, scale=1.0 / math.sqrt(head...  24.6 us
    unnamed x34, local copies, waits for them, and re-layouts  21.2 us
    all_to_all x1, waiting for transfers between devices, on_device(): attn_two = lax.all_to_all(attn_two, 'head', 1, 1, tiled=True)  15.2 us
    dot_general x8, matrix products, project_out(): jnp.dot(a_mine, mine[g], preferred_element_type=f32)  11.9 us
    dot_general x1, matrix products, on_device(): jnp.dot(normed_two, w_qkv2.reshape(feature_width, 3 * inner_dev), preferr...  10.6 us
  transfers between devices with their start and end apart: 10, of which 6 were waited for; matrix products, arithmetic and copies ran while one was open for 31% of the time, Pallas kernels for 7%

profile of v5, /device:TPU:1, one launch (start us, length us, event | category | flops | bytes accessed | tf_op | source)
XLA Modules:
  0.0 346.6 jit_solution(2693394226531302959)
XLA Ops:
  6.5 1.6 copy-done
  8.1 1.1 constant_dynamic-slice_fusion.1
  9.3 8.8 %copy.61 = bf16[2048,3,512]{0,2,1:T(8,128)(2,1)} copy(bf16[2048,3,512]{2,0,1:T(8,128)(2,1)} %param.13) | data formatting | bytes 12582912 | tf_op args[2]
  18.1 3.7 %fusion.3 = f32[1024]{0:T(1024)S(1)} fusion(bf16[1024,2048]{1,0:T(8,128)(2,1)} %param.11), kind=kLoop, calls=%fused_computation.8 | loop fusion | flops 6290432 | bytes 4198400 | tf_op jit(solution)/shard_map/reduce_sum | solution.py:33
  21.8 0.5 copy-done.2
  22.3 9.1 %fusion.8 = f32[1024,3,4,128]{3,0,2,1:T(8,128)S(1)} fusion(bf16[3,4,128,2048]{3,2,1,0:T(8,128)(2,1)} %bitcast.162, bf16[1024,2048]{1,0:T(8,128)(2,1)S(1)} %copy-done.2, f32[2048]{0:T(1024)S(1)} %copy-done.14, f32[1024]{0:T(1024)S(1)} %add_rsqrt_fusion.5), kind=kOutput, calls=%fused_computation.17 | convolution fusion | flops 6450839552 | bytes 16789504 | tf_op jit(solution)/shard_map/dot_general | solution.py:107
  31.6 1.0 select_convert_fusion.4
  32.6 0.5 fusion.128
  33.1 8.7 %all-gather = bf16[16,128,128]{2,1,0:T(8,128)(2,1)S(1)} all-gather(bf16[4,128,128]{2,1,0:T(8,128)(2,1)S(1)} %get-tuple-element.28), channel_id=2, replica_groups=mesh['groups'=2,'ctx'=4,'head'=4] {'ctx'}, dimensions={0}, use_global_device_ids=true | all-gather | bytes 655360 | tf_op jit(solution)/shard_map/all_gather | solution.py:121
  41.9 0.3 fusion.89
  42.3 0.4 fusion.90
  42.6 0.3 convolution_add_fusion.5
  43.0 0.4 convolution_add_fusion.4
  43.3 0.7 fusion.71
  44.1 0.7 fusion.72
  44.8 0.9 fusion.18
  45.7 0.9 fusion.17
  46.6 1.1 multiply_reduce_fusion.2
  47.7 1.1 multiply_reduce_fusion.3
  48.8 0.3 multiply_convert_fusion.3
  49.1 1.1 pad_maximum_fusion
  50.5 41.7 %all-gather.10.cloned.1.call-done = bf16[1024,2048]{1,0:T(8,128)(2,1)} async-done(((bf16[256,2048]{1,0:T(8,128)(2,1)}), bf16[1024,2048]{1,0:T(8,128)(2,1)}) %all-gather.10.cloned.1.call-update) | async-done | bytes 4194320 | tf_op jit(solution)/shard_map/all_gather | solution.py:135
  92.2 0.7 collective-permute-start
  92.9 8.9 %copy.73 = bf16[2048,3,512]{0,2,1:T(8,128)(2,1)} copy(bf16[2048,3,512]{2,0,1:T(8,128)(2,1)} %param.17) | data formatting | bytes 12582912 | tf_op args[6]
  101.8 71.3 %all-gather.8.cloned.1.call-done = bf16[4096,512]{0,1:T(8,128)(2,1)} async-done(((bf16[1024,512]{0,1:T(8,128)(2,1)}), bf16[4096,512]{0,1:T(8,128)(2,1)}) %all-gather.8.cloned.1.call-update) | async-done | bytes 4194320 | tf_op jit(solution)/shard_map/all_gather | solution.py:172
  173.1 6.5 %copy.72 = bf16[4096,512]{1,0:T(8,128)(2,1)} copy(bf16[4096,512]{0,1:T(8,128)(2,1)} %all-gather.8.cloned.1.call-done) | data formatting | bytes 8388608 | tf_op jit(solution)/shard_map/all_gather | solution.py:172
  179.6 1.1 constant_dynamic-slice_fusion
  180.7 2.7 fusion.126
  183.5 0.7 copy-done.4
  184.2 4.8 %fusion.65 = f32[1024,2048]{1,0:T(8,128)} fusion(bf16[1024,2048]{1,0:T(8,128)(2,1)S(1)} %copy-done.4, bf16[1,1024,512]{2,1,0:T(8,128)(2,1)S(1)} %get-tuple-element.21, s32[]{:T(128)S(6)} %select_n.60), kind=kOutput, calls=%fused_computation.100 | convolution fusion | flops 1073741824 | bytes 9961476 | tf_op jit(solution)/shard_map/dot_general | solution.py:144
  189.0 1.3 fusion.63
  190.3 1.3 fusion.61
  191.6 1.3 fusion.59
  192.8 7.1 %add_convert_fusion.3 = bf16[1024,2048]{1,0:T(8,128)(2,1)} fusion(f32[1024,2048]{1,0:T(8,128)} %fusion.65, bf16[4,256,2048]{2,1,0:T(8,128)(2,1)} %collective-permute-done, bf16[1,1024,512]{2,1,0:T(8,128)(2,1)S(1)} %get-tuple-element.21, s32[]{:T(128)S(6)} %select_n.61), kind=kOutput, calls=%fused_computation.15 | convolution fusion | flops 1077936128 | bytes 14155780 | tf_op jit(solution)/shard_map/dot_general | solution.py:144
  199.9 4.5 %add_convert_fusion.2 = bf16[1024,2048]{1,0:T(8,128)(2,1)} fusion(f32[1024,2048]{1,0:T(8,128)S(1)} %fusion.63, bf16[4,256,2048]{2,1,0:T(8,128)(2,1)} %collective-permute-done, bf16[1,1024,512]{2,1,0:T(8,128)(2,1)S(1)} %get-tuple-element.20, s32[]{:T(128)S(6)} %select_n.61), kind=kOutput, calls=%fused_computation.14 | convolution fusion | flops 1077936128 | bytes 14155780 | tf_op jit(solution)/shard_map/dot_general | solution.py:144
  204.3 4.6 %add_convert_fusion.1 = bf16[1024,2048]{1,0:T(8,128)(2,1)} fusion(f32[1024,2048]{1,0:T(8,128)S(1)} %fusion.61, bf16[4,256,2048]{2,1,0:T(8,128)(2,1)} %collective-permute-done, bf16[1,1024,512]{2,1,0:T(8,128)(2,1)S(1)} %get-tuple-element.19, s32[]{:T(128)S(6)} %select_n.61), kind=kOutput, calls=%fused_computation.13 | convolution fusion | flops 1077936128 | bytes 14155780 | tf_op jit(solution)/shard_map/dot_general | solution.py:144
  208.9 9.3 %fusion = (f32[1024]{0:T(1024)S(1)}, bf16[1024,2048]{1,0:T(8,128)(2,1)}) fusion(f32[1024,2048]{1,0:T(8,128)S(1)} %fusion.59, bf16[4,256,2048]{2,1,0:T(8,128)(2,1)} %collective-permute-done, bf16[1,1024,512]{2,1,0:T(8,128)(2,1)S(1)} %get-tuple-element.18, s32[]{:T(128)S(6)} %select_n.61, bf16[1024,2048]{1,0:T(8,128)(2,1)} %add_convert_fusion.1, ...), kind=kOutput, calls=%fused_computation.5 | convolution fusion | flops 1105198080 | bytes 30937092 | tf_op jit(solution)/shard_map/dot_general | solution.py:144
  218.3 10.6 %fusion.11 = f32[1024,3,4,128]{3,0,2,1:T(8,128)S(1)} fusion(bf16[3,4,128,2048]{3,2,1,0:T(8,128)(2,1)} %bitcast.161, bf16[1024,2048]{1,0:T(8,128)(2,1)} %get-tuple-element.35, f32[2048]{0:T(1024)S(1)} %copy-done.15, f32[1024]{0:T(1024)S(1)} %add_rsqrt_fusion.4), kind=kOutput, calls=%fused_computation.19 | convolution fusion | flops 6450839552 | bytes 16789504 | tf_op jit(solution)/shard_map/dot_general | solution.py:178
  228.9 1.2 multiply_reduce_fusion
  230.1 2.8 fusion.49
  232.9 3.8 %collective-permute-start.1 = (bf16[4,1024,128]{2,1,0:T(8,128)(2,1)S(1)}, bf16[4,1024,128]{2,1,0:T(8,128)(2,1)S(1)}, u32[]{:S(2)}, u32[]{:S(2)}) collective-permute-start(bf16[4,1024,128]{2,1,0:T(8,128)(2,1)S(1)} %get-tuple-element.14.ko_ref), channel_id=1, source_target_pairs={{0,4},{4,8},{8,12},{1,5},{5,9},{9,13},{2,6},{6,10},{10,14},{3,7},{... | collective-permute-start | bytes 3145736 | tf_op jit(solution)/shard_map/ppermute | solution.py:194
  236.7 1.9 collective-permute-start.2
  238.7 21.5 %all-gather.12.cloned.1.call-done = bf16[1024,2048]{1,0:T(8,128)(2,1)} async-done(((bf16[256,2048]{1,0:T(8,128)(2,1)}), bf16[1024,2048]{1,0:T(8,128)(2,1)}) %all-gather.12.cloned.1.call-update) | async-done | bytes 4194320 | tf_op jit(solution)/shard_map/all_gather | solution.py:135
  260.2 0.7 collective-permute-start.5
  260.8 1.7 fusion.50.vo_ref
  262.6 3.0 collective-permute-start.3
  265.6 2.3 collective-permute-start.4
  267.9 0.4 and_reduce_fusion.2
  268.4 0.7 convert_element_type.223.m_ref
  269.1 8.2 %collective-permute-done.3.vp_ref = bf16[4,1024,128]{2,1,0:T(8,128)(2,1)} collective-permute-done((bf16[4,1024,128]{2,1,0:T(8,128)(2,1)S(1)}, bf16[4,1024,128]{2,1,0:T(8,128)(2,1)}, u32[]{:S(2)}, u32[]{:S(2)}) %collective-permute-start.3) | collective-permute-done | bytes 1048608 | tf_op jit(solution)/shard_map/ppermute | solution.py:195
  277.3 4.5 %collective-permute-done.4.vn_ref = bf16[4,1024,128]{2,1,0:T(8,128)(2,1)} collective-permute-done((bf16[4,1024,128]{2,1,0:T(8,128)(2,1)S(1)}, bf16[4,1024,128]{2,1,0:T(8,128)(2,1)}, u32[]{:S(2)}, u32[]{:S(2)}) %collective-permute-start.4) | collective-permute-done | bytes 1048608 | tf_op jit(solution)/shard_map/ppermute | solution.py:197
  281.8 24.6 %shard_map.109 = bf16[4,1024,128]{2,1,0:T(8,128)(2,1)} custom-call(bf16[4,1024,128]{2,1,0:T(8,128)(2,1)} %get-tuple-element.15.q_ref, bf16[4,1024,128]{2,1,0:T(8,128)(2,1)} %copy-done.8, bf16[4,1024,128]{2,1,0:T(8,128)(2,1)} %copy-done.7, bf16[4,1024,128]{2,1,0:T(8,128)(2,1)} %collective-permute-done.2.kn_ref, ...), custom_call_target="tpu_custom_call" | custom-call | tf_op jit(solution)/shard_map/pallas_call | solution.py:79
  306.4 2.3 copy.78
  308.7 3.5 %all-to-all-start = ((bf16[4,4,256,128]{2,3,0,1:T(8,128)(2,1)}), bf16[4,4,256,128]{2,3,0,1:T(8,128)(2,1)S(1)}, u32[]{:S(2)}, u32[]{:S(2)}) async-start(bf16[4,4,256,128]{2,3,0,1:T(8,128)(2,1)} %copy.78), calls=%async_computation | async-start | bytes 2097152 | tf_op jit(solution)/shard_map/all_to_all | solution.py:215
  312.2 15.2 %all-to-all-done = bf16[4,4,256,128]{2,3,0,1:T(8,128)(2,1)S(1)} async-done(((bf16[4,4,256,128]{2,3,0,1:T(8,128)(2,1)}), bf16[4,4,256,128]{2,3,0,1:T(8,128)(2,1)S(1)}, u32[]{:S(2)}, u32[]{:S(2)}) %all-to-all-start) | async-done | bytes 1048608 | tf_op jit(solution)/shard_map/all_to_all | solution.py:215
  327.5 1.8 fusion.57
  329.4 0.6 copy-done.5
  330.0 0.5 fusion.55
  330.4 0.5 fusion.53
  330.9 0.5 fusion.51
  331.4 1.7 fusion.26
  333.1 1.7 fusion.28
  334.8 1.9 fusion.30
  336.7 3.4 fusion.31
  (53 shorter events, 1.1 us)
Async XLA Ops:
  6.5 1.6 copy-start
  6.5 85.7 %all-gather.10.cloned.1.call-start = ((), (), s32[]{:S(2)}) async-start(), calls=%async_computation.2 | async-start | bytes 5242880 | tf_op jit(solution)/shard_map/all_gather | solution.py:135
  9.2 163.9 %all-gather.8.cloned.1.call-start = ((), (), s32[]{:S(2)}) async-start(), calls=%async_computation.1 | async-start | bytes 5242880 | tf_op jit(solution)/shard_map/all_gather | solution.py:172
  18.1 4.2 %copy-start.2 = (bf16[1024,2048]{1,0:T(8,128)(2,1)S(1)}, bf16[1024,2048]{1,0:T(8,128)(2,1)}, u32[]{:S(2)}) copy-start(bf16[1024,2048]{1,0:T(8,128)(2,1)} %param.11) | copy-start | bytes 12582916
  18.1 4.2 %copy-start.14 = (f32[2048]{0:T(1024)S(1)}, f32[2048]{0:T(1024)}, u32[]{:S(2)}) copy-start(f32[2048]{0:T(1024)} %param.12) | copy-start | bytes 24580
  47.7 1.1 copy-start.11
  50.2 209.9 %all-gather.12.cloned.1.call-start = ((), (), s32[]{:S(2)}) async-start(), calls=%async_computation.3 | async-start | bytes 5242880 | tf_op jit(solution)/shard_map/all_gather | solution.py:135
  92.2 100.6 %collective-permute-start = (bf16[4,256,2048]{2,1,0:T(8,128)(2,1)}, bf16[4,256,2048]{2,1,0:T(8,128)(2,1)}, u32[]{:S(2)}, u32[]{:S(2)}) collective-permute-start(bf16[4,256,2048]{2,1,0:T(8,128)(2,1)} %bitcast.163), channel_id=1, source_target_pairs={{0,4},{4,0},{8,12},{12,8},{1,5},{5,1},{9,13},{13,9},{2,6},{6,2},{1... | collective-permute-start | bytes 12582920 | tf_op jit(solution)/shard_map/ppermute | solution.py:136
  101.8 77.8 %copy-start.9 = (bf16[512,2048]{1,0:T(8,128)(2,1)S(1)}, bf16[512,2048]{1,0:T(8,128)(2,1)}, u32[]{:S(2)}) copy-start(bf16[512,2048]{1,0:T(8,128)(2,1)} %param.20) | copy-start | bytes 6291460
  180.7 3.5 copy-start.4
  208.9 9.4 %copy-start.15 = (f32[2048]{0:T(1024)S(1)}, f32[2048]{0:T(1024)}, u32[]{:S(2)}) copy-start(f32[2048]{0:T(1024)} %param.16) | copy-start | bytes 24580
  228.9 4.0 %copy-start.3 = (f32[1024,3,4,128]{3,0,2,1:T(8,128)}, f32[1024,3,4,128]{3,0,2,1:T(8,128)S(1)}, u32[]{:S(2)}) copy-start(f32[1024,3,4,128]{3,0,2,1:T(8,128)S(1)} %fusion.11) | copy-start | bytes 18874372
  228.9 1.2 copy-start.12
  228.9 1.2 copy-start.13
  230.1 37.8 %copy-start.10 = (s32[4,8]{1,0:T(4,128)S(1)}, s32[4,8]{1,0:T(4,128)}, u32[]{:S(2)}) copy-start(s32[4,8]{1,0:T(4,128)} %param.21) | copy-start | bytes 388
  232.9 48.9 %copy-start.7 = (bf16[4,1024,128]{2,1,0:T(8,128)(2,1)}, bf16[4,1024,128]{2,1,0:T(8,128)(2,1)S(1)}, u32[]{:S(2)}) copy-start(bf16[4,1024,128]{2,1,0:T(8,128)(2,1)S(1)} %get-tuple-element.14.ko_ref) | copy-start | bytes 3145732
  232.9 36.2 %collective-permute-start.1 = (bf16[4,1024,128]{2,1,0:T(8,128)(2,1)S(1)}, bf16[4,1024,128]{2,1,0:T(8,128)(2,1)S(1)}, u32[]{:S(2)}, u32[]{:S(2)}) collective-permute-start(bf16[4,1024,128]{2,1,0:T(8,128)(2,1)S(1)} %get-tuple-element.14.ko_ref), channel_id=1, source_target_pairs={{0,4},{4,8},{8,12},{1,5},{5,9},{9,13},{2,6},{6,10},{10,14},{3,7},{... | collective-permute-start | bytes 3145736 | tf_op jit(solution)/shard_map/ppermute | solution.py:194
  236.7 32.4 %collective-permute-start.2 = (bf16[4,1024,128]{2,1,0:T(8,128)(2,1)S(1)}, bf16[4,1024,128]{2,1,0:T(8,128)(2,1)}, u32[]{:S(2)}, u32[]{:S(2)}) collective-permute-start(bf16[4,1024,128]{2,1,0:T(8,128)(2,1)S(1)} %get-tuple-element.14.ko_ref), channel_id=1, source_target_pairs={{4,0},{8,4},{12,8},{5,1},{9,5},{13,9},{6,2},{10,6},{14,10},{7,3},{... | collective-permute-start | bytes 3145736 | tf_op jit(solution)/shard_map/ppermute | solution.py:196
  260.2 71.2 %collective-permute-start.5 = (bf16[4,256,2048]{2,1,0:T(8,128)(2,1)}, bf16[4,256,2048]{2,1,0:T(8,128)(2,1)}, u32[]{:S(2)}, u32[]{:S(2)}) collective-permute-start(bf16[4,256,2048]{2,1,0:T(8,128)(2,1)} %bitcast.164), channel_id=1, source_target_pairs={{0,4},{4,0},{8,12},{12,8},{1,5},{5,1},{9,13},{13,9},{2,6},{6,2},{1... | collective-permute-start | bytes 12582920 | tf_op jit(solution)/shard_map/ppermute | solution.py:136
  262.6 19.3 %copy-start.6 = (bf16[4,1024,128]{2,1,0:T(8,128)(2,1)}, bf16[4,1024,128]{2,1,0:T(8,128)(2,1)S(1)}, u32[]{:S(2)}) copy-start(bf16[4,1024,128]{2,1,0:T(8,128)(2,1)S(1)} %fusion.50.vo_ref) | copy-start | bytes 3145732
  262.6 14.8 %collective-permute-start.3 = (bf16[4,1024,128]{2,1,0:T(8,128)(2,1)S(1)}, bf16[4,1024,128]{2,1,0:T(8,128)(2,1)}, u32[]{:S(2)}, u32[]{:S(2)}) collective-permute-start(bf16[4,1024,128]{2,1,0:T(8,128)(2,1)S(1)} %fusion.50.vo_ref), channel_id=1, source_target_pairs={{0,4},{4,8},{8,12},{1,5},{5,9},{9,13},{2,6},{6,10},{10,14},{3,7},{... | collective-permute-start | bytes 3145736 | tf_op jit(solution)/shard_map/ppermute | solution.py:195
  265.6 16.2 %collective-permute-start.4 = (bf16[4,1024,128]{2,1,0:T(8,128)(2,1)S(1)}, bf16[4,1024,128]{2,1,0:T(8,128)(2,1)}, u32[]{:S(2)}, u32[]{:S(2)}) collective-permute-start(bf16[4,1024,128]{2,1,0:T(8,128)(2,1)S(1)} %fusion.50.vo_ref), channel_id=1, source_target_pairs={{4,0},{8,4},{12,8},{5,1},{9,5},{13,9},{6,2},{10,6},{14,10},{7,3},{... | collective-permute-start | bytes 3145736 | tf_op jit(solution)/shard_map/ppermute | solution.py:197
  269.1 12.7 %copy-start.8 = (bf16[4,1024,128]{2,1,0:T(8,128)(2,1)}, bf16[4,1024,128]{2,1,0:T(8,128)(2,1)S(1)}, u32[]{:S(2)}) copy-start(bf16[4,1024,128]{2,1,0:T(8,128)(2,1)S(1)} %collective-permute-done.1.kp_ref) | copy-start | bytes 3145732
  308.7 18.8 %all-to-all-start = ((bf16[4,4,256,128]{2,3,0,1:T(8,128)(2,1)}), bf16[4,4,256,128]{2,3,0,1:T(8,128)(2,1)S(1)}, u32[]{:S(2)}, u32[]{:S(2)}) async-start(bf16[4,4,256,128]{2,3,0,1:T(8,128)(2,1)} %copy.78), calls=%async_computation | async-start | bytes 2097152 | tf_op jit(solution)/shard_map/all_to_all | solution.py:215
  327.5 2.5 copy-start.5
  334.8 5.3 %copy-start.1 = (bf16[512,2048]{1,0:T(8,128)(2,1)S(1)}, bf16[512,2048]{1,0:T(8,128)(2,1)}, u32[]{:S(2)}) copy-start(bf16[512,2048]{1,0:T(8,128)(2,1)} %param.15) | copy-start | bytes 6291460
Sparse Core Ops, SparseCore 0:
  9.4 82.8 all-gather.9
  93.8 79.2 all-gather.7
  180.8 79.2 all-gather.11

commit v6 on v5

--- a/solution.py
+++ b/solution.py
@@ -127,27 +127,36 @@
     )
     head_size = lax.axis_size("head")
     core = ctx_index % 2
-    partner = [(i, i ^ 1) for i in range(ctx_size)]
-    half_rows = inner_dev // 2
-
-    def gather_rows(w):
-        local = lax.dynamic_slice_in_dim(w, core * half_rows, half_rows, 0)
+
+    group_index = lax.axis_index("groups")
+    y_bit = (ctx_index // 2) % 2
+    slot = group_index * 4 + y_bit * 2 + core
+    slice_rows = inner_dev // 8
+    core_pairs = [(i, i ^ 1) for i in range(ctx_size)]
+    y_pairs = [(i, i ^ 2) for i in range(ctx_size)]
+    group_pairs = [(i, i ^ 1) for i in range(lax.axis_size("groups"))]
+
+    def ordered(bit, own, other):
+        return jnp.where(bit == 0, jnp.stack([own, other]), jnp.stack([other, own]))
+
+    def gather_weight(w):
+        local = lax.dynamic_slice_in_dim(w, slot * slice_rows, slice_rows, 0)
         mine = lax.all_gather(local, "head", axis=0)
-        other = lax.ppermute(mine, "ctx", partner)
-        return mine, other
-
-    def project_out(parts, mine, other):
+        by_y = ordered(y_bit, mine, lax.ppermute(mine, "ctx", y_pairs))
+        by_group = ordered(group_index, by_y, lax.ppermute(by_y, "groups", group_pairs))
+        by_core = ordered(core, by_group, lax.ppermute(by_group, "ctx", core_pairs))
+        full = jnp.transpose(by_core, (1, 2, 0, 3, 4, 5)).reshape((8,) + mine.shape)
+        return jnp.transpose(full, (1, 0, 2, 3)).reshape(head_size, inner_dev, w.shape[1])
+
+    def project_out(parts, full):
         total = 0.0
         for g in range(head_size):
-            a_mine = lax.dynamic_slice_in_dim(parts[g], core * half_rows, half_rows, 1)
-            a_other = lax.dynamic_slice_in_dim(parts[g], (1 - core) * half_rows, half_rows, 1)
-            term = jnp.dot(a_mine, mine[g], preferred_element_type=f32) + jnp.dot(
-                a_other, other[g], preferred_element_type=f32
-            )
+            term = jnp.dot(parts[g], full[g], preferred_element_type=f32)
             total = total + term.astype(bf16).astype(f32)
         return total
 
-    w1_mine, w1_other = gather_rows(w_out1)
+    w1_full = gather_weight(w_out1)
+    w2_full = gather_weight(w_out2)
     attn_parts = []
     for n in range(block_count):
         q_n, k_n, v_n = q_blocks[n], k_blocks[n], v_blocks[n]
@@ -170,9 +179,7 @@
         )
     attn_one = jnp.concatenate(attn_parts, axis=0)
     gathered_one = lax.all_gather(attn_one, "head", axis=0)
-    w2_local, gathered_one = lax.optimization_barrier((w_out2, gathered_one))
-    w2_mine, w2_other = gather_rows(w2_local)
-    residual = (tokens.astype(f32) + project_out(gathered_one, w1_mine, w1_other)).astype(bf16)
+    residual = (tokens.astype(f32) + project_out(gathered_one, w1_full)).astype(bf16)
 
     normed_two = rms_rows(residual.astype(f32), norm_two).astype(bf16)
     projected_two = jnp.dot(
@@ -215,7 +222,7 @@
     attn_two = lax.all_to_all(attn_two, "head", 1, 1, tiled=True)
     attn_two = jnp.transpose(attn_two, (1, 2, 0, 3)).reshape(head_size, rows_mine, inner_dev)
     residual_mine = lax.dynamic_slice_in_dim(residual, head_index * rows_mine, rows_mine, 0)
-    mixed = residual_mine.astype(f32) + project_out(attn_two, w2_mine, w2_other)
+    mixed = residual_mine.astype(f32) + project_out(attn_two, w2_full)
     return mixed.astype(bf16)
 
 

time: 348 us -> 341 us (0.980); the launches traced: 347 us -> 335 us
  waiting for transfers between devices: 163 us -> 108 us
  other arithmetic: 10.7 us -> 46.2 us
  local copies, waits for them, and re-layouts: 37.5 us -> 47 us
  matrix products: 72.9 us -> 63.6 us
  starting transfers between devices: 16.2 us -> 22.4 us
    ppermute x2 -> x6, waiting for transfers between devices: 0.01 us -> 91.7 us  [the longest x2 75 us: gather_weight(): lax.ppermute(by_y, 'groups', group_pairs)]
    all_gather x1, waiting for transfers between devices: 71.3 us -> 0.01 us  [on_device(): gathered_one = lax.all_gather(attn_one, 'head', axis=0)]
    all_gather x2, waiting for transfers between devices: 63.2 us -> 0.02 us  [gather_weight(): mine = lax.all_gather(local, 'head', axis=0)]
    select_n x0 -> x9, other arithmetic: none -> 24.6 us  [ordered(): return jnp.where(bit == 0, jnp.stack([own, other]), jnp.stack([other, own]))]
    dot_general x16 -> x8, matrix products: 45.9 us -> 29.8 us  [project_out(): term = jnp.dot(parts[g], full[g], preferred_element_type=f32)]
    all_to_all x1, waiting for transfers between devices: 15.2 us -> 0.01 us  [on_device(): attn_two = lax.all_to_all(attn_two, 'head', 1, 1, tiled=True)]
    transpose x0 -> x1, local copies, waits for them, and re-layouts: none -> 8.32 us  [gather_weight(): full = jnp.transpose(by_core, (1, 2, 0, 3, 4, 5)).reshape((8,) + mine.shape)]
    transpose x0 -> x1, other arithmetic: none -> 7.98 us  [gather_weight(): full = jnp.transpose(by_core, (1, 2, 0, 3, 4, 5)).reshape((8,) + mine.shape)]
  transfers between devices with their start and end apart: 10 -> 14, of which waited for: 6 -> 7; matrix products, arithmetic and copies ran while one was open for 31% -> 43% of each run, Pallas kernels for 7% -> 7%
where the time goes in v6:
time: 341 us; the launch traced here: 335 us
  waiting for transfers between devices  108 us (32%)
  matrix products  63.6 us (19%)
  local copies, waits for them, and re-layouts  47 us (14%)
  other arithmetic  46.2 us (14%)
  Pallas kernels  24.6 us (7%)
  starting transfers between devices  22.4 us (7%)
  between operations  13.9 us (4%)
  blocking collectives  9.09 us (3%)
    ppermute x2, waiting for transfers between devices, gather_weight(): lax.ppermute(by_y, 'groups', group_pairs)  75 us
    dot_general x8, matrix products, project_out(): term = jnp.dot(parts[g], full[g], preferred_element_type=f32)  29.8 us
    pallas_call x1, Pallas kernels, tile_attention(): pl.pallas_call(functools.partial(_attn_kernel, scale=1.0 / math.sqrt(head...  24.6 us
    select_n x9, other arithmetic, ordered(): return jnp.where(bit == 0, jnp.stack([own, other]), jnp.stack([other, own]))  24.6 us
    unnamed x68, local copies, waits for them, and re-layouts  23.6 us
    ppermute x2, waiting for transfers between devices, gather_weight(): by_y = ordered(y_bit, mine, lax.ppermute(mine, 'ctx', y_pairs))  16.7 us
    slice x3, local copies, waits for them, and re-layouts, project_out(): term = jnp.dot(parts[g], full[g], preferred_element_type=f32)  9.19 us
    dot_general x1, matrix products, on_device(): jnp.dot(normed, w_qkv1.reshape(feature_width, 3 * inner_dev), preferred_e...  9.1 us
  transfers between devices with their start and end apart: 14, of which 7 were waited for; matrix products, arithmetic and copies ran while one was open for 43% of the time, Pallas kernels for 7%

profile of v6, /device:TPU:1, one launch (start us, length us, event | category | flops | bytes accessed | tf_op | source)
XLA Modules:
  0.0 335.0 jit_solution(13221315048797662846)
XLA Ops:
  6.5 1.6 copy-done
  8.9 1.7 constant_dynamic-slice_fusion
  10.7 8.9 %copy.69 = bf16[2048,3,512]{0,2,1:T(8,128)(2,1)} copy(bf16[2048,3,512]{2,0,1:T(8,128)(2,1)} %param.13) | data formatting | bytes 12582912 | tf_op args[2]
  19.5 3.2 fusion.3
  23.0 9.1 %fusion.9 = f32[1024,3,4,128]{3,0,2,1:T(8,128)S(1)} fusion(bf16[3,4,128,2048]{3,2,1,0:T(8,128)(2,1)} %bitcast.188, bf16[1024,2048]{1,0:T(8,128)(2,1)S(1)} %copy-done.15, f32[2048]{0:T(1024)S(1)} %copy-done.29, f32[1024]{0:T(1024)S(1)} %add_rsqrt_fusion.5), kind=kOutput, calls=%fused_computation.17 | convolution fusion | flops 6450839552 | bytes 16789504 | tf_op jit(solution)/shard_map/dot_general | solution.py:107
  32.3 1.0 select_convert_fusion.4
  33.3 2.7 fusion.59
  36.0 2.7 fusion.60
  39.2 9.1 %all-gather = bf16[16,128,128]{2,1,0:T(8,128)(2,1)S(1)} all-gather(bf16[4,128,128]{2,1,0:T(8,128)(2,1)S(1)} %get-tuple-element.28), channel_id=2, replica_groups=mesh['groups'=2,'ctx'=4,'head'=4] {'ctx'}, dimensions={0}, use_global_device_ids=true | all-gather | bytes 655360 | tf_op jit(solution)/shard_map/all_gather | solution.py:121
  48.5 1.4 fusion.61
  49.9 1.3 fusion.62
  51.2 0.8 collective-permute-start
  52.0 1.7 convolution_add_fusion
  53.8 3.2 fusion.19
  57.3 2.0 fusion.18
  59.3 16.7 %collective-permute-done = bf16[4,64,2048]{2,1,0:T(8,128)(2,1)S(1)} collective-permute-done((bf16[4,64,2048]{2,1,0:T(8,128)(2,1)}, bf16[4,64,2048]{2,1,0:T(8,128)(2,1)S(1)}, u32[]{:S(2)}, u32[]{:S(2)}) %collective-permute-start) | collective-permute-done | bytes 1048608 | tf_op jit(solution)/shard_map/ppermute | solution.py:145
  76.0 1.7 maximum_select_fusion.6
  77.7 1.2 collective-permute-start.1
  79.8 1.0 multiply_reduce_fusion.2
  80.8 1.0 multiply_reduce_fusion.3
  82.1 1.1 pad_maximum_fusion
  83.3 0.9 collective-permute-start.7
  84.5 39.7 %collective-permute-done.1 = bf16[2,4,64,2048]{3,2,1,0:T(8,128)(2,1)} collective-permute-done((bf16[2,4,64,2048]{3,2,1,0:T(8,128)(2,1)}, bf16[2,4,64,2048]{3,2,1,0:T(8,128)(2,1)}, u32[]{:S(2)}, u32[]{:S(2)}) %collective-permute-start.1) | collective-permute-done | bytes 2097184 | tf_op jit(solution)/shard_map/ppermute | solution.py:146
  124.2 4.7 %maximum_select_fusion.2 = bf16[2,2,4,64,2048]{4,3,2,1,0:T(8,128)(2,1)} fusion(bf16[1,2,4,64,2048]{4,3,2,1,0:T(8,128)(2,1)} %bitcast.30, bf16[1,2,4,64,2048]{4,3,2,1,0:T(8,128)(2,1)S(1)} %maximum_select_fusion.5, pred[]{:T(512)S(6)} %eq.24), kind=kLoop, calls=%fused_computation.22 | loop fusion | flops 6291456 | bytes 8388609 | tf_op jit(solution)/shard_map/jit(_where)/select_n | solution.py:140
  129.0 1.9 collective-permute-start.2
  130.8 1.7 maximum_select_fusion.8
  132.5 1.2 collective-permute-start.8
  133.8 8.8 %copy.84 = bf16[2048,3,512]{0,2,1:T(8,128)(2,1)} copy(bf16[2048,3,512]{2,0,1:T(8,128)(2,1)} %param.17) | data formatting | bytes 12582912 | tf_op args[6]
  142.6 1.9 fusion.93
  144.9 35.2 %collective-permute-done.8 = bf16[2,4,64,2048]{3,2,1,0:T(8,128)(2,1)} collective-permute-done((bf16[2,4,64,2048]{3,2,1,0:T(8,128)(2,1)}, bf16[2,4,64,2048]{3,2,1,0:T(8,128)(2,1)}, u32[]{:S(2)}, u32[]{:S(2)}) %collective-permute-start.8) | collective-permute-done | bytes 2097184 | tf_op jit(solution)/shard_map/ppermute | solution.py:146
  180.1 4.6 %maximum_select_fusion.4 = bf16[2,2,4,64,2048]{4,3,2,1,0:T(8,128)(2,1)} fusion(bf16[1,2,4,64,2048]{4,3,2,1,0:T(8,128)(2,1)} %bitcast.63, bf16[1,2,4,64,2048]{4,3,2,1,0:T(8,128)(2,1)S(1)} %maximum_select_fusion.7, pred[]{:T(512)S(6)} %eq.24), kind=kLoop, calls=%fused_computation.24 | loop fusion | flops 6291456 | bytes 8388609 | tf_op jit(solution)/shard_map/jit(_where)/select_n | solution.py:140
  184.7 0.8 collective-permute-start.9
  185.5 2.8 bitcast_select_fusion
  188.4 5.3 %maximum_select_fusion = bf16[2,2,2,4,64,2048]{5,4,3,0,2,1:T(8,128)(2,1)S(1)} fusion(bf16[1,2,2,4,64,2048]{5,4,3,0,2,1:T(8,128)(2,1)} %bitcast.31, bf16[1,2,2,4,64,2048]{5,4,3,0,2,1:T(8,128)(2,1)S(1)} %bitcast_select_fusion, pred[]{:T(512)S(6)} %eq.23), kind=kLoop, calls=%fused_computation.12 | loop fusion | flops 12582912 | bytes 16777216 | tf_op jit(solution)/shard_map/jit(_where)/select_n | solution.py:140
  193.7 3.4 %fusion.75 = (bf16[1,8,64,2048]{3,2,0,1:T(8,128)(2,1)}, bf16[1,8,64,2048]{3,2,0,1:T(8,128)(2,1)}, bf16[1,8,64,2048]{3,2,0,1:T(8,128)(2,1)}, bf16[1,8,64,2048]{3,2,0,1:T(8,128)(2,1)}) fusion(bf16[4,8,64,2048]{3,2,0,1:T(8,128)(2,1)S(1)} %bitcast.164), kind=kLoop, calls=%fused_computation.140 | loop fusion | bytes 16777216 | tf_op jit(solution)/shard_map/slice | solution.py:154
  197.2 6.5 %fusion.53 = bf16[1024,2048]{1,0:T(8,128)(2,1)} fusion(bf16[512,2048]{1,0:T(8,128)(2,1)} %bitcast.198, bf16[4096,512]{0,1:T(8,128)(2,1)} %all-gather.8.cloned.1.call-done), kind=kOutput, calls=%fused_computation.88 | convolution fusion | flops 2147483648 | bytes 7340032 | tf_op jit(solution)/shard_map/dot_general | solution.py:154
  203.6 4.4 %fusion.51 = bf16[1024,2048]{1,0:T(8,128)(2,1)} fusion(bf16[512,2048]{1,0:T(8,128)(2,1)S(1)} %bitcast.197, bf16[4096,512]{0,1:T(8,128)(2,1)S(1)} %copy-done.28), kind=kOutput, calls=%fused_computation.86 | convolution fusion | flops 2147483648 | bytes 7340032 | tf_op jit(solution)/shard_map/dot_general | solution.py:154
  208.0 4.6 %fusion.49 = bf16[1024,2048]{1,0:T(8,128)(2,1)} fusion(bf16[512,2048]{1,0:T(8,128)(2,1)S(1)} %bitcast.196, bf16[4096,512]{0,1:T(8,128)(2,1)S(1)} %copy-done.28), kind=kOutput, calls=%fused_computation.84 | convolution fusion | flops 2147483648 | bytes 7340032 | tf_op jit(solution)/shard_map/dot_general | solution.py:154
  212.6 8.8 %fusion = (f32[1024]{0:T(1024)S(1)}, bf16[1024,2048]{1,0:T(8,128)(2,1)S(1)}) fusion(bf16[512,2048]{1,0:T(8,128)(2,1)S(1)} %bitcast.195, bf16[4096,512]{0,1:T(8,128)(2,1)} %all-gather.8.cloned.1.call-done, bf16[1024,2048]{1,0:T(8,128)(2,1)} %fusion.49, bf16[1024,2048]{1,0:T(8,128)(2,1)} %fusion.51, bf16[1024,2048]{1,0:T(8,128)(2,1)} %fusion.53, ...), kind=kOutput, calls=%fused_computation.5 | convolution fusion | flops 2176842752 | bytes 24121344 | tf_op jit(solution)/shard_map/dot_general | solution.py:154
  221.5 6.7 %fusion.12 = f32[1024,3,4,128]{3,0,2,1:T(8,128)S(1)} fusion(bf16[3,4,128,2048]{3,2,1,0:T(8,128)(2,1)S(1)} %bitcast.187, bf16[1024,2048]{1,0:T(8,128)(2,1)S(1)} %get-tuple-element.35, f32[2048]{0:T(1024)S(1)} %copy-done.30, f32[1024]{0:T(1024)S(1)} %add_rsqrt_fusion.4), kind=kOutput, calls=%fused_computation.19 | convolution fusion | flops 6450839552 | bytes 16789504 | tf_op jit(solution)/shard_map/dot_general | solution.py:185
  228.3 1.2 multiply_reduce_fusion
  229.5 2.6 fusion.46
  232.1 2.7 collective-permute-start.3
  234.9 2.7 collective-permute-start.4
  237.7 2.9 collective-permute-start.5
  240.6 2.4 collective-permute-start.6
  244.3 1.7 fusion.92
  246.0 1.0 collective-permute-done.3.kp_ref
  246.9 4.4 %collective-permute-done.4.kn_ref = bf16[4,1024,128]{2,1,0:T(8,128)(2,1)} collective-permute-done((bf16[4,1024,128]{2,1,0:T(8,128)(2,1)}, bf16[4,1024,128]{2,1,0:T(8,128)(2,1)}, u32[]{:S(2)}, u32[]{:S(2)}) %collective-permute-start.4) | collective-permute-done | bytes 1048608 | tf_op jit(solution)/shard_map/ppermute | solution.py:203
  251.3 6.7 %collective-permute-done.5.vp_ref = bf16[4,1024,128]{2,1,0:T(8,128)(2,1)} collective-permute-done((bf16[4,1024,128]{2,1,0:T(8,128)(2,1)S(1)}, bf16[4,1024,128]{2,1,0:T(8,128)(2,1)}, u32[]{:S(2)}, u32[]{:S(2)}) %collective-permute-start.5) | collective-permute-done | bytes 1048608 | tf_op jit(solution)/shard_map/ppermute | solution.py:202
  258.0 4.5 %collective-permute-done.6.vn_ref = bf16[4,1024,128]{2,1,0:T(8,128)(2,1)} collective-permute-done((bf16[4,1024,128]{2,1,0:T(8,128)(2,1)S(1)}, bf16[4,1024,128]{2,1,0:T(8,128)(2,1)}, u32[]{:S(2)}, u32[]{:S(2)}) %collective-permute-start.6) | collective-permute-done | bytes 1048608 | tf_op jit(solution)/shard_map/ppermute | solution.py:204
  262.5 24.6 %shard_map.109 = bf16[4,1024,128]{2,1,0:T(8,128)(2,1)} custom-call(bf16[4,1024,128]{2,1,0:T(8,128)(2,1)} %get-tuple-element.19.q_ref, bf16[4,1024,128]{2,1,0:T(8,128)(2,1)} %collective-permute-done.3.kp_ref, bf16[4,1024,128]{2,1,0:T(8,128)(2,1)} %get-tuple-element.18.ko_ref, bf16[4,1024,128]{2,1,0:T(8,128)(2,1)} %collective-permute-done.4.kn_ref, ...), custom_call_target="tpu_custom_call" | custom-call | tf_op jit(solution)/shard_map/pallas_call | solution.py:79
  287.1 2.4 copy.89
  289.5 4.9 %all-to-all-start = ((bf16[4,4,256,128]{2,3,0,1:T(8,128)(2,1)}), bf16[4,4,256,128]{2,3,0,1:T(8,128)(2,1)S(1)}, u32[]{:S(2)}, u32[]{:S(2)}) async-start(bf16[4,4,256,128]{2,3,0,1:T(8,128)(2,1)} %copy.89), calls=%async_computation | async-start | bytes 2097152 | tf_op jit(solution)/shard_map/all_to_all | solution.py:222
  294.4 2.9 maximum_select_fusion.3
  297.4 8.0 %fusion.7 = bf16[2,2,2,4,64,2048]{5,4,3,1,0,2:T(8,128)(2,1)} fusion(bf16[1,2,2,4,64,2048]{5,4,3,2,1,0:T(8,128)(2,1)} %bitcast.64, bf16[1,2,2,4,64,2048]{5,4,3,2,1,0:T(8,128)(2,1)S(1)} %maximum_select_fusion.3, pred[]{:T(512)S(6)} %eq.23), kind=kLoop, calls=%fused_computation.14 | loop fusion | flops 12582912 | bytes 16777216 | tf_op jit(solution)/shard_map/transpose | solution.py:148
  305.3 8.3 %copy.90 = bf16[2,2,2,4,64,2048]{5,4,3,2,1,0:T(8,128)(2,1)} copy(bf16[2,2,2,4,64,2048]{5,4,3,1,0,2:T(8,128)(2,1)} %fusion.7) | data formatting | bytes 16777216 | tf_op jit(solution)/shard_map/transpose | solution.py:148
  313.7 5.7 %fusion.74 = (bf16[1,8,64,2048]{3,2,0,1:T(8,128)(2,1)}, bf16[1,8,64,2048]{3,2,0,1:T(8,128)(2,1)S(1)}, bf16[1,8,64,2048]{3,2,0,1:T(8,128)(2,1)}, bf16[1,8,64,2048]{3,2,0,1:T(8,128)(2,1)}) fusion(bf16[4,8,64,2048]{3,2,0,1:T(8,128)(2,1)} %bitcast.165), kind=kLoop, calls=%fused_computation.139 | loop fusion | bytes 16777216 | tf_op jit(solution)/shard_map/slice | solution.py:154
  319.5 1.5 copy-done.11
  321.0 0.7 fusion.26
  321.7 0.9 copy-done.10
  323.3 0.7 fusion.28
  324.0 0.9 copy-done.12
  324.9 3.4 %fusion.25 = bf16[256,2048]{1,0:T(8,128)(2,1)} fusion(f32[256,2048]{1,0:T(8,128)S(1)} %fusion.28, f32[256,2048]{1,0:T(8,128)S(1)} %fusion.27, f32[256,2048]{1,0:T(8,128)S(1)} %fusion.26, bf16[256,512]{0,1:T(8,128)(2,1)S(1)} %bitcast.199, bf16[512,2048]{1,0:T(8,128)(2,1)S(1)} %bitcast.184, bf16[1024,2048]{1,0:T(8,128)(2,1)} %copy-done.23, s32[]{:T(128)S(6)} %select_n.157), kind=kOutput, calls=%fused_computation.44 | convolution fusion | flops 541065216 | bytes 10747908 | tf_op jit(solution)/shard_map/dot_general | solution.py:154
  (101 shorter events, 6.4 us)
Async XLA Ops:
  6.5 1.6 copy-start
  6.5 44.7 %all-gather.10.cloned.1.call-start = ((), (), s32[]{:S(2)}) async-start(), calls=%async_computation.2 | async-start | bytes 1310720 | tf_op jit(solution)/shard_map/all_gather | solution.py:144
  8.9 74.4 %all-gather.12.cloned.1.call-start = ((), (), s32[]{:S(2)}) async-start(), calls=%async_computation.3 | async-start | bytes 1310720 | tf_op jit(solution)/shard_map/all_gather | solution.py:144
  10.6 186.5 %all-gather.8.cloned.1.call-start = ((), (), s32[]{:S(2)}) async-start(), calls=%async_computation.1 | async-start | bytes 5242880 | tf_op jit(solution)/shard_map/all_gather | solution.py:181
  19.5 3.5 %copy-start.15 = (bf16[1024,2048]{1,0:T(8,128)(2,1)S(1)}, bf16[1024,2048]{1,0:T(8,128)(2,1)}, u32[]{:S(2)}) copy-start(bf16[1024,2048]{1,0:T(8,128)(2,1)} %param.11) | copy-start | bytes 12582916
  19.5 3.5 %copy-start.29 = (f32[2048]{0:T(1024)S(1)}, f32[2048]{0:T(1024)}, u32[]{:S(2)}) copy-start(f32[2048]{0:T(1024)} %param.12) | copy-start | bytes 24580
  32.2 21.5 %copy-start.7 = (bf16[1024,1,4,128]{3,0,2,1:T(8,128)(2,1)}, bf16[1024,1,4,128]{3,0,2,1:T(8,128)(2,1)S(1)}, u32[]{:S(2)}) copy-start(bf16[1024,1,4,128]{3,0,2,1:T(8,128)(2,1)S(1)} %slice.250) | copy-start | bytes 3145732
  39.2 10.7 %copy-start.22 = (f32[2,4,128,128]{3,2,1,0:T(8,128)}, f32[2,4,128,128]{3,2,1,0:T(8,128)S(1)}, u32[]{:S(2)}) copy-start(f32[2,4,128,128]{3,2,1,0:T(8,128)S(1)} %get-tuple-element.29) | copy-start | bytes 1572868
  48.5 2.7 copy-start.13
  51.2 24.8 %collective-permute-start = (bf16[4,64,2048]{2,1,0:T(8,128)(2,1)}, bf16[4,64,2048]{2,1,0:T(8,128)(2,1)S(1)}, u32[]{:S(2)}, u32[]{:S(2)}) collective-permute-start(bf16[4,64,2048]{2,1,0:T(8,128)(2,1)} %bitcast.173), channel_id=1, source_target_pairs={{0,8},{4,12},{8,0},{12,4},{1,9},{5,13},{9,1},{13,5},{2,10},{6,14},... | collective-permute-start | bytes 3145736 | tf_op jit(solution)/shard_map/ppermute | solution.py:145
  53.8 3.5 %copy-start.2 = (f32[4,512,512]{2,1,0:T(8,128)S(1)}, f32[4,512,512]{2,1,0:T(8,128)}, u32[]{:S(2)}) copy-start(f32[4,512,512]{2,1,0:T(8,128)} %fusion.60) | copy-start | bytes 12582916
  57.3 18.8 %copy-start.5 = (bf16[256,2048]{1,0:T(8,128)(2,1)S(1)}, bf16[256,2048]{1,0:T(8,128)(2,1)}, u32[]{:S(2)}) copy-start(bf16[256,2048]{1,0:T(8,128)(2,1)} %all-gather.10.cloned.1.call-done) | copy-start | bytes 3145732
  57.3 21.7 %copy-start.14 = (f32[4,128,128]{2,1,0:T(8,128)S(1)}, f32[4,128,128]{2,1,0:T(8,128)}, u32[]{:S(2)}) copy-start(f32[4,128,128]{2,1,0:T(8,128)} %copy-done.13) | copy-start | bytes 786436
  57.3 21.7 %copy-start.17 = (f32[4,128,512]{2,1,0:T(8,128)S(1)}, f32[4,128,512]{2,1,0:T(8,128)}, u32[]{:S(2)}) copy-start(f32[4,128,512]{2,1,0:T(8,128)} %fusion.61) | copy-start | bytes 3145732
  76.0 8.1 %copy-start.6 = (bf16[4,64,2048]{2,1,0:T(8,128)(2,1)}, bf16[4,64,2048]{2,1,0:T(8,128)(2,1)S(1)}, u32[]{:S(2)}) copy-start(bf16[4,64,2048]{2,1,0:T(8,128)(2,1)S(1)} %collective-permute-done) | copy-start | bytes 3145732
  76.0 3.3 copy-start.3
  77.7 2.1 copy-start.8
  77.7 46.5 %collective-permute-start.1 = (bf16[2,4,64,2048]{3,2,1,0:T(8,128)(2,1)}, bf16[2,4,64,2048]{3,2,1,0:T(8,128)(2,1)}, u32[]{:S(2)}, u32[]{:S(2)}) collective-permute-start(bf16[2,4,64,2048]{3,2,1,0:T(8,128)(2,1)} %maximum_select_fusion.6), channel_id=1, source_target_pairs={{0,16},{16,0},{1,17},{17,1},{2,18},{18,2},{3,19},{19,3},{4,20},{20... | collective-permute-start | bytes 6291464 | tf_op jit(solution)/shard_map/ppermute | solution.py:146
  80.8 1.1 copy-start.25
  83.3 47.5 %collective-permute-start.7 = (bf16[4,64,2048]{2,1,0:T(8,128)(2,1)}, bf16[4,64,2048]{2,1,0:T(8,128)(2,1)S(1)}, u32[]{:S(2)}, u32[]{:S(2)}) collective-permute-start(bf16[4,64,2048]{2,1,0:T(8,128)(2,1)} %bitcast.166), channel_id=1, source_target_pairs={{0,8},{4,12},{8,0},{12,4},{1,9},{5,13},{9,1},{13,5},{2,10},{6,14},... | collective-permute-start | bytes 3145736 | tf_op jit(solution)/shard_map/ppermute | solution.py:145
  124.2 6.6 %copy-start.4 = (bf16[256,2048]{1,0:T(8,128)(2,1)S(1)}, bf16[256,2048]{1,0:T(8,128)(2,1)}, u32[]{:S(2)}) copy-start(bf16[256,2048]{1,0:T(8,128)(2,1)} %all-gather.12.cloned.1.call-done) | copy-start | bytes 3145732
  129.0 59.4 %collective-permute-start.2 = (bf16[2,2,4,64,2048]{4,3,2,1,0:T(8,128)(2,1)}, bf16[2,2,4,64,2048]{4,3,2,1,0:T(8,128)(2,1)}, u32[]{:S(2)}, u32[]{:S(2)}) collective-permute-start(bf16[2,2,4,64,2048]{4,3,2,1,0:T(8,128)(2,1)} %maximum_select_fusion.2), channel_id=1, source_target_pairs={{0,4},{4,0},{8,12},{12,8},{1,5},{5,1},{9,13},{13,9},{2,6},{6,2},{1... | collective-permute-start | bytes 12582920 | tf_op jit(solution)/shard_map/ppermute | solution.py:147
  132.5 47.6 %collective-permute-start.8 = (bf16[2,4,64,2048]{3,2,1,0:T(8,128)(2,1)}, bf16[2,4,64,2048]{3,2,1,0:T(8,128)(2,1)}, u32[]{:S(2)}, u32[]{:S(2)}) collective-permute-start(bf16[2,4,64,2048]{3,2,1,0:T(8,128)(2,1)} %maximum_select_fusion.8), channel_id=1, source_target_pairs={{0,16},{16,0},{1,17},{17,1},{2,18},{18,2},{3,19},{19,3},{4,20},{20... | collective-permute-start | bytes 6291464 | tf_op jit(solution)/shard_map/ppermute | solution.py:146
  184.7 112.6 %collective-permute-start.9 = (bf16[2,2,4,64,2048]{4,3,2,1,0:T(8,128)(2,1)}, bf16[2,2,4,64,2048]{4,3,2,1,0:T(8,128)(2,1)}, u32[]{:S(2)}, u32[]{:S(2)}) collective-permute-start(bf16[2,2,4,64,2048]{4,3,2,1,0:T(8,128)(2,1)} %maximum_select_fusion.4), channel_id=1, source_target_pairs={{0,4},{4,0},{8,12},{12,8},{1,5},{5,1},{9,13},{13,9},{2,6},{6,2},{1... | collective-permute-start | bytes 12582920 | tf_op jit(solution)/shard_map/ppermute | solution.py:147
  197.1 6.5 %copy-start.21 = (bf16[1,8,64,2048]{3,2,0,1:T(8,128)(2,1)S(1)}, bf16[1,8,64,2048]{3,2,0,1:T(8,128)(2,1)}, u32[]{:S(2)}) copy-start(bf16[1,8,64,2048]{3,2,0,1:T(8,128)(2,1)} %get-tuple-element.16) | copy-start | bytes 6291460
  197.1 6.5 %copy-start.28 = (bf16[4096,512]{0,1:T(8,128)(2,1)S(1)}, bf16[4096,512]{0,1:T(8,128)(2,1)}, u32[]{:S(2)}) copy-start(bf16[4096,512]{0,1:T(8,128)(2,1)} %all-gather.8.cloned.1.call-done) | copy-start | bytes 12582916
  203.6 4.4 %copy-start.20 = (bf16[1,8,64,2048]{3,2,0,1:T(8,128)(2,1)S(1)}, bf16[1,8,64,2048]{3,2,0,1:T(8,128)(2,1)}, u32[]{:S(2)}) copy-start(bf16[1,8,64,2048]{3,2,0,1:T(8,128)(2,1)} %get-tuple-element.15) | copy-start | bytes 6291460
  208.0 4.6 %copy-start.16 = (bf16[1024,2048]{1,0:T(8,128)(2,1)S(1)}, bf16[1024,2048]{1,0:T(8,128)(2,1)}, u32[]{:S(2)}) copy-start(bf16[1024,2048]{1,0:T(8,128)(2,1)} %param.11) | copy-start | bytes 12582916
  208.0 4.6 %copy-start.19 = (bf16[1,8,64,2048]{3,2,0,1:T(8,128)(2,1)S(1)}, bf16[1,8,64,2048]{3,2,0,1:T(8,128)(2,1)}, u32[]{:S(2)}) copy-start(bf16[1,8,64,2048]{3,2,0,1:T(8,128)(2,1)} %get-tuple-element.14) | copy-start | bytes 6291460
  208.0 13.4 %slice-start = ((s8[6291456]{0:T(1024)(128)(4,1)}), s8[4194304]{0:T(1024)(128)(4,1)S(1)}, s32[]{:S(2)}) async-start(s8[6291456]{0:T(1024)(128)(4,1)} %bitcast.185), calls=%async_computation.4 | async-start | bytes 8388608
  212.6 8.9 %slice-start.1 = ((s8[6291456]{0:T(1024)(128)(4,1)}), s8[2097152]{0:T(1024)(128)(4,1)S(1)}, s32[]{:S(2)}) async-start(s8[6291456]{0:T(1024)(128)(4,1)} %bitcast.185), calls=%async_computation.5 | async-start | bytes 4194304
  212.6 8.9 %copy-start.30 = (f32[2048]{0:T(1024)S(1)}, f32[2048]{0:T(1024)}, u32[]{:S(2)}) copy-start(f32[2048]{0:T(1024)} %param.16) | copy-start | bytes 24580
  221.5 6.8 %copy-start.23 = (bf16[1024,2048]{1,0:T(8,128)(2,1)}, bf16[1024,2048]{1,0:T(8,128)(2,1)S(1)}, u32[]{:S(2)}) copy-start(bf16[1024,2048]{1,0:T(8,128)(2,1)S(1)} %get-tuple-element.35) | copy-start | bytes 12582916
  228.3 1.2 copy-start.26
  228.3 1.2 copy-start.27
  232.1 10.9 %copy-start.24 = (s32[4,8]{1,0:T(4,128)S(1)}, s32[4,8]{1,0:T(4,128)}, u32[]{:S(2)}) copy-start(s32[4,8]{1,0:T(4,128)} %param.21) | copy-start | bytes 388
  232.1 14.8 %collective-permute-start.3 = (bf16[4,1024,128]{2,1,0:T(8,128)(2,1)}, bf16[4,1024,128]{2,1,0:T(8,128)(2,1)}, u32[]{:S(2)}, u32[]{:S(2)}) collective-permute-start(bf16[4,1024,128]{2,1,0:T(8,128)(2,1)} %get-tuple-element.18.ko_ref), channel_id=1, source_target_pairs={{0,4},{4,8},{8,12},{1,5},{5,9},{9,13},{2,6},{6,10},{10,14},{3,7},{... | collective-permute-start | bytes 3145736 | tf_op jit(solution)/shard_map/ppermute | solution.py:201
  234.9 16.4 %collective-permute-start.4 = (bf16[4,1024,128]{2,1,0:T(8,128)(2,1)}, bf16[4,1024,128]{2,1,0:T(8,128)(2,1)}, u32[]{:S(2)}, u32[]{:S(2)}) collective-permute-start(bf16[4,1024,128]{2,1,0:T(8,128)(2,1)} %get-tuple-element.18.ko_ref), channel_id=1, source_target_pairs={{4,0},{8,4},{12,8},{5,1},{9,5},{13,9},{6,2},{10,6},{14,10},{7,3},{... | collective-permute-start | bytes 3145736 | tf_op jit(solution)/shard_map/ppermute | solution.py:203
  237.7 8.2 %copy-start.18 = (bf16[4,1024,128]{2,1,0:T(8,128)(2,1)}, bf16[4,1024,128]{2,1,0:T(8,128)(2,1)S(1)}, u32[]{:S(2)}) copy-start(bf16[4,1024,128]{2,1,0:T(8,128)(2,1)S(1)} %fusion.47.vo_ref) | copy-start | bytes 3145732
  237.7 20.3 %collective-permute-start.5 = (bf16[4,1024,128]{2,1,0:T(8,128)(2,1)S(1)}, bf16[4,1024,128]{2,1,0:T(8,128)(2,1)}, u32[]{:S(2)}, u32[]{:S(2)}) collective-permute-start(bf16[4,1024,128]{2,1,0:T(8,128)(2,1)S(1)} %fusion.47.vo_ref), channel_id=1, source_target_pairs={{0,4},{4,8},{8,12},{1,5},{5,9},{9,13},{2,6},{6,10},{10,14},{3,7},{... | collective-permute-start | bytes 3145736 | tf_op jit(solution)/shard_map/ppermute | solution.py:202
  240.6 21.9 %collective-permute-start.6 = (bf16[4,1024,128]{2,1,0:T(8,128)(2,1)S(1)}, bf16[4,1024,128]{2,1,0:T(8,128)(2,1)}, u32[]{:S(2)}, u32[]{:S(2)}) collective-permute-start(bf16[4,1024,128]{2,1,0:T(8,128)(2,1)S(1)} %fusion.47.vo_ref), channel_id=1, source_target_pairs={{4,0},{8,4},{12,8},{5,1},{9,5},{13,9},{6,2},{10,6},{14,10},{7,3},{... | collective-permute-start | bytes 3145736 | tf_op jit(solution)/shard_map/ppermute | solution.py:204
  287.1 7.3 %copy-start.9 = (bf16[1,1,2,4,64,2048]{5,4,3,2,1,0:T(8,128)(2,1)S(1)}, bf16[1,1,2,4,64,2048]{5,4,3,2,1,0:T(8,128)(2,1)}, u32[]{:S(2)}) copy-start(bf16[1,1,2,4,64,2048]{5,4,3,2,1,0:T(8,128)(2,1)} %fusion.92) | copy-start | bytes 6291460
  289.5 29.8 %all-to-all-start = ((bf16[4,4,256,128]{2,3,0,1:T(8,128)(2,1)}), bf16[4,4,256,128]{2,3,0,1:T(8,128)(2,1)S(1)}, u32[]{:S(2)}, u32[]{:S(2)}) async-start(bf16[4,4,256,128]{2,3,0,1:T(8,128)(2,1)} %copy.89), calls=%async_computation | async-start | bytes 2097152 | tf_op jit(solution)/shard_map/all_to_all | solution.py:222
  319.4 1.6 copy-start.11
  320.9 1.6 copy-start.10
  323.3 1.6 copy-start.12
  324.9 3.4 %copy-start.1 = (bf16[512,2048]{1,0:T(8,128)(2,1)S(1)}, bf16[512,2048]{1,0:T(8,128)(2,1)}, u32[]{:S(2)}) copy-start(bf16[512,2048]{1,0:T(8,128)(2,1)} %param.15) | copy-start | bytes 6291460
Sparse Core Ops, SparseCore 0:
  9.0 29.8 all-gather.9
  40.5 27.4 all-gather.11
  83.4 81.9 all-gather.7
